TPU v7x, 256 devices: a whole 4x4x8 slice. The times are simulated.
256 devices in a mesh: dp: 4 (over y), seq: 8 (over z), expert: 8 (over x, core).
Axes of the slice: x: 4, y: 4, z: 8, core: 2. Of those that a mesh axis runs over, the one named last changes fastest.
Arguments:
- frames: bfloat16 [32, 1024, 1024], P(('dp', 'expert'), 'seq'), may hold values from -6 to 6
- lengths: int32 [32], P(('dp', 'expert')), may hold values from 256 to 1024, as said below
- routes: int32 [32, 1024, 2], P(('dp', 'expert'), 'seq'), may hold values from 0 to 63, all different within a row; in each aligned block of 128 rows (0 to 127, 128 to 255, ..., all dimensions but the last counted through in order) at most 6 rows name the same one
- norm_conv: float32 [1024], replicated, may hold values from 0.1 to 1.9
- point_in: bfloat16 [1024, 2048], replicated, may hold values from -0.1875 to 0.1875
- depth_kernel: float32 [31, 1024], replicated, may hold values from -1 to 1
- bn_scale: float32 [1024], replicated, may hold values from 0.1 to 1.9
- bn_shift: float32 [1024], replicated, may hold values from -3 to 3
- point_out: bfloat16 [1024, 1024], replicated, may hold values from -0.1875 to 0.1875
- norm_moe: float32 [1024], replicated, may hold values from 0.1 to 1.9
- router: bfloat16 [1024, 64], replicated, may hold values from -0.1875 to 0.1875
- gate_weight: bfloat16 [64, 1024, 4096], P(('seq', 'expert'), None, 'dp'), may hold values from -0.1875 to 0.1875
- up_weight: bfloat16 [64, 1024, 4096], P(('seq', 'expert'), None, 'dp'), may hold values from -0.1875 to 0.1875
- down_weight: bfloat16 [64, 1024, 4096], P(('seq', 'expert'), None, 'dp'), may hold values from -0.09375 to 0.09375
Outputs:
- layer_out: bfloat16 [32, 1024, 1024], P(('dp', 'expert'), 'seq')
Inputs may be any that keep to these rules, and one draw needn't show every extreme that they name: `lengths`: each utterance has between 256 and 1024 valid frames; some utterance has all 1024, some only 256. `routes`: the two experts of a frame differ. Among the 128 frames of one device (aligned blocks of frames of one utterance), no expert is named more than 6 times, and in some blocks one expert is named exactly 6 times. Padded frames are routed too.
All inputs are finite; a program needn't handle non-finite values.
Results may differ from a plain program's by a relative error of at most 0.0085.
Values may be sent and summed in bfloat16 or wider, within the bound.
No kernel may reach another device: no remote copies, remote signals or barrier semaphores. Data moves between devices by JAX's collectives and lax.ppermute only.
A program may use at most 128 MiB of HBM per device.

v0:
```python
import jax
import jax.numpy as jnp
from jax import lax
from jax.sharding import PartitionSpec as P


def padded_2(x, sides, width):
    for axis, dim in sides:
        size, length = (lax.axis_size(axis), x.shape[dim])
        up = [(i, (i + 1) % size) for i in range(size - 1)]
        down = [(j, i) for i, j in up]
        last = lax.slice_in_dim(x, length - width, length, axis=dim)
        initial = lax.slice_in_dim(x, 0, width, axis=dim)
        before = lax.ppermute(last, axis, up)
        after = lax.ppermute(initial, axis, down)
        x = jnp.concatenate([before, x, after], axis=dim)
    return x


def layer_norm(values, gain):
    values = values.astype(jnp.float32)
    center = values - jnp.mean(values, axis=-1, keepdims=True)
    spread = jnp.mean(center * center, axis=-1, keepdims=True)
    return center * lax.rsqrt(spread + 1e-05) * gain


def local(
    frames,
    lengths,
    routes,
    norm_conv,
    point_in,
    depth_kernel,
    bn_scale,
    bn_shift,
    point_out,
    norm_moe,
    router,
    gate_weight,
    up_weight,
    down_weight,
):
    frame_rows = frames[0]
    token_count = frame_rows.shape[0]
    model_width = frame_rows.shape[1]
    position = lax.axis_index("seq") * token_count + jnp.arange(token_count, dtype=jnp.int32)
    frame_mask = (position < lengths[0]).astype(jnp.float32)[:, None]
    conv_in = layer_norm(frame_rows, norm_conv).astype(jnp.bfloat16)
    lifted = jnp.dot(conv_in, point_in, preferred_element_type=jnp.float32)
    gated = (lifted[:, :model_width] * jax.nn.sigmoid(lifted[:, model_width:]) * frame_mask).astype(
        jnp.bfloat16
    )
    reach = depth_kernel.shape[0] // 2
    padded = padded_2(gated, (("seq", 0),), reach)
    depth = jnp.zeros((token_count, model_width), jnp.float32)
    for offset in range(depth_kernel.shape[0]):
        depth = (
            depth + padded[offset : offset + token_count].astype(jnp.float32) * depth_kernel[offset]
        )
    swished = jax.nn.silu(depth * bn_scale + bn_shift).astype(jnp.bfloat16)
    residual = frame_rows.astype(jnp.float32) + jnp.dot(
        swished, point_out, preferred_element_type=jnp.float32
    )
    moe_in = layer_norm(residual, norm_moe).astype(jnp.bfloat16)
    logits = jnp.dot(moe_in, router, preferred_element_type=jnp.float32)
    seq_count = lax.axis_size("seq")
    expert_count = seq_count * lax.axis_size("expert")
    capacity = 3 * token_count // expert_count
    choice_ids = routes[0]
    expert_ids = jnp.arange(expert_count, dtype=jnp.int32)
    pick_one = (choice_ids[:, 0:1] == expert_ids[None, :]).astype(jnp.int32)
    pick_two = (choice_ids[:, 1:2] == expert_ids[None, :]).astype(jnp.int32)
    logit_one = jnp.sum(logits * pick_one.astype(jnp.float32), axis=1)
    logit_two = jnp.sum(logits * pick_two.astype(jnp.float32), axis=1)
    weight_one = jax.nn.sigmoid(logit_one - logit_two)
    weight_two = jax.nn.sigmoid(logit_two - logit_one)
    both = pick_one + pick_two
    earlier = jnp.cumsum(both, axis=0) - both
    place_one = choice_ids[:, 0] * capacity + jnp.sum(earlier * pick_one, axis=1)
    place_two = choice_ids[:, 1] * capacity + jnp.sum(earlier * pick_two, axis=1)
    slot_ids = jnp.arange(expert_count * capacity, dtype=jnp.int32)
    slot_one = (place_one[:, None] == slot_ids[None, :]).astype(jnp.bfloat16)
    slot_two = (place_two[:, None] == slot_ids[None, :]).astype(jnp.bfloat16)
    outgoing = lax.dot_general(
        slot_one + slot_two, moe_in, (((0,), (0,)), ((), ())), preferred_element_type=jnp.float32
    ).astype(jnp.bfloat16)
    outgoing = outgoing.reshape(expert_count, capacity, model_width)
    gate_local = gate_weight[0]
    up_local = up_weight[0]
    down_local = down_weight[0]
    arrived = lax.all_to_all(outgoing, ("seq", "expert"), split_axis=0, concat_axis=0, tiled=True)
    arrived_shape = arrived.shape
    shard_rows = lax.all_gather(arrived.reshape(-1, arrived_shape[2]), "dp", axis=0, tiled=True)
    gate_part = jnp.dot(shard_rows, gate_local, preferred_element_type=jnp.float32)
    up_part = jnp.dot(shard_rows, up_local, preferred_element_type=jnp.float32)
    hidden = (jax.nn.silu(gate_part) * up_part).astype(jnp.bfloat16)
    summed = lax.psum_scatter(
        lax.dot_general(
            hidden, down_local, (((1,), (1,)), ((), ())), preferred_element_type=jnp.float32
        ).astype(jnp.bfloat16),
        "dp",
        scatter_dimension=0,
        tiled=True,
    )
    served = summed.reshape(arrived_shape)
    returned_rows = lax.all_to_all(
        served, ("seq", "expert"), split_axis=0, concat_axis=0, tiled=True
    )
    returned_rows = returned_rows.reshape(expert_count * capacity, model_width)
    from_one = jnp.dot(slot_one, returned_rows, preferred_element_type=jnp.float32)
    from_two = jnp.dot(slot_two, returned_rows, preferred_element_type=jnp.float32)
    layer_out = (
        residual + weight_one[:, None] * from_one + weight_two[:, None] * from_two
    ) * frame_mask
    return layer_out.astype(jnp.bfloat16)[None]


def solution(mesh):
    return jax.shard_map(
        local,
        mesh=mesh,
        in_specs=(
            P(("dp", "expert"), "seq", None),
            P(("dp", "expert")),
            P(("dp", "expert"), "seq", None),
            P(),
            P(),
            P(),
            P(),
            P(),
            P(),
            P(),
            P(),
            P(("seq", "expert"), None, "dp"),
            P(("seq", "expert"), None, "dp"),
            P(("seq", "expert"), None, "dp"),
        ),
        out_specs=P(("dp", "expert"), "seq", None),
        check_vma=False,
    )
```

profile of v0, /device:TPU:1, one launch (start us, length us, event | category | flops | bytes accessed | tf_op | source)
XLA Modules:
  0.0 224.1 jit_solution(1226122052598003649)
XLA Ops:
  7.3 1.1 convert_reduce_fusion
  8.4 1.2 fusion.13
  9.7 3.1 %fusion.22 = f32[128,2048]{1,0:T(8,128)S(1)} fusion(bf16[1024,2048]{1,0:T(8,128)(2,1)} %param.18, bf16[1,128,1024]{2,1,0:T(8,128)(2,1)} %param.14, f32[1024]{0:T(1024)} %param.17, f32[128]{0:T(128)S(1)} %add_rsqrt_fusion.1, f32[128]{0:T(128)S(1)} %broadcast_multiply_fusion.1), kind=kOutput, calls=%fused_computation.61 | convolution fusion | flops 537526272 | bytes 5510144 | tf_op jit(solution)/shard_map/dot_general | solution.py:49
  13.0 4.4 %collective-permute-start = (bf16[15,1024]{1,0:T(8,128)(2,1)S(1)}, bf16[15,1024]{1,0:T(8,128)(2,1)S(1)}, u32[]{:S(2)}, u32[]{:S(2)}) collective-permute-start(bf16[15,1024]{1,0:T(8,128)(2,1)S(1)} %get-tuple-element.9), channel_id=1, source_target_pairs={{0,8},{8,16},{16,24},{24,32},{32,40},{40,48},{48,56},{1,9},{9,17},... | collective-permute-start | bytes 92168 | tf_op jit(solution)/shard_map/ppermute | solution.py:14
  17.4 1.3 collective-permute-start.1
  19.2 3.0 %collective-permute-done.1 = bf16[15,1024]{1,0:T(8,128)(2,1)S(1)} collective-permute-done((bf16[15,1024]{1,0:T(8,128)(2,1)S(1)}, bf16[15,1024]{1,0:T(8,128)(2,1)S(1)}, u32[]{:S(2)}, u32[]{:S(2)}) %collective-permute-start.1) | collective-permute-done | bytes 30752 | tf_op jit(solution)/shard_map/ppermute | solution.py:15
  22.2 5.0 %fusion.76 = (f32[128]{0:T(128)S(1)}, f32[128,1024]{1,0:T(8,128)S(1)}) fusion(bf16[1024,1024]{1,0:T(8,128)(2,1)} %param.22, bf16[128,1024]{1,0:T(8,128)(2,1)S(1)} %fusion.21, bf16[15,1024]{1,0:T(8,128)(2,1)S(1)} %collective-permute-done.1, bf16[15,1024]{1,0:T(8,128)(2,1)S(1)} %collective-permute-done, f32[1024]{0:T(1024)S(1)} %copy-done.8, ...), kind=kOutput, calls=%fused_computation.154 | convolution fusion | flops 293601152 | bytes 3342848 | tf_op jit(solution)/shard_map/dot_general | solution.py:61
  27.2 0.2 multiply_reduce_fusion
  27.6 0.7 copy-done.1
  28.3 0.5 convolution_convert_fusion.1
  28.8 1.3 reshape.67
  30.1 41.5 %all_to_all.10 = bf16[64,6,1024]{2,1,0:T(8,128)(2,1)} all-to-all(bf16[64,6,1024]{2,1,0:T(8,128)(2,1)} %reshape.67), channel_id=1, replica_groups=mesh['dp'=4,'seq'=8,'expert'=8] {'seq','expert'}, dimensions={0} | all-to-all | bytes 1572864 | tf_op jit(solution)/shard_map/all_to_all | solution.py:91
  71.6 2.2 reshape.68
  73.8 39.1 %all-gather.2.cloned.1.call-done = bf16[1536,1024]{1,0:T(8,128)(2,1)} async-done(((bf16[384,1024]{1,0:T(8,128)(2,1)}), bf16[1536,1024]{1,0:T(8,128)(2,1)}) %all-gather.2.cloned.1.call-update) | async-done | bytes 3145744 | tf_op jit(solution)/shard_map/all_gather | solution.py:93
  112.9 7.3 %fusion.3 = f32[1536,1024]{1,0:T(8,128)} fusion(bf16[1536,1024]{1,0:T(8,128)(2,1)} %all-gather.2.cloned.1.call-done, bf16[1,1024,1024]{2,1,0:T(8,128)(2,1)S(1)} %copy-done), kind=kOutput, calls=%fused_computation.4 | convolution fusion | flops 3221225472 | bytes 11534336 | tf_op jit(solution)/shard_map/dot_general | solution.py:94
  120.2 11.7 %convolution_convert_fusion = bf16[1536,1024]{1,0:T(8,128)(2,1)} fusion(f32[1536,1024]{1,0:T(8,128)} %fusion.3, bf16[1536,1024]{1,0:T(8,128)(2,1)} %all-gather.2.cloned.1.call-done, bf16[1,1024,1024]{2,1,0:T(8,128)(2,1)} %param.27, bf16[1,1024,1024]{2,1,0:T(8,128)(2,1)} %param.26), kind=kOutput, calls=%fused_computation.1 | convolution fusion | flops 6453460992 | bytes 16777216 | tf_op jit(solution)/shard_map/dot_general | solution.py:98
  131.9 41.3 %reduce-scatter.2.cloned.1.call-done = bf16[384,1024]{1,0:T(8,128)(2,1)} async-done(((bf16[1536,1024]{1,0:T(8,128)(2,1)}), bf16[384,1024]{1,0:T(8,128)(2,1)}) %reduce-scatter.2.cloned.1.call-update) | async-done | bytes 786448 | tf_op jit(solution)/shard_map/reduce_scatter | solution.py:97
  173.2 2.2 reshape.69
  175.4 10.9 %all-to-all-start.1 = ((bf16[64,6,1024]{2,1,0:T(8,128)(2,1)}), bf16[64,6,1024]{2,1,0:T(8,128)(2,1)}, u32[]{:S(2)}, u32[]{:S(2)}) async-start(bf16[64,6,1024]{2,1,0:T(8,128)(2,1)} %reshape.69), calls=%async_computation.2 | async-start | bytes 2097152 | tf_op jit(solution)/shard_map/all_to_all | solution.py:106
  186.3 0.2 fusion.67
  186.6 27.8 %all-to-all-done.1 = bf16[64,6,1024]{2,1,0:T(8,128)(2,1)} async-done(((bf16[64,6,1024]{2,1,0:T(8,128)(2,1)}), bf16[64,6,1024]{2,1,0:T(8,128)(2,1)}, u32[]{:S(2)}, u32[]{:S(2)}) %all-to-all-start.1) | async-done | bytes 786464 | tf_op jit(solution)/shard_map/all_to_all | solution.py:106
  214.4 1.4 reshape.70
  215.8 0.4 fusion.7
  216.2 1.1 fusion.9
  (42 shorter events, 1.0 us)
Async XLA Ops:
  6.5 106.4 %copy-start = (bf16[1,1024,1024]{2,1,0:T(8,128)(2,1)S(1)}, bf16[1,1024,1024]{2,1,0:T(8,128)(2,1)}, u32[]{:S(2)}) copy-start(bf16[1,1024,1024]{2,1,0:T(8,128)(2,1)} %param.25) | copy-start | bytes 6291460
  6.5 106.4 %all-gather.2.cloned.1.call-start = ((), (), s32[]{:S(2)}) async-start(), calls=%async_computation.3 | async-start | bytes 3932160 | tf_op jit(solution)/shard_map/all_gather | solution.py:93
  9.6 9.1 %copy-start.5 = (f32[31,1024]{1,0:T(8,128)S(1)}, f32[31,1024]{1,0:T(8,128)}, u32[]{:S(2)}) copy-start(f32[31,1024]{1,0:T(8,128)} %param.19) | copy-start | bytes 380932
  9.6 9.2 %copy-start.7 = (s32[1,128,2]{1,2,0:T(2,128)S(1)}, s32[1,128,2]{1,2,0:T(2,128)}, u32[]{:S(2)}) copy-start(s32[1,128,2]{1,2,0:T(2,128)} %param.16) | copy-start | bytes 3076
  9.6 12.6 %copy-start.3 = (bf16[1,128,1024]{2,1,0:T(8,128)(2,1)S(1)}, bf16[1,128,1024]{2,1,0:T(8,128)(2,1)}, u32[]{:S(2)}) copy-start(bf16[1,128,1024]{2,1,0:T(8,128)(2,1)} %param.14) | copy-start | bytes 786436
  9.6 12.6 %copy-start.8 = (f32[1024]{0:T(1024)S(1)}, f32[1024]{0:T(1024)}, u32[]{:S(2)}) copy-start(f32[1024]{0:T(1024)} %param.21) | copy-start | bytes 12292
  9.7 12.6 %copy-start.9 = (f32[1024]{0:T(1024)S(1)}, f32[1024]{0:T(1024)}, u32[]{:S(2)}) copy-start(f32[1024]{0:T(1024)} %param.20) | copy-start | bytes 12292
  13.0 6.2 %collective-permute-start = (bf16[15,1024]{1,0:T(8,128)(2,1)S(1)}, bf16[15,1024]{1,0:T(8,128)(2,1)S(1)}, u32[]{:S(2)}, u32[]{:S(2)}) collective-permute-start(bf16[15,1024]{1,0:T(8,128)(2,1)S(1)} %get-tuple-element.9), channel_id=1, source_target_pairs={{0,8},{8,16},{16,24},{24,32},{32,40},{40,48},{48,56},{1,9},{9,17},... | collective-permute-start | bytes 92168 | tf_op jit(solution)/shard_map/ppermute | solution.py:14
  17.4 4.8 %collective-permute-start.1 = (bf16[15,1024]{1,0:T(8,128)(2,1)S(1)}, bf16[15,1024]{1,0:T(8,128)(2,1)S(1)}, u32[]{:S(2)}, u32[]{:S(2)}) collective-permute-start(bf16[15,1024]{1,0:T(8,128)(2,1)S(1)} %get-tuple-element.10), channel_id=1, source_target_pairs={{8,0},{16,8},{24,16},{32,24},{40,32},{48,40},{56,48},{9,1},{17,9},... | collective-permute-start | bytes 92168 | tf_op jit(solution)/shard_map/ppermute | solution.py:15
  22.2 5.2 %copy-start.6 = (f32[1024]{0:T(1024)S(1)}, f32[1024]{0:T(1024)}, u32[]{:S(2)}) copy-start(f32[1024]{0:T(1024)} %param.23) | copy-start | bytes 12292
  27.6 0.7 copy-start.1
  73.8 99.4 %reduce-scatter.2.cloned.1.call-start = ((), (), s32[]{:S(2)}) async-start(), calls=%async_computation.4 | async-start | bytes 3932160 | tf_op jit(solution)/shard_map/reduce_scatter | solution.py:97
  131.9 54.4 %copy-start.2 = (bf16[128,1024]{1,0:T(8,128)(2,1)S(1)}, bf16[128,1024]{1,0:T(8,128)(2,1)}, u32[]{:S(2)}) copy-start(bf16[128,1024]{1,0:T(8,128)(2,1)} %copy-done.1) | copy-start | bytes 786436
  131.9 54.5 %copy-start.4 = (bf16[1024,64]{0,1:T(8,128)(2,1)S(1)}, bf16[1024,64]{0,1:T(8,128)(2,1)}, u32[]{:S(2)}) copy-start(bf16[1024,64]{0,1:T(8,128)(2,1)} %param.24) | copy-start | bytes 393220
  175.4 39.0 %all-to-all-start.1 = ((bf16[64,6,1024]{2,1,0:T(8,128)(2,1)}), bf16[64,6,1024]{2,1,0:T(8,128)(2,1)}, u32[]{:S(2)}, u32[]{:S(2)}) async-start(bf16[64,6,1024]{2,1,0:T(8,128)(2,1)} %reshape.69), calls=%async_computation.2 | async-start | bytes 2097152 | tf_op jit(solution)/shard_map/all_to_all | solution.py:106
Sparse Core Ops, SparseCore 0:
  73.9 38.9 all-gather.1
  132.0 41.1 reduce-scatter.1
where the time goes:
time: 225 us; the launch traced here: 224 us
  waiting for transfers between devices  111 us (49%)
  blocking collectives  41.5 us (18%)
  matrix products  29.1 us (13%)
  starting transfers between devices  16.6 us (7%)
  between operations  14.5 us (6%)
  local copies, waits for them, and re-layouts  8.08 us (4%)
  other arithmetic  3.03 us (1%)
    all_to_all x1, blocking collectives, local(): lax.all_to_all(outgoing, ('seq', 'expert'), split_axis=0, concat_axis=0,...  41.5 us
    reduce_scatter x1, waiting for transfers between devices, local(): lax.psum_scatter(lax.dot_general(hidden, down_local, (((1,), (1,)), ((),...  41.3 us
    all_gather x1, waiting for transfers between devices, local(): lax.all_gather(arrived.reshape(-1, arrived_shape[2]), 'dp', axis=0, tiled...  39.1 us
    all_to_all x1, waiting for transfers between devices, local(): lax.all_to_all(served, ('seq', 'expert'), split_axis=0, concat_axis=0, ti...  27.8 us
    dot_general x1, matrix products, local(): lax.dot_general(hidden, down_local, (((1,), (1,)), ((), ())), preferred_e...  11.7 us
    all_to_all x1, starting transfers between devices, local(): lax.all_to_all(served, ('seq', 'expert'), split_axis=0, concat_axis=0, ti...  10.9 us
    dot_general x1, matrix products, local(): jnp.dot(shard_rows, gate_local, preferred_element_type=jnp.float32)  7.26 us
    dot_general x1, matrix products, local(): jnp.dot(swished, point_out, preferred_element_type=jnp.float32)  4.96 us
  transfers between devices with their start and end apart: 5, of which 4 were waited for; matrix products, arithmetic and copies ran while one was open for 0% of the time, Pallas kernels for 0%

commit v1 on v0

--- a/solution.py
+++ b/solution.py
@@ -15,6 +15,35 @@
         after = lax.ppermute(initial, axis, down)
         x = jnp.concatenate([before, x, after], axis=dim)
     return x
+
+
+def ring_gather(rows, axis):
+    size = lax.axis_size(axis)
+    up = [(i, (i + 1) % size) for i in range(size)]
+    down = [(i, (i - 1) % size) for i in range(size)]
+    half = rows.shape[0] // 2
+    from_below = lax.ppermute(rows, axis, up)
+    from_above = lax.ppermute(rows, axis, down)
+    far = jnp.concatenate(
+        [lax.ppermute(from_below[:half], axis, up), lax.ppermute(from_above[half:], axis, down)], axis=0
+    )
+    return jnp.concatenate([rows, from_below, from_above, far], axis=0)
+
+
+def ring_scatter(partial, axis, count):
+    size = lax.axis_size(axis)
+    up = [(i, (i + 1) % size) for i in range(size)]
+    down = [(i, (i - 1) % size) for i in range(size)]
+    half = count // 2
+    own, to_below, to_above, far = (partial[i * count : (i + 1) * count] for i in range(4))
+    far = far.astype(jnp.bfloat16)
+    far_up = lax.ppermute(far[:half], axis, up).astype(jnp.float32)
+    far_down = lax.ppermute(far[half:], axis, down).astype(jnp.float32)
+    send_up = to_above + jnp.concatenate([far_up, jnp.zeros_like(far_down)], axis=0)
+    send_down = to_below + jnp.concatenate([jnp.zeros_like(far_up), far_down], axis=0)
+    got_below = lax.ppermute(send_up.astype(jnp.bfloat16), axis, up).astype(jnp.float32)
+    got_above = lax.ppermute(send_down.astype(jnp.bfloat16), axis, down).astype(jnp.float32)
+    return own + got_below + got_above
 
 
 def layer_norm(values, gain):
@@ -90,19 +119,16 @@
     down_local = down_weight[0]
     arrived = lax.all_to_all(outgoing, ("seq", "expert"), split_axis=0, concat_axis=0, tiled=True)
     arrived_shape = arrived.shape
-    shard_rows = lax.all_gather(arrived.reshape(-1, arrived_shape[2]), "dp", axis=0, tiled=True)
+    own_rows = arrived.reshape(-1, arrived_shape[2])
+    shard_rows = ring_gather(own_rows, "dp")
     gate_part = jnp.dot(shard_rows, gate_local, preferred_element_type=jnp.float32)
     up_part = jnp.dot(shard_rows, up_local, preferred_element_type=jnp.float32)
     hidden = (jax.nn.silu(gate_part) * up_part).astype(jnp.bfloat16)
-    summed = lax.psum_scatter(
-        lax.dot_general(
-            hidden, down_local, (((1,), (1,)), ((), ())), preferred_element_type=jnp.float32
-        ).astype(jnp.bfloat16),
-        "dp",
-        scatter_dimension=0,
-        tiled=True,
+    partial = lax.dot_general(
+        hidden, down_local, (((1,), (1,)), ((), ())), preferred_element_type=jnp.float32
     )
-    served = summed.reshape(arrived_shape)
+    summed = ring_scatter(partial, "dp", own_rows.shape[0])
+    served = summed.astype(jnp.bfloat16).reshape(arrived_shape)
     returned_rows = lax.all_to_all(
         served, ("seq", "expert"), split_axis=0, concat_axis=0, tiled=True
     )

time: 225 us -> 195 us (0.87)
  waiting for transfers between devices: 111 us -> 74.7 us
  starting transfers between devices: 16.6 us -> 31.3 us
  between operations: 14.5 us -> 1.21 us
  other arithmetic: 3.03 us -> 7.13 us
    ppermute x0 -> x8, waiting for transfers between devices: none -> 44.8 us  [the longest x1 15.7 us: ring_gather(): from_above = lax.ppermute(rows, axis, down)]
    reduce_scatter x1 -> x0, waiting for transfers between devices: 41.3 us -> none  [local(): lax.psum_scatter(lax.dot_general(hidden, down_local, (((1,), (1,)), ((),...]
    all_gather x1 -> x0, waiting for transfers between devices: 39.1 us -> none  [local(): lax.all_gather(arrived.reshape(-1, arrived_shape[2]), 'dp', axis=0, tiled...]
    ppermute x0 -> x8, starting transfers between devices: none -> 12 us  [the longest x1 3.49 us: ring_gather(): lax.ppermute(from_above[half:], axis, down)]
    convert_element_type x0 -> x2, other arithmetic: none -> 4.1 us  [the longest x1 2.29 us: ring_scatter(): send_up.astype(jnp.bfloat16)]
    all_to_all x1, starting transfers between devices: 10.9 us -> 13.6 us  [local(): lax.all_to_all(served, ('seq', 'expert'), split_axis=0, concat_axis=0, ti...]
  transfers between devices with their start and end apart: 5 -> 11, of which waited for: 4 -> 6; matrix products, arithmetic and copies ran while one was open for 0% -> 1% of each run, Pallas kernels for 0% -> 0%
where the time goes in v1:
time: 195 us
  waiting for transfers between devices  74.7 us (38%)
  blocking collectives  41.5 us (21%)
  starting transfers between devices  31.3 us (16%)
  matrix products  29.3 us (15%)
  local copies, waits for them, and re-layouts  9.37 us (5%)
  other arithmetic  7.13 us (4%)
    all_to_all x1, blocking collectives, local(): lax.all_to_all(outgoing, ('seq', 'expert'), split_axis=0, concat_axis=0,...  41.5 us
    all_to_all x1, waiting for transfers between devices, local(): lax.all_to_all(served, ('seq', 'expert'), split_axis=0, concat_axis=0, ti...  26.9 us
    ppermute x1, waiting for transfers between devices, ring_gather(): from_above = lax.ppermute(rows, axis, down)  15.7 us
    ppermute x1, waiting for transfers between devices, ring_scatter(): lax.ppermute(send_up.astype(jnp.bfloat16), axis, up).astype(jnp.float32)  13.6 us
    all_to_all x1, starting transfers between devices, local(): lax.all_to_all(served, ('seq', 'expert'), split_axis=0, concat_axis=0, ti...  13.6 us
    dot_general x1, matrix products, local(): lax.dot_general(hidden, down_local, (((1,), (1,)), ((), ())), preferred_e...  12.2 us
    ppermute x1, waiting for transfers between devices, ring_gather(): lax.ppermute(from_below[:half], axis, up)  9.4 us
    ppermute x1, waiting for transfers between devices, ring_scatter(): far_up = lax.ppermute(far[:half], axis, up).astype(jnp.float32)  6.06 us
  transfers between devices with their start and end apart: 11, of which 6 were waited for; matrix products, arithmetic and copies ran while one was open for 1% of the time, Pallas kernels for 0%

profile of v1, /device:TPU:1, one launch (start us, length us, event | category | flops | bytes accessed | tf_op | source)
XLA Modules:
  0.0 194.5 jit_solution(12367276500139985302)
XLA Ops:
  3.1 3.1 %fusion.31 = f32[128,2048]{1,0:T(8,128)S(1)} fusion(bf16[1024,2048]{1,0:T(8,128)(2,1)} %param.18, bf16[1,128,1024]{2,1,0:T(8,128)(2,1)} %param.14, f32[1024]{0:T(1024)} %param.17, f32[128]{0:T(128)S(1)} %add_rsqrt_fusion.1, f32[128]{0:T(128)S(1)} %broadcast_multiply_fusion.1), kind=kOutput, calls=%fused_computation.69 | convolution fusion | flops 537526272 | bytes 5510144 | tf_op jit(solution)/shard_map/dot_general | solution.py:78
  6.5 4.4 %collective-permute-start = (bf16[15,1024]{1,0:T(8,128)(2,1)S(1)}, bf16[15,1024]{1,0:T(8,128)(2,1)S(1)}, u32[]{:S(2)}, u32[]{:S(2)}) collective-permute-start(bf16[15,1024]{1,0:T(8,128)(2,1)S(1)} %get-tuple-element.13), channel_id=1, source_target_pairs={{0,8},{8,16},{16,24},{24,32},{32,40},{40,48},{48,56},{1,9},{9,17},... | collective-permute-start | bytes 92168 | tf_op jit(solution)/shard_map/ppermute | solution.py:14
  10.9 1.3 collective-permute-start.1
  12.7 3.0 %collective-permute-done.1 = bf16[15,1024]{1,0:T(8,128)(2,1)S(1)} collective-permute-done((bf16[15,1024]{1,0:T(8,128)(2,1)S(1)}, bf16[15,1024]{1,0:T(8,128)(2,1)S(1)}, u32[]{:S(2)}, u32[]{:S(2)}) %collective-permute-start.1) | collective-permute-done | bytes 30752 | tf_op jit(solution)/shard_map/ppermute | solution.py:15
  15.7 5.0 %fusion.86 = (f32[128]{0:T(128)S(1)}, f32[128,1024]{1,0:T(8,128)S(1)}) fusion(bf16[1024,1024]{1,0:T(8,128)(2,1)} %param.22, bf16[128,1024]{1,0:T(8,128)(2,1)S(1)} %fusion.30, bf16[15,1024]{1,0:T(8,128)(2,1)S(1)} %collective-permute-done.1, bf16[15,1024]{1,0:T(8,128)(2,1)S(1)} %collective-permute-done, f32[1024]{0:T(1024)S(1)} %copy-done.10, ...), kind=kOutput, calls=%fused_computation.168 | convolution fusion | flops 293601152 | bytes 3342848 | tf_op jit(solution)/shard_map/dot_general | solution.py:90
  23.5 41.5 %all_to_all.10 = bf16[64,6,1024]{2,1,0:T(8,128)(2,1)} all-to-all(bf16[64,6,1024]{2,1,0:T(8,128)(2,1)} %reshape.67), channel_id=1, replica_groups=mesh['dp'=4,'seq'=8,'expert'=8] {'seq','expert'}, dimensions={0} | all-to-all | bytes 1572864 | tf_op jit(solution)/shard_map/all_to_all | solution.py:120
  65.0 1.4 reshape.68
  66.4 2.8 %collective-permute-start.3 = (bf16[384,1024]{1,0:T(8,128)(2,1)S(1)}, bf16[384,1024]{1,0:T(8,128)(2,1)S(1)}, u32[]{:S(2)}, u32[]{:S(2)}) collective-permute-start(bf16[384,1024]{1,0:T(8,128)(2,1)S(1)} %reshape.68), channel_id=1, source_target_pairs={{0,192},{64,0},{128,64},{192,128},{1,193},{65,1},{129,65},{193,129... | collective-permute-start | bytes 2359304 | tf_op jit(solution)/shard_map/ppermute | solution.py:26
  69.2 15.7 %collective-permute-done.3 = bf16[384,1024]{1,0:T(8,128)(2,1)S(1)} collective-permute-done((bf16[384,1024]{1,0:T(8,128)(2,1)S(1)}, bf16[384,1024]{1,0:T(8,128)(2,1)S(1)}, u32[]{:S(2)}, u32[]{:S(2)}) %collective-permute-start.3) | collective-permute-done | bytes 786464 | tf_op jit(solution)/shard_map/ppermute | solution.py:26
  85.0 3.5 %collective-permute-start.5 = (bf16[192,1024]{1,0:T(8,128)(2,1)S(1)}, bf16[192,1024]{1,0:T(8,128)(2,1)S(1)}, u32[]{:S(2)}, u32[]{:S(2)}) collective-permute-start(bf16[192,1024]{1,0:T(8,128)(2,1)S(1)} %slice.393), channel_id=1, source_target_pairs={{0,192},{64,0},{128,64},{192,128},{1,193},{65,1},{129,65},{193,129... | collective-permute-start | bytes 1179656 | tf_op jit(solution)/shard_map/ppermute | solution.py:28
  89.0 9.4 %collective-permute-done.4 = bf16[192,1024]{1,0:T(8,128)(2,1)S(1)} collective-permute-done((bf16[192,1024]{1,0:T(8,128)(2,1)S(1)}, bf16[192,1024]{1,0:T(8,128)(2,1)S(1)}, u32[]{:S(2)}, u32[]{:S(2)}) %collective-permute-start.4) | collective-permute-done | bytes 393248 | tf_op jit(solution)/shard_map/ppermute | solution.py:28
  98.5 1.6 copy-done.3
  100.1 5.3 %fusion.8 = f32[1536,1024]{1,0:T(8,128)} fusion(bf16[1536,1024]{1,0:T(8,128)(2,1)S(1)} %constant_dynamic-update-slice_fusion, bf16[1,1024,1024]{2,1,0:T(8,128)(2,1)S(1)} %copy-done.9), kind=kOutput, calls=%fused_computation.5 | convolution fusion | flops 3221225472 | bytes 11534336 | tf_op jit(solution)/shard_map/dot_general | solution.py:124
  105.4 12.2 %fusion.87 = (bf16[1536,1024]{1,0:T(8,128)(2,1)}, f32[1536,1024]{1,0:T(8,128)}) fusion(bf16[1,1024,1024]{2,1,0:T(8,128)(2,1)S(1)} %copy-done, f32[1536,1024]{1,0:T(8,128)} %fusion.8, bf16[1536,1024]{1,0:T(8,128)(2,1)} %copy-done.3, bf16[1,1024,1024]{2,1,0:T(8,128)(2,1)} %param.26), kind=kOutput, calls=%fused_computation.169 | convolution fusion | flops 6453460992 | bytes 23068672 | tf_op jit(solution)/shard_map/dot_general | solution.py:127
  118.8 2.7 %collective-permute-start.8 = (bf16[192,1024]{1,0:T(8,128)(2,1)S(1)}, bf16[192,1024]{1,0:T(8,128)(2,1)S(1)}, u32[]{:S(2)}, u32[]{:S(2)}) collective-permute-start(bf16[192,1024]{1,0:T(8,128)(2,1)S(1)} %get-tuple-element.12), channel_id=1, source_target_pairs={{0,192},{64,0},{128,64},{192,128},{1,193},{65,1},{129,65},{193,129... | collective-permute-start | bytes 1179656 | tf_op jit(solution)/shard_map/ppermute | solution.py:41
  121.5 6.1 %collective-permute-done.6 = bf16[192,1024]{1,0:T(8,128)(2,1)S(1)} collective-permute-done((bf16[192,1024]{1,0:T(8,128)(2,1)S(1)}, bf16[192,1024]{1,0:T(8,128)(2,1)S(1)}, u32[]{:S(2)}, u32[]{:S(2)}) %collective-permute-start.6) | collective-permute-done | bytes 393248 | tf_op jit(solution)/shard_map/ppermute | solution.py:40
  127.5 2.3 %fusion.11 = (bf16[384,1024]{1,0:T(8,128)(2,1)S(1)}, bf16[384,1024]{1,0:T(8,128)(2,1)S(1)}) fusion(f32[1536,1024]{1,0:T(8,128)} %get-tuple-element.55, bf16[192,1024]{1,0:T(8,128)(2,1)S(1)} %collective-permute-done.6, bf16[192,1024]{1,0:T(8,128)(2,1)S(1)} %collective-permute-done.8), kind=kLoop, calls=%fused_computation.10 | loop fusion | flops 2359296 | bytes 5505024 | tf_op jit(solution)/shard_map/convert_element_type | solution.py:44
  129.9 2.7 %collective-permute-start.9 = (bf16[384,1024]{1,0:T(8,128)(2,1)S(1)}, bf16[384,1024]{1,0:T(8,128)(2,1)S(1)}, u32[]{:S(2)}, u32[]{:S(2)}) collective-permute-start(bf16[384,1024]{1,0:T(8,128)(2,1)S(1)} %get-tuple-element.10), channel_id=1, source_target_pairs={{0,192},{64,0},{128,64},{192,128},{1,193},{65,1},{129,65},{193,129... | collective-permute-start | bytes 2359304 | tf_op jit(solution)/shard_map/ppermute | solution.py:45
  132.6 13.6 %collective-permute-done.7 = bf16[384,1024]{1,0:T(8,128)(2,1)S(1)} collective-permute-done((bf16[384,1024]{1,0:T(8,128)(2,1)S(1)}, bf16[384,1024]{1,0:T(8,128)(2,1)S(1)}, u32[]{:S(2)}, u32[]{:S(2)}) %collective-permute-start.7) | collective-permute-done | bytes 786464 | tf_op jit(solution)/shard_map/ppermute | solution.py:44
  146.2 1.8 fusion.13
  149.3 13.6 %all-to-all-start.1 = ((bf16[64,6,1024]{2,1,0:T(8,128)(2,1)}), bf16[64,6,1024]{2,1,0:T(8,128)(2,1)}, u32[]{:S(2)}, u32[]{:S(2)}) async-start(bf16[64,6,1024]{2,1,0:T(8,128)(2,1)} %reshape.69), calls=%async_computation.1 | async-start | bytes 2097152 | tf_op jit(solution)/shard_map/all_to_all | solution.py:132
  164.1 26.9 %all-to-all-done.1 = bf16[64,6,1024]{2,1,0:T(8,128)(2,1)} async-done(((bf16[64,6,1024]{2,1,0:T(8,128)(2,1)}), bf16[64,6,1024]{2,1,0:T(8,128)(2,1)}, u32[]{:S(2)}, u32[]{:S(2)}) %all-to-all-start.1) | async-done | bytes 786464 | tf_op jit(solution)/shard_map/all_to_all | solution.py:132
  191.0 1.4 reshape.70
  192.8 1.7 fusion.18
  (66 shorter events, 10.4 us)
Async XLA Ops:
  0.0 105.4 %copy-start = (bf16[1,1024,1024]{2,1,0:T(8,128)(2,1)S(1)}, bf16[1,1024,1024]{2,1,0:T(8,128)(2,1)}, u32[]{:S(2)}) copy-start(bf16[1,1024,1024]{2,1,0:T(8,128)(2,1)} %param.27) | copy-start | bytes 6291460
  3.1 3.4 %copy-start.8 = (f32[128]{0:T(128)}, f32[128]{0:T(128)S(1)}, u32[]{:S(2)}) copy-start(f32[128]{0:T(128)S(1)} %compare_convert_fusion) | copy-start | bytes 1540
  3.1 9.1 %copy-start.5 = (f32[31,1024]{1,0:T(8,128)S(1)}, f32[31,1024]{1,0:T(8,128)}, u32[]{:S(2)}) copy-start(f32[31,1024]{1,0:T(8,128)} %param.19) | copy-start | bytes 380932
  3.1 9.2 %copy-start.7 = (s32[1,128,2]{1,2,0:T(2,128)S(1)}, s32[1,128,2]{1,2,0:T(2,128)}, u32[]{:S(2)}) copy-start(s32[1,128,2]{1,2,0:T(2,128)} %param.16) | copy-start | bytes 3076
  3.1 12.6 %copy-start.2 = (bf16[1,128,1024]{2,1,0:T(8,128)(2,1)S(1)}, bf16[1,128,1024]{2,1,0:T(8,128)(2,1)}, u32[]{:S(2)}) copy-start(bf16[1,128,1024]{2,1,0:T(8,128)(2,1)} %param.14) | copy-start | bytes 786436
  3.1 12.6 %copy-start.10 = (f32[1024]{0:T(1024)S(1)}, f32[1024]{0:T(1024)}, u32[]{:S(2)}) copy-start(f32[1024]{0:T(1024)} %param.21) | copy-start | bytes 12292
  3.1 12.6 %copy-start.11 = (f32[1024]{0:T(1024)S(1)}, f32[1024]{0:T(1024)}, u32[]{:S(2)}) copy-start(f32[1024]{0:T(1024)} %param.20) | copy-start | bytes 12292
  6.5 6.2 %collective-permute-start = (bf16[15,1024]{1,0:T(8,128)(2,1)S(1)}, bf16[15,1024]{1,0:T(8,128)(2,1)S(1)}, u32[]{:S(2)}, u32[]{:S(2)}) collective-permute-start(bf16[15,1024]{1,0:T(8,128)(2,1)S(1)} %get-tuple-element.13), channel_id=1, source_target_pairs={{0,8},{8,16},{16,24},{24,32},{32,40},{40,48},{48,56},{1,9},{9,17},... | collective-permute-start | bytes 92168 | tf_op jit(solution)/shard_map/ppermute | solution.py:14
  10.9 4.8 %collective-permute-start.1 = (bf16[15,1024]{1,0:T(8,128)(2,1)S(1)}, bf16[15,1024]{1,0:T(8,128)(2,1)S(1)}, u32[]{:S(2)}, u32[]{:S(2)}) collective-permute-start(bf16[15,1024]{1,0:T(8,128)(2,1)S(1)} %get-tuple-element.14), channel_id=1, source_target_pairs={{8,0},{16,8},{24,16},{32,24},{40,32},{48,40},{56,48},{9,1},{17,9},... | collective-permute-start | bytes 92168 | tf_op jit(solution)/shard_map/ppermute | solution.py:15
  15.7 5.2 %copy-start.6 = (f32[1024]{0:T(1024)S(1)}, f32[1024]{0:T(1024)}, u32[]{:S(2)}) copy-start(f32[1024]{0:T(1024)} %param.23) | copy-start | bytes 12292
  21.1 0.7 copy-start.1
  66.4 18.5 %collective-permute-start.3 = (bf16[384,1024]{1,0:T(8,128)(2,1)S(1)}, bf16[384,1024]{1,0:T(8,128)(2,1)S(1)}, u32[]{:S(2)}, u32[]{:S(2)}) collective-permute-start(bf16[384,1024]{1,0:T(8,128)(2,1)S(1)} %reshape.68), channel_id=1, source_target_pairs={{0,192},{64,0},{128,64},{192,128},{1,193},{65,1},{129,65},{193,129... | collective-permute-start | bytes 2359304 | tf_op jit(solution)/shard_map/ppermute | solution.py:26
  69.2 19.3 %collective-permute-start.2 = (bf16[384,1024]{1,0:T(8,128)(2,1)S(1)}, bf16[384,1024]{1,0:T(8,128)(2,1)S(1)}, u32[]{:S(2)}, u32[]{:S(2)}) collective-permute-start(bf16[384,1024]{1,0:T(8,128)(2,1)S(1)} %reshape.68), channel_id=1, source_target_pairs={{0,64},{64,128},{128,192},{192,0},{1,65},{65,129},{129,193},{193,1... | collective-permute-start | bytes 2359304 | tf_op jit(solution)/shard_map/ppermute | solution.py:25
  85.0 13.4 %collective-permute-start.5 = (bf16[192,1024]{1,0:T(8,128)(2,1)S(1)}, bf16[192,1024]{1,0:T(8,128)(2,1)S(1)}, u32[]{:S(2)}, u32[]{:S(2)}) collective-permute-start(bf16[192,1024]{1,0:T(8,128)(2,1)S(1)} %slice.393), channel_id=1, source_target_pairs={{0,192},{64,0},{128,64},{192,128},{1,193},{65,1},{129,65},{193,129... | collective-permute-start | bytes 1179656 | tf_op jit(solution)/shard_map/ppermute | solution.py:28
  88.5 11.6 %copy-start.9 = (bf16[1,1024,1024]{2,1,0:T(8,128)(2,1)S(1)}, bf16[1,1024,1024]{2,1,0:T(8,128)(2,1)}, u32[]{:S(2)}) copy-start(bf16[1,1024,1024]{2,1,0:T(8,128)(2,1)} %param.25) | copy-start | bytes 6291460
  88.5 9.9 %collective-permute-start.4 = (bf16[192,1024]{1,0:T(8,128)(2,1)S(1)}, bf16[192,1024]{1,0:T(8,128)(2,1)S(1)}, u32[]{:S(2)}, u32[]{:S(2)}) collective-permute-start(bf16[192,1024]{1,0:T(8,128)(2,1)S(1)} %slice.392), channel_id=1, source_target_pairs={{0,64},{64,128},{128,192},{192,0},{1,65},{65,129},{129,193},{193,1... | collective-permute-start | bytes 1179656 | tf_op jit(solution)/shard_map/ppermute | solution.py:28
  98.5 1.6 copy-start.3
  118.7 8.8 %collective-permute-start.6 = (bf16[192,1024]{1,0:T(8,128)(2,1)S(1)}, bf16[192,1024]{1,0:T(8,128)(2,1)S(1)}, u32[]{:S(2)}, u32[]{:S(2)}) collective-permute-start(bf16[192,1024]{1,0:T(8,128)(2,1)S(1)} %get-tuple-element.11), channel_id=1, source_target_pairs={{0,64},{64,128},{128,192},{192,0},{1,65},{65,129},{129,193},{193,1... | collective-permute-start | bytes 1179656 | tf_op jit(solution)/shard_map/ppermute | solution.py:40
  118.8 8.7 %collective-permute-start.8 = (bf16[192,1024]{1,0:T(8,128)(2,1)S(1)}, bf16[192,1024]{1,0:T(8,128)(2,1)S(1)}, u32[]{:S(2)}, u32[]{:S(2)}) collective-permute-start(bf16[192,1024]{1,0:T(8,128)(2,1)S(1)} %get-tuple-element.12), channel_id=1, source_target_pairs={{0,192},{64,0},{128,64},{192,128},{1,193},{65,1},{129,65},{193,129... | collective-permute-start | bytes 1179656 | tf_op jit(solution)/shard_map/ppermute | solution.py:41
  129.8 16.4 %collective-permute-start.7 = (bf16[384,1024]{1,0:T(8,128)(2,1)S(1)}, bf16[384,1024]{1,0:T(8,128)(2,1)S(1)}, u32[]{:S(2)}, u32[]{:S(2)}) collective-permute-start(bf16[384,1024]{1,0:T(8,128)(2,1)S(1)} %get-tuple-element.9), channel_id=1, source_target_pairs={{0,64},{64,128},{128,192},{192,0},{1,65},{65,129},{129,193},{193,1... | collective-permute-start | bytes 2359304 | tf_op jit(solution)/shard_map/ppermute | solution.py:44
  129.9 33.0 %copy-start.4 = (bf16[1024,64]{0,1:T(8,128)(2,1)S(1)}, bf16[1024,64]{0,1:T(8,128)(2,1)}, u32[]{:S(2)}) copy-start(bf16[1024,64]{0,1:T(8,128)(2,1)} %param.24) | copy-start | bytes 393220
  129.9 16.3 %collective-permute-start.9 = (bf16[384,1024]{1,0:T(8,128)(2,1)S(1)}, bf16[384,1024]{1,0:T(8,128)(2,1)S(1)}, u32[]{:S(2)}, u32[]{:S(2)}) collective-permute-start(bf16[384,1024]{1,0:T(8,128)(2,1)S(1)} %get-tuple-element.10), channel_id=1, source_target_pairs={{0,192},{64,0},{128,64},{192,128},{1,193},{65,1},{129,65},{193,129... | collective-permute-start | bytes 2359304 | tf_op jit(solution)/shard_map/ppermute | solution.py:45
  149.3 41.7 %all-to-all-start.1 = ((bf16[64,6,1024]{2,1,0:T(8,128)(2,1)}), bf16[64,6,1024]{2,1,0:T(8,128)(2,1)}, u32[]{:S(2)}, u32[]{:S(2)}) async-start(bf16[64,6,1024]{2,1,0:T(8,128)(2,1)} %reshape.69), calls=%async_computation.1 | async-start | bytes 2097152 | tf_op jit(solution)/shard_map/all_to_all | solution.py:132

commit v2 on v1

--- a/solution.py
+++ b/solution.py
@@ -2,6 +2,8 @@
 import jax.numpy as jnp
 from jax import lax
 from jax.sharding import PartitionSpec as P
+
+CHUNKS = 2
 
 
 def padded_2(x, sides, width):
@@ -117,22 +119,27 @@
     gate_local = gate_weight[0]
     up_local = up_weight[0]
     down_local = down_weight[0]
-    arrived = lax.all_to_all(outgoing, ("seq", "expert"), split_axis=0, concat_axis=0, tiled=True)
-    arrived_shape = arrived.shape
-    own_rows = arrived.reshape(-1, arrived_shape[2])
-    shard_rows = ring_gather(own_rows, "dp")
-    gate_part = jnp.dot(shard_rows, gate_local, preferred_element_type=jnp.float32)
-    up_part = jnp.dot(shard_rows, up_local, preferred_element_type=jnp.float32)
-    hidden = (jax.nn.silu(gate_part) * up_part).astype(jnp.bfloat16)
-    partial = lax.dot_general(
-        hidden, down_local, (((1,), (1,)), ((), ())), preferred_element_type=jnp.float32
-    )
-    summed = ring_scatter(partial, "dp", own_rows.shape[0])
-    served = summed.astype(jnp.bfloat16).reshape(arrived_shape)
-    returned_rows = lax.all_to_all(
-        served, ("seq", "expert"), split_axis=0, concat_axis=0, tiled=True
-    )
-    returned_rows = returned_rows.reshape(expert_count * capacity, model_width)
+    returned = []
+    step = capacity // CHUNKS
+    for first in range(0, capacity, step):
+        arrived = lax.all_to_all(
+            outgoing[:, first : first + step], ("seq", "expert"), split_axis=0, concat_axis=0, tiled=True
+        )
+        arrived_shape = arrived.shape
+        own_rows = arrived.reshape(-1, arrived_shape[2])
+        shard_rows = ring_gather(own_rows, "dp")
+        gate_part = jnp.dot(shard_rows, gate_local, preferred_element_type=jnp.float32)
+        up_part = jnp.dot(shard_rows, up_local, preferred_element_type=jnp.float32)
+        hidden = (jax.nn.silu(gate_part) * up_part).astype(jnp.bfloat16)
+        partial = lax.dot_general(
+            hidden, down_local, (((1,), (1,)), ((), ())), preferred_element_type=jnp.float32
+        )
+        summed = ring_scatter(partial, "dp", own_rows.shape[0])
+        served = summed.astype(jnp.bfloat16).reshape(arrived_shape)
+        returned.append(
+            lax.all_to_all(served, ("seq", "expert"), split_axis=0, concat_axis=0, tiled=True)
+        )
+    returned_rows = jnp.concatenate(returned, axis=1).reshape(expert_count * capacity, model_width)
     from_one = jnp.dot(slot_one, returned_rows, preferred_element_type=jnp.float32)
     from_two = jnp.dot(slot_two, returned_rows, preferred_element_type=jnp.float32)
     layer_out = (

time: 195 us -> 205 us (1.051)
  waiting for transfers between devices: 74.7 us -> 45.4 us
  starting transfers between devices: 31.3 us -> 54.2 us
  local copies, waits for them, and re-layouts: 9.37 us -> 23.6 us
  blocking collectives: 41.5 us -> 30.8 us
  matrix products: 29.3 us -> 37.2 us
  other arithmetic: 7.13 us -> 11.7 us
    ppermute x1 -> x2, waiting for transfers between devices: 15.7 us -> 0.01 us  [ring_gather(): from_above = lax.ppermute(rows, axis, down)]
    all_to_all x0 -> x1, waiting for transfers between devices: none -> 12.9 us  [local(): lax.all_to_all(outgoing[:, first:first + step], ('seq', 'expert'), split_...]
    all_to_all x1, blocking collectives: 41.5 us -> 30.8 us  [local(): lax.all_to_all(outgoing[:, first:first + step], ('seq', 'expert'), split_...]
    ppermute x1 -> x2, waiting for transfers between devices: 9.4 us -> 0.01 us  [ring_gather(): lax.ppermute(from_below[:half], axis, up)]
    all_to_all x1 -> x2, waiting for transfers between devices: 26.9 us -> 17.7 us  [local(): lax.all_to_all(served, ('seq', 'expert'), split_axis=0, concat_axis=0, ti...]
    all_to_all x1 -> x2, starting transfers between devices: 13.6 us -> 20.5 us  [local(): lax.all_to_all(served, ('seq', 'expert'), split_axis=0, concat_axis=0, ti...]
    ppermute x1 -> x2, waiting for transfers between devices: 6.06 us -> 0.01 us  [ring_scatter(): far_up = lax.ppermute(far[:half], axis, up).astype(jnp.float32)]
    all_to_all x0 -> x1, starting transfers between devices: none -> 5.69 us  [local(): lax.all_to_all(outgoing[:, first:first + step], ('seq', 'expert'), split_...]
  transfers between devices with their start and end apart: 11 -> 21, of which waited for: 6 -> 6; matrix products, arithmetic and copies ran while one was open for 1% -> 23% of each run, Pallas kernels for 0% -> 0%
where the time goes in v2:
time: 205 us; the launch traced here: 204 us
  starting transfers between devices  54.2 us (26%)
  waiting for transfers between devices  45.4 us (22%)
  matrix products  37.2 us (18%)
  blocking collectives  30.8 us (15%)
  local copies, waits for them, and re-layouts  23.6 us (12%)
  other arithmetic  11.7 us (6%)
    all_to_all x1, blocking collectives, local(): lax.all_to_all(outgoing[:, first:first + step], ('seq', 'expert'), split_...  30.8 us
    all_to_all x2, starting transfers between devices, local(): lax.all_to_all(served, ('seq', 'expert'), split_axis=0, concat_axis=0, ti...  20.5 us
    dot_general x2, matrix products, local(): lax.dot_general(hidden, down_local, (((1,), (1,)), ((), ())), preferred_e...  17.8 us
    all_to_all x2, waiting for transfers between devices, local(): lax.all_to_all(served, ('seq', 'expert'), split_axis=0, concat_axis=0, ti...  17.7 us
    all_to_all x1, waiting for transfers between devices, local(): lax.all_to_all(outgoing[:, first:first + step], ('seq', 'expert'), split_...  12.9 us
    dot_general x2, matrix products, local(): up_part = jnp.dot(shard_rows, up_local, preferred_element_type=jnp.float32)  9.2 us
    ppermute x2, waiting for transfers between devices, ring_scatter(): lax.ppermute(send_up.astype(jnp.bfloat16), axis, up).astype(jnp.float32)  8.75 us
    unnamed x40, local copies, waits for them, and re-layouts  6.87 us
  transfers between devices with their start and end apart: 21, of which 6 were waited for; matrix products, arithmetic and copies ran while one was open for 23% of the time, Pallas kernels for 0%

profile of v2, /device:TPU:1, one launch (start us, length us, event | category | flops | bytes accessed | tf_op | source)
XLA Modules:
  0.0 204.1 jit_solution(2063119049852997426)
XLA Ops:
  3.1 3.1 %fusion.45 = f32[128,2048]{1,0:T(8,128)S(1)} fusion(bf16[1024,2048]{1,0:T(8,128)(2,1)} %param.18, bf16[1,128,1024]{2,1,0:T(8,128)(2,1)} %param.14, f32[1024]{0:T(1024)} %param.17, f32[128]{0:T(128)S(1)} %add_rsqrt_fusion.1, f32[128]{0:T(128)S(1)} %broadcast_multiply_fusion.1), kind=kOutput, calls=%fused_computation.84 | convolution fusion | flops 537526272 | bytes 5510144 | tf_op jit(solution)/shard_map/dot_general | solution.py:80
  6.5 4.4 %collective-permute-start = (bf16[15,1024]{1,0:T(8,128)(2,1)S(1)}, bf16[15,1024]{1,0:T(8,128)(2,1)S(1)}, u32[]{:S(2)}, u32[]{:S(2)}) collective-permute-start(bf16[15,1024]{1,0:T(8,128)(2,1)S(1)} %get-tuple-element.19), channel_id=1, source_target_pairs={{0,8},{8,16},{16,24},{24,32},{32,40},{40,48},{48,56},{1,9},{9,17},... | collective-permute-start | bytes 92168 | tf_op jit(solution)/shard_map/ppermute | solution.py:16
  12.7 3.0 %collective-permute-done.1 = bf16[15,1024]{1,0:T(8,128)(2,1)S(1)} collective-permute-done((bf16[15,1024]{1,0:T(8,128)(2,1)S(1)}, bf16[15,1024]{1,0:T(8,128)(2,1)S(1)}, u32[]{:S(2)}, u32[]{:S(2)}) %collective-permute-start.1) | collective-permute-done | bytes 30752 | tf_op jit(solution)/shard_map/ppermute | solution.py:17
  15.7 5.0 %fusion.103 = (f32[128]{0:T(128)S(1)}, f32[128,1024]{1,0:T(8,128)S(1)}) fusion(bf16[1024,1024]{1,0:T(8,128)(2,1)} %param.22, bf16[128,1024]{1,0:T(8,128)(2,1)S(1)} %fusion.44, bf16[15,1024]{1,0:T(8,128)(2,1)S(1)} %collective-permute-done.1, bf16[15,1024]{1,0:T(8,128)(2,1)S(1)} %collective-permute-done, f32[1024]{0:T(1024)S(1)} %copy-done.14, ...), kind=kOutput, calls=%fused_computation.191 | convolution fusion | flops 293601152 | bytes 3342848 | tf_op jit(solution)/shard_map/dot_general | solution.py:92
  23.5 2.9 %fusion.99 = (bf16[64,3,1024]{2,1,0:T(4,128)(2,1)S(1)}, bf16[64,3,1024]{2,1,0:T(4,128)(2,1)}) fusion(bf16[64,6,1024]{2,1,0:T(8,128)(2,1)} %reshape.73), kind=kLoop, calls=%fused_computation.187 | loop fusion | bytes 1572864 | tf_op jit(solution)/shard_map/slice | solution.py:126
  26.4 30.8 %all_to_all.20 = bf16[64,3,1024]{2,1,0:T(4,128)(2,1)} all-to-all(bf16[64,3,1024]{2,1,0:T(4,128)(2,1)S(1)} %get-tuple-element.17), channel_id=1, replica_groups=mesh['dp'=4,'seq'=8,'expert'=8] {'seq','expert'}, dimensions={0} | all-to-all | bytes 786432 | tf_op jit(solution)/shard_map/all_to_all | solution.py:125
  57.2 5.7 %all-to-all-start.2 = ((bf16[64,3,1024]{2,1,0:T(4,128)(2,1)}), bf16[64,3,1024]{2,1,0:T(4,128)(2,1)S(1)}, u32[]{:S(2)}, u32[]{:S(2)}) async-start(bf16[64,3,1024]{2,1,0:T(4,128)(2,1)} %get-tuple-element.18), calls=%async_computation.2 | async-start | bytes 1048576 | tf_op jit(solution)/shard_map/all_to_all | solution.py:125
  67.7 12.9 %all-to-all-done.2 = bf16[64,3,1024]{2,1,0:T(4,128)(2,1)S(1)} async-done(((bf16[64,3,1024]{2,1,0:T(4,128)(2,1)}), bf16[64,3,1024]{2,1,0:T(4,128)(2,1)S(1)}, u32[]{:S(2)}, u32[]{:S(2)}) %all-to-all-start.2) | async-done | bytes 393248 | tf_op jit(solution)/shard_map/all_to_all | solution.py:125
  86.9 2.7 %collective-permute-start.5 = (bf16[96,1024]{1,0:T(8,128)(2,1)S(1)}, bf16[96,1024]{1,0:T(8,128)(2,1)S(1)}, u32[]{:S(2)}, u32[]{:S(2)}) collective-permute-start(bf16[96,1024]{1,0:T(8,128)(2,1)S(1)} %slice.434), channel_id=1, source_target_pairs={{0,192},{64,0},{128,64},{192,128},{1,193},{65,1},{129,65},{193,129... | collective-permute-start | bytes 589832 | tf_op jit(solution)/shard_map/ppermute | solution.py:30
  89.6 3.0 %collective-permute-done.10 = bf16[192,1024]{1,0:T(8,128)(2,1)S(1)} collective-permute-done((bf16[192,1024]{1,0:T(8,128)(2,1)S(1)}, bf16[192,1024]{1,0:T(8,128)(2,1)S(1)}, u32[]{:S(2)}, u32[]{:S(2)}) %collective-permute-start.10) | collective-permute-done | bytes 393248 | tf_op jit(solution)/shard_map/ppermute | solution.py:27
  93.0 2.7 %collective-permute-start.13 = (bf16[96,1024]{1,0:T(8,128)(2,1)S(1)}, bf16[96,1024]{1,0:T(8,128)(2,1)S(1)}, u32[]{:S(2)}, u32[]{:S(2)}) collective-permute-start(bf16[96,1024]{1,0:T(8,128)(2,1)S(1)} %slice.442), channel_id=1, source_target_pairs={{0,192},{64,0},{128,64},{192,128},{1,193},{65,1},{129,65},{193,129... | collective-permute-start | bytes 589832 | tf_op jit(solution)/shard_map/ppermute | solution.py:30
  100.1 3.5 %fusion.6 = f32[768,1024]{1,0:T(8,128)} fusion(bf16[768,1024]{1,0:T(8,128)(2,1)S(1)} %constant_dynamic-update-slice_fusion, bf16[1,1024,1024]{2,1,0:T(8,128)(2,1)S(1)} %copy-done.13), kind=kOutput, calls=%fused_computation.8 | convolution fusion | flops 1610612736 | bytes 6815744 | tf_op jit(solution)/shard_map/dot_general | solution.py:132
  103.6 8.9 %fusion.104 = (bf16[768,1024]{1,0:T(8,128)(2,1)}, f32[768,1024]{1,0:T(8,128)}) fusion(bf16[1,1024,1024]{2,1,0:T(8,128)(2,1)S(1)} %copy-done, f32[768,1024]{1,0:T(8,128)} %fusion.6, bf16[768,1024]{1,0:T(8,128)(2,1)} %copy-done.8, bf16[1,1024,1024]{2,1,0:T(8,128)(2,1)} %param.25), kind=kOutput, calls=%fused_computation.192 | convolution fusion | flops 3226730496 | bytes 13631488 | tf_op jit(solution)/shard_map/dot_general | solution.py:134
  113.7 2.7 %collective-permute-start.8 = (bf16[96,1024]{1,0:T(8,128)(2,1)S(1)}, bf16[96,1024]{1,0:T(8,128)(2,1)S(1)}, u32[]{:S(2)}, u32[]{:S(2)}) collective-permute-start(bf16[96,1024]{1,0:T(8,128)(2,1)S(1)} %get-tuple-element.14), channel_id=1, source_target_pairs={{0,192},{64,0},{128,64},{192,128},{1,193},{65,1},{129,65},{193,129... | collective-permute-start | bytes 589832 | tf_op jit(solution)/shard_map/ppermute | solution.py:43
  117.8 5.7 %fusion.4 = f32[768,1024]{1,0:T(8,128)} fusion(bf16[768,1024]{1,0:T(8,128)(2,1)} %constant_dynamic-update-slice_fusion.5, bf16[1,1024,1024]{2,1,0:T(8,128)(2,1)} %param.26), kind=kOutput, calls=%fused_computation.6 | convolution fusion | flops 1610612736 | bytes 6815744 | tf_op jit(solution)/shard_map/dot_general | solution.py:132
  124.4 2.7 %collective-permute-start.9 = (bf16[192,1024]{1,0:T(8,128)(2,1)S(1)}, bf16[192,1024]{1,0:T(8,128)(2,1)}, u32[]{:S(2)}, u32[]{:S(2)}) collective-permute-start(bf16[192,1024]{1,0:T(8,128)(2,1)S(1)} %get-tuple-element.10), channel_id=1, source_target_pairs={{0,192},{64,0},{128,64},{192,128},{1,193},{65,1},{129,65},{193,129... | collective-permute-start | bytes 1179656 | tf_op jit(solution)/shard_map/ppermute | solution.py:47
  127.1 8.9 %fusion.107 = (bf16[768,1024]{1,0:T(8,128)(2,1)}, f32[768,1024]{1,0:T(8,128)}) fusion(bf16[1,1024,1024]{2,1,0:T(8,128)(2,1)S(1)} %copy-done, f32[768,1024]{1,0:T(8,128)} %fusion.4, bf16[768,1024]{1,0:T(8,128)(2,1)} %constant_dynamic-update-slice_fusion.5, bf16[1,1024,1024]{2,1,0:T(8,128)(2,1)} %param.25), kind=kOutput, calls=%fused_computation.193 | convolution fusion | flops 3226730496 | bytes 13631488 | tf_op jit(solution)/shard_map/dot_general | solution.py:134
  137.8 2.7 %collective-permute-start.16 = (bf16[96,1024]{1,0:T(8,128)(2,1)}, bf16[96,1024]{1,0:T(8,128)(2,1)}, u32[]{:S(2)}, u32[]{:S(2)}) collective-permute-start(bf16[96,1024]{1,0:T(8,128)(2,1)} %get-tuple-element.16), channel_id=1, source_target_pairs={{0,192},{64,0},{128,64},{192,128},{1,193},{65,1},{129,65},{193,129... | collective-permute-start | bytes 589832 | tf_op jit(solution)/shard_map/ppermute | solution.py:43
  142.9 9.5 %all-to-all-start.1 = ((bf16[64,3,1024]{2,1,0:T(4,128)(2,1)}), bf16[64,3,1024]{2,1,0:T(4,128)(2,1)S(1)}, u32[]{:S(2)}, u32[]{:S(2)}) async-start(bf16[64,3,1024]{2,1,0:T(4,128)(2,1)} %reshape.75), calls=%async_computation.1 | async-start | bytes 1048576 | tf_op jit(solution)/shard_map/all_to_all | solution.py:140
  154.2 2.7 %collective-permute-start.17 = (bf16[192,1024]{1,0:T(8,128)(2,1)S(1)}, bf16[192,1024]{1,0:T(8,128)(2,1)S(1)}, u32[]{:S(2)}, u32[]{:S(2)}) collective-permute-start(bf16[192,1024]{1,0:T(8,128)(2,1)S(1)} %get-tuple-element.12), channel_id=1, source_target_pairs={{0,192},{64,0},{128,64},{192,128},{1,193},{65,1},{129,65},{193,129... | collective-permute-start | bytes 1179656 | tf_op jit(solution)/shard_map/ppermute | solution.py:47
  156.8 8.8 %collective-permute-done.15 = bf16[192,1024]{1,0:T(8,128)(2,1)S(1)} collective-permute-done((bf16[192,1024]{1,0:T(8,128)(2,1)S(1)}, bf16[192,1024]{1,0:T(8,128)(2,1)S(1)}, u32[]{:S(2)}, u32[]{:S(2)}) %collective-permute-start.15) | collective-permute-done | bytes 393248 | tf_op jit(solution)/shard_map/ppermute | solution.py:46
  170.1 11.0 %all-to-all-start.3 = ((bf16[64,3,1024]{2,1,0:T(4,128)(2,1)}), bf16[64,3,1024]{2,1,0:T(4,128)(2,1)}, u32[]{:S(2)}, u32[]{:S(2)}) async-start(bf16[64,3,1024]{2,1,0:T(4,128)(2,1)} %reshape.77), calls=%async_computation.3 | async-start | bytes 1048576 | tf_op jit(solution)/shard_map/all_to_all | solution.py:140
  181.4 17.3 %all-to-all-done.3 = bf16[64,3,1024]{2,1,0:T(4,128)(2,1)} async-done(((bf16[64,3,1024]{2,1,0:T(4,128)(2,1)}), bf16[64,3,1024]{2,1,0:T(4,128)(2,1)}, u32[]{:S(2)}, u32[]{:S(2)}) %all-to-all-start.3) | async-done | bytes 393248 | tf_op jit(solution)/shard_map/all_to_all | solution.py:140
  198.7 2.5 %pad_maximum_fusion = bf16[64,6,1024]{2,1,0:T(8,128)(2,1)} fusion(bf16[64,3,1024]{2,1,0:T(4,128)(2,1)} %all-to-all-done.3, bf16[64,3,1024]{2,1,0:T(4,128)(2,1)S(1)} %all-to-all-done.1), kind=kLoop, calls=%fused_computation.51 | loop fusion | flops 1572864 | bytes 1572864 | tf_op jit(solution)/shard_map/concatenate | solution.py:142
  (110 shorter events, 39.8 us)
Async XLA Ops:
  0.0 103.6 %copy-start = (bf16[1,1024,1024]{2,1,0:T(8,128)(2,1)S(1)}, bf16[1,1024,1024]{2,1,0:T(8,128)(2,1)}, u32[]{:S(2)}) copy-start(bf16[1,1024,1024]{2,1,0:T(8,128)(2,1)} %param.27) | copy-start | bytes 6291460
  6.5 6.2 %collective-permute-start = (bf16[15,1024]{1,0:T(8,128)(2,1)S(1)}, bf16[15,1024]{1,0:T(8,128)(2,1)S(1)}, u32[]{:S(2)}, u32[]{:S(2)}) collective-permute-start(bf16[15,1024]{1,0:T(8,128)(2,1)S(1)} %get-tuple-element.19), channel_id=1, source_target_pairs={{0,8},{8,16},{16,24},{24,32},{32,40},{40,48},{48,56},{1,9},{9,17},... | collective-permute-start | bytes 92168 | tf_op jit(solution)/shard_map/ppermute | solution.py:16
  10.8 4.8 %collective-permute-start.1 = (bf16[15,1024]{1,0:T(8,128)(2,1)S(1)}, bf16[15,1024]{1,0:T(8,128)(2,1)S(1)}, u32[]{:S(2)}, u32[]{:S(2)}) collective-permute-start(bf16[15,1024]{1,0:T(8,128)(2,1)S(1)} %get-tuple-element.20), channel_id=1, source_target_pairs={{8,0},{16,8},{24,16},{32,24},{40,32},{48,40},{56,48},{9,1},{17,9},... | collective-permute-start | bytes 92168 | tf_op jit(solution)/shard_map/ppermute | solution.py:17
  57.2 23.4 %all-to-all-start.2 = ((bf16[64,3,1024]{2,1,0:T(4,128)(2,1)}), bf16[64,3,1024]{2,1,0:T(4,128)(2,1)S(1)}, u32[]{:S(2)}, u32[]{:S(2)}) async-start(bf16[64,3,1024]{2,1,0:T(4,128)(2,1)} %get-tuple-element.18), calls=%async_computation.2 | async-start | bytes 1048576 | tf_op jit(solution)/shard_map/all_to_all | solution.py:125
  64.9 20.0 %collective-permute-start.2 = (bf16[192,1024]{1,0:T(8,128)(2,1)}, bf16[192,1024]{1,0:T(8,128)(2,1)}, u32[]{:S(2)}, u32[]{:S(2)}) collective-permute-start(bf16[192,1024]{1,0:T(8,128)(2,1)} %reshape.74), channel_id=1, source_target_pairs={{0,64},{64,128},{128,192},{192,0},{1,65},{65,129},{129,193},{193,1... | collective-permute-start | bytes 1179656 | tf_op jit(solution)/shard_map/ppermute | solution.py:27
  66.2 19.7 %collective-permute-start.3 = (bf16[192,1024]{1,0:T(8,128)(2,1)}, bf16[192,1024]{1,0:T(8,128)(2,1)}, u32[]{:S(2)}, u32[]{:S(2)}) collective-permute-start(bf16[192,1024]{1,0:T(8,128)(2,1)} %reshape.74), channel_id=1, source_target_pairs={{0,192},{64,0},{128,64},{192,128},{1,193},{65,1},{129,65},{193,129... | collective-permute-start | bytes 1179656 | tf_op jit(solution)/shard_map/ppermute | solution.py:28
  80.9 11.7 %collective-permute-start.10 = (bf16[192,1024]{1,0:T(8,128)(2,1)S(1)}, bf16[192,1024]{1,0:T(8,128)(2,1)S(1)}, u32[]{:S(2)}, u32[]{:S(2)}) collective-permute-start(bf16[192,1024]{1,0:T(8,128)(2,1)S(1)} %reshape.76), channel_id=1, source_target_pairs={{0,64},{64,128},{128,192},{192,0},{1,65},{65,129},{129,193},{193,1... | collective-permute-start | bytes 1179656 | tf_op jit(solution)/shard_map/ppermute | solution.py:27
  82.3 10.6 %collective-permute-start.11 = (bf16[192,1024]{1,0:T(8,128)(2,1)S(1)}, bf16[192,1024]{1,0:T(8,128)(2,1)S(1)}, u32[]{:S(2)}, u32[]{:S(2)}) collective-permute-start(bf16[192,1024]{1,0:T(8,128)(2,1)S(1)} %reshape.76), channel_id=1, source_target_pairs={{0,192},{64,0},{128,64},{192,128},{1,193},{65,1},{129,65},{193,129... | collective-permute-start | bytes 1179656 | tf_op jit(solution)/shard_map/ppermute | solution.py:28
  85.8 12.0 %collective-permute-start.4 = (bf16[96,1024]{1,0:T(8,128)(2,1)S(1)}, bf16[96,1024]{1,0:T(8,128)(2,1)S(1)}, u32[]{:S(2)}, u32[]{:S(2)}) collective-permute-start(bf16[96,1024]{1,0:T(8,128)(2,1)S(1)} %slice.433), channel_id=1, source_target_pairs={{0,64},{64,128},{128,192},{192,0},{1,65},{65,129},{129,193},{193,1... | collective-permute-start | bytes 589832 | tf_op jit(solution)/shard_map/ppermute | solution.py:30
  86.9 11.0 %collective-permute-start.5 = (bf16[96,1024]{1,0:T(8,128)(2,1)S(1)}, bf16[96,1024]{1,0:T(8,128)(2,1)S(1)}, u32[]{:S(2)}, u32[]{:S(2)}) collective-permute-start(bf16[96,1024]{1,0:T(8,128)(2,1)S(1)} %slice.434), channel_id=1, source_target_pairs={{0,192},{64,0},{128,64},{192,128},{1,193},{65,1},{129,65},{193,129... | collective-permute-start | bytes 589832 | tf_op jit(solution)/shard_map/ppermute | solution.py:30
  92.6 23.7 %collective-permute-start.12 = (bf16[96,1024]{1,0:T(8,128)(2,1)S(1)}, bf16[96,1024]{1,0:T(8,128)(2,1)S(1)}, u32[]{:S(2)}, u32[]{:S(2)}) collective-permute-start(bf16[96,1024]{1,0:T(8,128)(2,1)S(1)} %slice.441), channel_id=1, source_target_pairs={{0,64},{64,128},{128,192},{192,0},{1,65},{65,129},{129,193},{193,1... | collective-permute-start | bytes 589832 | tf_op jit(solution)/shard_map/ppermute | solution.py:30
  93.0 24.1 %collective-permute-start.13 = (bf16[96,1024]{1,0:T(8,128)(2,1)S(1)}, bf16[96,1024]{1,0:T(8,128)(2,1)S(1)}, u32[]{:S(2)}, u32[]{:S(2)}) collective-permute-start(bf16[96,1024]{1,0:T(8,128)(2,1)S(1)} %slice.442), channel_id=1, source_target_pairs={{0,192},{64,0},{128,64},{192,128},{1,193},{65,1},{129,65},{193,129... | collective-permute-start | bytes 589832 | tf_op jit(solution)/shard_map/ppermute | solution.py:30
  113.6 9.9 %collective-permute-start.6 = (bf16[96,1024]{1,0:T(8,128)(2,1)S(1)}, bf16[96,1024]{1,0:T(8,128)(2,1)S(1)}, u32[]{:S(2)}, u32[]{:S(2)}) collective-permute-start(bf16[96,1024]{1,0:T(8,128)(2,1)S(1)} %get-tuple-element.13), channel_id=1, source_target_pairs={{0,64},{64,128},{128,192},{192,0},{1,65},{65,129},{129,193},{193,1... | collective-permute-start | bytes 589832 | tf_op jit(solution)/shard_map/ppermute | solution.py:42
  113.7 9.8 %collective-permute-start.8 = (bf16[96,1024]{1,0:T(8,128)(2,1)S(1)}, bf16[96,1024]{1,0:T(8,128)(2,1)S(1)}, u32[]{:S(2)}, u32[]{:S(2)}) collective-permute-start(bf16[96,1024]{1,0:T(8,128)(2,1)S(1)} %get-tuple-element.14), channel_id=1, source_target_pairs={{0,192},{64,0},{128,64},{192,128},{1,193},{65,1},{129,65},{193,129... | collective-permute-start | bytes 589832 | tf_op jit(solution)/shard_map/ppermute | solution.py:43
  124.4 16.0 %collective-permute-start.7 = (bf16[192,1024]{1,0:T(8,128)(2,1)}, bf16[192,1024]{1,0:T(8,128)(2,1)S(1)}, u32[]{:S(2)}, u32[]{:S(2)}) collective-permute-start(bf16[192,1024]{1,0:T(8,128)(2,1)} %get-tuple-element.9), channel_id=1, source_target_pairs={{0,64},{64,128},{128,192},{192,0},{1,65},{65,129},{129,193},{193,1... | collective-permute-start | bytes 1179656 | tf_op jit(solution)/shard_map/ppermute | solution.py:46
  124.4 16.0 %collective-permute-start.9 = (bf16[192,1024]{1,0:T(8,128)(2,1)S(1)}, bf16[192,1024]{1,0:T(8,128)(2,1)}, u32[]{:S(2)}, u32[]{:S(2)}) collective-permute-start(bf16[192,1024]{1,0:T(8,128)(2,1)S(1)} %get-tuple-element.10), channel_id=1, source_target_pairs={{0,192},{64,0},{128,64},{192,128},{1,193},{65,1},{129,65},{193,129... | collective-permute-start | bytes 1179656 | tf_op jit(solution)/shard_map/ppermute | solution.py:47
  137.8 14.6 %collective-permute-start.14 = (bf16[96,1024]{1,0:T(8,128)(2,1)}, bf16[96,1024]{1,0:T(8,128)(2,1)}, u32[]{:S(2)}, u32[]{:S(2)}) collective-permute-start(bf16[96,1024]{1,0:T(8,128)(2,1)} %get-tuple-element.15), channel_id=1, source_target_pairs={{0,64},{64,128},{128,192},{192,0},{1,65},{65,129},{129,193},{193,1... | collective-permute-start | bytes 589832 | tf_op jit(solution)/shard_map/ppermute | solution.py:42
  137.8 14.6 %collective-permute-start.16 = (bf16[96,1024]{1,0:T(8,128)(2,1)}, bf16[96,1024]{1,0:T(8,128)(2,1)}, u32[]{:S(2)}, u32[]{:S(2)}) collective-permute-start(bf16[96,1024]{1,0:T(8,128)(2,1)} %get-tuple-element.16), channel_id=1, source_target_pairs={{0,192},{64,0},{128,64},{192,128},{1,193},{65,1},{129,65},{193,129... | collective-permute-start | bytes 589832 | tf_op jit(solution)/shard_map/ppermute | solution.py:43
  142.9 27.2 %all-to-all-start.1 = ((bf16[64,3,1024]{2,1,0:T(4,128)(2,1)}), bf16[64,3,1024]{2,1,0:T(4,128)(2,1)S(1)}, u32[]{:S(2)}, u32[]{:S(2)}) async-start(bf16[64,3,1024]{2,1,0:T(4,128)(2,1)} %reshape.75), calls=%async_computation.1 | async-start | bytes 1048576 | tf_op jit(solution)/shard_map/all_to_all | solution.py:140
  154.0 27.1 %copy-start.2 = (bf16[128,1024]{1,0:T(8,128)(2,1)S(1)}, bf16[128,1024]{1,0:T(8,128)(2,1)}, u32[]{:S(2)}) copy-start(bf16[128,1024]{1,0:T(8,128)(2,1)} %copy-done.1) | copy-start | bytes 786436
  154.0 27.1 %copy-start.5 = (bf16[1024,64]{0,1:T(8,128)(2,1)S(1)}, bf16[1024,64]{0,1:T(8,128)(2,1)}, u32[]{:S(2)}) copy-start(bf16[1024,64]{0,1:T(8,128)(2,1)} %param.24) | copy-start | bytes 393220
  154.1 11.5 %collective-permute-start.15 = (bf16[192,1024]{1,0:T(8,128)(2,1)S(1)}, bf16[192,1024]{1,0:T(8,128)(2,1)S(1)}, u32[]{:S(2)}, u32[]{:S(2)}) collective-permute-start(bf16[192,1024]{1,0:T(8,128)(2,1)S(1)} %get-tuple-element.11), channel_id=1, source_target_pairs={{0,64},{64,128},{128,192},{192,0},{1,65},{65,129},{129,193},{193,1... | collective-permute-start | bytes 1179656 | tf_op jit(solution)/shard_map/ppermute | solution.py:46
  154.2 11.4 %collective-permute-start.17 = (bf16[192,1024]{1,0:T(8,128)(2,1)S(1)}, bf16[192,1024]{1,0:T(8,128)(2,1)S(1)}, u32[]{:S(2)}, u32[]{:S(2)}) collective-permute-start(bf16[192,1024]{1,0:T(8,128)(2,1)S(1)} %get-tuple-element.12), channel_id=1, source_target_pairs={{0,192},{64,0},{128,64},{192,128},{1,193},{65,1},{129,65},{193,129... | collective-permute-start | bytes 1179656 | tf_op jit(solution)/shard_map/ppermute | solution.py:47
  170.1 28.6 %all-to-all-start.3 = ((bf16[64,3,1024]{2,1,0:T(4,128)(2,1)}), bf16[64,3,1024]{2,1,0:T(4,128)(2,1)}, u32[]{:S(2)}, u32[]{:S(2)}) async-start(bf16[64,3,1024]{2,1,0:T(4,128)(2,1)} %reshape.77), calls=%async_computation.3 | async-start | bytes 1048576 | tf_op jit(solution)/shard_map/all_to_all | solution.py:140
  (13 other events, 72.8 us)

commit v3 on v0

--- a/solution.py
+++ b/solution.py
@@ -90,19 +90,39 @@
     down_local = down_weight[0]
     arrived = lax.all_to_all(outgoing, ("seq", "expert"), split_axis=0, concat_axis=0, tiled=True)
     arrived_shape = arrived.shape
-    shard_rows = lax.all_gather(arrived.reshape(-1, arrived_shape[2]), "dp", axis=0, tiled=True)
-    gate_part = jnp.dot(shard_rows, gate_local, preferred_element_type=jnp.float32)
-    up_part = jnp.dot(shard_rows, up_local, preferred_element_type=jnp.float32)
-    hidden = (jax.nn.silu(gate_part) * up_part).astype(jnp.bfloat16)
-    summed = lax.psum_scatter(
-        lax.dot_general(
+    own_rows = arrived.reshape(-1, arrived_shape[2])
+
+    def serve(rows):
+        gate_part = jnp.dot(rows, gate_local, preferred_element_type=jnp.float32)
+        up_part = jnp.dot(rows, up_local, preferred_element_type=jnp.float32)
+        hidden = (jax.nn.silu(gate_part) * up_part).astype(jnp.bfloat16)
+        return lax.dot_general(
             hidden, down_local, (((1,), (1,)), ((), ())), preferred_element_type=jnp.float32
-        ).astype(jnp.bfloat16),
-        "dp",
-        scatter_dimension=0,
-        tiled=True,
+        )
+
+    size = lax.axis_size("dp")
+    up = [(i, (i + 1) % size) for i in range(size)]
+    down = [(i, (i - 1) % size) for i in range(size)]
+    half = own_rows.shape[0] // 2
+    from_below = lax.ppermute(own_rows, "dp", up)
+    from_above = lax.ppermute(own_rows, "dp", down)
+    for_own = serve(own_rows)
+    for_own, from_below, from_above = lax.optimization_barrier((for_own, from_below, from_above))
+    far_rows = jnp.concatenate(
+        [lax.ppermute(from_below[:half], "dp", up), lax.ppermute(from_above[half:], "dp", down)], axis=0
     )
-    served = summed.reshape(arrived_shape)
+    for_below = serve(from_below)
+    for_above = serve(from_above)
+    far_rows, for_below, for_above = lax.optimization_barrier((far_rows, for_below, for_above))
+    for_far = serve(far_rows).astype(jnp.bfloat16)
+    far_up = lax.ppermute(for_far[:half], "dp", up).astype(jnp.float32)
+    far_down = lax.ppermute(for_far[half:], "dp", down).astype(jnp.float32)
+    send_up = for_above + jnp.concatenate([far_up, jnp.zeros_like(far_down)], axis=0)
+    send_down = for_below + jnp.concatenate([jnp.zeros_like(far_up), far_down], axis=0)
+    got_below = lax.ppermute(send_up.astype(jnp.bfloat16), "dp", up).astype(jnp.float32)
+    got_above = lax.ppermute(send_down.astype(jnp.bfloat16), "dp", down).astype(jnp.float32)
+    summed = for_own + got_below + got_above
+    served = summed.astype(jnp.bfloat16).reshape(arrived_shape)
     returned_rows = lax.all_to_all(
         served, ("seq", "expert"), split_axis=0, concat_axis=0, tiled=True
     )

time: 225 us -> 192 us (0.85)
  waiting for transfers between devices: 111 us -> 64.8 us
  matrix products: 29.1 us -> 43.1 us
  between operations: 14.5 us -> 1.23 us
  starting transfers between devices: 16.6 us -> 26.9 us
    reduce_scatter x1 -> x0, waiting for transfers between devices: 41.3 us -> none  [local(): lax.psum_scatter(lax.dot_general(hidden, down_local, (((1,), (1,)), ((),...]
    all_gather x1 -> x0, waiting for transfers between devices: 39.1 us -> none  [local(): lax.all_gather(arrived.reshape(-1, arrived_shape[2]), 'dp', axis=0, tiled...]
    ppermute x0 -> x8, waiting for transfers between devices: none -> 34 us  [the longest x1 13.2 us: local(): lax.ppermute(send_down.astype(jnp.bfloat16), 'dp', down).astype(jnp.float32)]
    dot_general x2 -> x8, matrix products: 18.9 us -> 32.9 us  [the longest x4 21.3 us: serve(): lax.dot_general(hidden, down_local, (((1,), (1,)), ((), ())), preferred_e...]
    ppermute x0 -> x8, starting transfers between devices: none -> 8.98 us  [the longest x1 3.06 us: local(): lax.ppermute(send_down.astype(jnp.bfloat16), 'dp', down).astype(jnp.float32)]
  transfers between devices with their start and end apart: 5 -> 11, of which waited for: 4 -> 7; matrix products, arithmetic and copies ran while one was open for 0% -> 10% of each run, Pallas kernels for 0% -> 0%
where the time goes in v3:
time: 192 us
  waiting for transfers between devices  64.8 us (34%)
  matrix products  43.1 us (22%)
  blocking collectives  41.5 us (22%)
  starting transfers between devices  26.9 us (14%)
  local copies, waits for them, and re-layouts  9.32 us (5%)
  other arithmetic  4.91 us (3%)
    all_to_all x1, blocking collectives, local(): lax.all_to_all(outgoing, ('seq', 'expert'), split_axis=0, concat_axis=0,...  41.5 us
    all_to_all x1, waiting for transfers between devices, local(): lax.all_to_all(served, ('seq', 'expert'), split_axis=0, concat_axis=0, ti...  27.8 us
    dot_general x4, matrix products, serve(): lax.dot_general(hidden, down_local, (((1,), (1,)), ((), ())), preferred_e...  21.3 us
    ppermute x1, waiting for transfers between devices, local(): lax.ppermute(send_down.astype(jnp.bfloat16), 'dp', down).astype(jnp.float32)  13.2 us
    all_to_all x1, starting transfers between devices, local(): lax.all_to_all(served, ('seq', 'expert'), split_axis=0, concat_axis=0, ti...  12.2 us
    ppermute x1, waiting for transfers between devices, local(): from_above = lax.ppermute(own_rows, 'dp', down)  7.86 us
    dot_general x2, matrix products, serve(): up_part = jnp.dot(rows, up_local, preferred_element_type=jnp.float32)  7.38 us
    ppermute x1, waiting for transfers between devices, local(): far_down = lax.ppermute(for_far[half:], 'dp', down).astype(jnp.float32)  6.33 us
  transfers between devices with their start and end apart: 11, of which 7 were waited for; matrix products, arithmetic and copies ran while one was open for 10% of the time, Pallas kernels for 0%

profile of v3, /device:TPU:1, one launch (start us, length us, event | category | flops | bytes accessed | tf_op | source)
XLA Modules:
  0.0 191.8 jit_solution(6505725959797157721)
XLA Ops:
  3.1 3.1 %fusion.64 = f32[128,2048]{1,0:T(8,128)S(1)} fusion(bf16[1024,2048]{1,0:T(8,128)(2,1)} %param.18, bf16[1,128,1024]{2,1,0:T(8,128)(2,1)} %param.14, f32[1024]{0:T(1024)} %param.17, f32[128]{0:T(128)S(1)} %add_rsqrt_fusion.1, f32[128]{0:T(128)S(1)} %broadcast_multiply_fusion.1), kind=kOutput, calls=%fused_computation.92 | convolution fusion | flops 537526272 | bytes 5510144 | tf_op jit(solution)/shard_map/dot_general | solution.py:49
  6.5 4.4 %collective-permute-start = (bf16[15,1024]{1,0:T(8,128)(2,1)S(1)}, bf16[15,1024]{1,0:T(8,128)(2,1)S(1)}, u32[]{:S(2)}, u32[]{:S(2)}) collective-permute-start(bf16[15,1024]{1,0:T(8,128)(2,1)S(1)} %get-tuple-element.23), channel_id=1, source_target_pairs={{0,8},{8,16},{16,24},{24,32},{32,40},{40,48},{48,56},{1,9},{9,17},... | collective-permute-start | bytes 92168 | tf_op jit(solution)/shard_map/ppermute | solution.py:14
  12.7 3.0 %collective-permute-done.1 = bf16[15,1024]{1,0:T(8,128)(2,1)S(1)} collective-permute-done((bf16[15,1024]{1,0:T(8,128)(2,1)S(1)}, bf16[15,1024]{1,0:T(8,128)(2,1)S(1)}, u32[]{:S(2)}, u32[]{:S(2)}) %collective-permute-start.1) | collective-permute-done | bytes 30752 | tf_op jit(solution)/shard_map/ppermute | solution.py:15
  15.7 5.0 %fusion.122 = (f32[128]{0:T(128)S(1)}, f32[128,1024]{1,0:T(8,128)S(1)}) fusion(bf16[1024,1024]{1,0:T(8,128)(2,1)} %param.22, bf16[128,1024]{1,0:T(8,128)(2,1)S(1)} %fusion.63, bf16[15,1024]{1,0:T(8,128)(2,1)S(1)} %collective-permute-done.1, bf16[15,1024]{1,0:T(8,128)(2,1)S(1)} %collective-permute-done, f32[1024]{0:T(1024)S(1)} %copy-done.15, ...), kind=kOutput, calls=%fused_computation.189 | convolution fusion | flops 293601152 | bytes 3342848 | tf_op jit(solution)/shard_map/dot_general | solution.py:61
  23.5 41.5 %all_to_all.10 = bf16[64,6,1024]{2,1,0:T(8,128)(2,1)} all-to-all(bf16[64,6,1024]{2,1,0:T(8,128)(2,1)} %reshape.67), channel_id=1, replica_groups=mesh['dp'=4,'seq'=8,'expert'=8] {'seq','expert'}, dimensions={0} | all-to-all | bytes 1572864 | tf_op jit(solution)/shard_map/all_to_all | solution.py:91
  65.0 1.4 reshape.68
  66.4 2.8 %collective-permute-start.3 = (bf16[384,1024]{1,0:T(8,128)(2,1)S(1)}, bf16[384,1024]{1,0:T(8,128)(2,1)}, u32[]{:S(2)}, u32[]{:S(2)}) collective-permute-start(bf16[384,1024]{1,0:T(8,128)(2,1)S(1)} %reshape.68), channel_id=1, source_target_pairs={{0,192},{64,0},{128,64},{192,128},{1,193},{65,1},{129,65},{193,129... | collective-permute-start | bytes 2359304 | tf_op jit(solution)/shard_map/ppermute | solution.py:108
  69.2 2.1 %fusion.22 = f32[384,1024]{1,0:T(8,128)} fusion(bf16[384,1024]{1,0:T(8,128)(2,1)S(1)} %reshape.68, bf16[1,1024,1024]{2,1,0:T(8,128)(2,1)S(1)} %copy-done), kind=kOutput, calls=%fused_computation.22 | convolution fusion | flops 805306368 | bytes 4456448 | tf_op jit(solution)/shard_map/dot_general | solution.py:96
  71.3 5.8 %fusion.6 = f32[384,1024]{1,0:T(8,128)} fusion(bf16[1,1024,1024]{2,1,0:T(8,128)(2,1)} %param.27, f32[384,1024]{1,0:T(8,128)} %fusion.22, bf16[384,1024]{1,0:T(8,128)(2,1)S(1)} %reshape.68, bf16[1,1024,1024]{2,1,0:T(8,128)(2,1)} %param.26), kind=kOutput, calls=%fused_computation.6 | convolution fusion | flops 1612972032 | bytes 8126464 | tf_op jit(solution)/shard_map/dot_general | solution.py:99
  77.1 7.9 %collective-permute-done.3 = bf16[384,1024]{1,0:T(8,128)(2,1)} collective-permute-done((bf16[384,1024]{1,0:T(8,128)(2,1)S(1)}, bf16[384,1024]{1,0:T(8,128)(2,1)}, u32[]{:S(2)}, u32[]{:S(2)}) %collective-permute-start.3) | collective-permute-done | bytes 786464 | tf_op jit(solution)/shard_map/ppermute | solution.py:108
  84.9 3.2 %collective-permute-done.2 = bf16[384,1024]{1,0:T(8,128)(2,1)} collective-permute-done((bf16[384,1024]{1,0:T(8,128)(2,1)S(1)}, bf16[384,1024]{1,0:T(8,128)(2,1)}, u32[]{:S(2)}, u32[]{:S(2)}) %collective-permute-start.2) | collective-permute-done | bytes 786464 | tf_op jit(solution)/shard_map/ppermute | solution.py:107
  89.2 4.1 %fusion.12 = f32[384,1024]{1,0:T(8,128)} fusion(bf16[384,1024]{1,0:T(8,128)(2,1)} %collective-permute-done.2, bf16[1,1024,1024]{2,1,0:T(8,128)(2,1)} %param.26), kind=kOutput, calls=%fused_computation.12 | convolution fusion | flops 805306368 | bytes 4456448 | tf_op jit(solution)/shard_map/dot_general | solution.py:97
  94.3 3.3 %fusion.10 = f32[384,1024]{1,0:T(8,128)} fusion(bf16[384,1024]{1,0:T(8,128)(2,1)} %collective-permute-done.3, bf16[1,1024,1024]{2,1,0:T(8,128)(2,1)S(1)} %copy-done.14), kind=kOutput, calls=%fused_computation.10 | convolution fusion | flops 805306368 | bytes 4456448 | tf_op jit(solution)/shard_map/dot_general | solution.py:97
  99.1 5.4 %fusion.4 = f32[384,1024]{1,0:T(8,128)} fusion(bf16[1,1024,1024]{2,1,0:T(8,128)(2,1)} %param.27, f32[384,1024]{1,0:T(8,128)} %fusion.12, bf16[384,1024]{1,0:T(8,128)(2,1)} %collective-permute-done.2, bf16[1,1024,1024]{2,1,0:T(8,128)(2,1)S(1)} %copy-done), kind=kOutput, calls=%fused_computation.4 | convolution fusion | flops 1612972032 | bytes 8126464 | tf_op jit(solution)/shard_map/dot_general | solution.py:99
  104.5 5.4 %fusion.2 = f32[384,1024]{1,0:T(8,128)} fusion(bf16[1,1024,1024]{2,1,0:T(8,128)(2,1)} %param.27, f32[384,1024]{1,0:T(8,128)} %fusion.10, bf16[384,1024]{1,0:T(8,128)(2,1)} %collective-permute-done.3, bf16[1,1024,1024]{2,1,0:T(8,128)(2,1)S(1)} %copy-done), kind=kOutput, calls=%fused_computation.2 | convolution fusion | flops 1612972032 | bytes 8126464 | tf_op jit(solution)/shard_map/dot_general | solution.py:99
  111.9 2.1 %fusion.16 = f32[384,1024]{1,0:T(8,128)} fusion(bf16[384,1024]{1,0:T(8,128)(2,1)S(1)} %pad_maximum_fusion, bf16[1,1024,1024]{2,1,0:T(8,128)(2,1)S(1)} %copy-done), kind=kOutput, calls=%fused_computation.16 | convolution fusion | flops 805306368 | bytes 4456448 | tf_op jit(solution)/shard_map/dot_general | solution.py:96
  114.0 4.8 %fusion.28 = bf16[384,1024]{1,0:T(8,128)(2,1)S(1)} fusion(bf16[1,1024,1024]{2,1,0:T(8,128)(2,1)} %param.27, f32[384,1024]{1,0:T(8,128)} %fusion.16, bf16[384,1024]{1,0:T(8,128)(2,1)} %copy-done.7, bf16[1,1024,1024]{2,1,0:T(8,128)(2,1)} %param.26), kind=kOutput, calls=%fused_computation.60 | convolution fusion | flops 1613365248 | bytes 7340032 | tf_op jit(solution)/shard_map/dot_general | solution.py:99
  118.9 1.6 collective-permute-start.8
  120.5 6.3 %collective-permute-done.8 = bf16[192,1024]{1,0:T(8,128)(2,1)S(1)} collective-permute-done((bf16[192,1024]{1,0:T(8,128)(2,1)S(1)}, bf16[192,1024]{1,0:T(8,128)(2,1)S(1)}, u32[]{:S(2)}, u32[]{:S(2)}) %collective-permute-start.8) | collective-permute-done | bytes 393248 | tf_op jit(solution)/shard_map/ppermute | solution.py:119
  127.0 3.1 %collective-permute-start.9 = (bf16[384,1024]{1,0:T(8,128)(2,1)S(1)}, bf16[384,1024]{1,0:T(8,128)(2,1)S(1)}, u32[]{:S(2)}, u32[]{:S(2)}) collective-permute-start(bf16[384,1024]{1,0:T(8,128)(2,1)S(1)} %add_convert_fusion.1), channel_id=1, source_target_pairs={{0,192},{64,0},{128,64},{192,128},{1,193},{65,1},{129,65},{193,129... | collective-permute-start | bytes 2359304 | tf_op jit(solution)/shard_map/ppermute | solution.py:123
  130.4 13.2 %collective-permute-done.9 = bf16[384,1024]{1,0:T(8,128)(2,1)S(1)} collective-permute-done((bf16[384,1024]{1,0:T(8,128)(2,1)S(1)}, bf16[384,1024]{1,0:T(8,128)(2,1)S(1)}, u32[]{:S(2)}, u32[]{:S(2)}) %collective-permute-start.9) | collective-permute-done | bytes 786464 | tf_op jit(solution)/shard_map/ppermute | solution.py:123
  143.6 3.4 %collective-permute-done.7 = bf16[384,1024]{1,0:T(8,128)(2,1)S(1)} collective-permute-done((bf16[384,1024]{1,0:T(8,128)(2,1)S(1)}, bf16[384,1024]{1,0:T(8,128)(2,1)S(1)}, u32[]{:S(2)}, u32[]{:S(2)}) %collective-permute-start.7) | collective-permute-done | bytes 786464 | tf_op jit(solution)/shard_map/ppermute | solution.py:122
  148.6 12.2 %all-to-all-start.1 = ((bf16[64,6,1024]{2,1,0:T(8,128)(2,1)}), bf16[64,6,1024]{2,1,0:T(8,128)(2,1)}, u32[]{:S(2)}, u32[]{:S(2)}) async-start(bf16[64,6,1024]{2,1,0:T(8,128)(2,1)} %reshape.69), calls=%async_computation.1 | async-start | bytes 2097152 | tf_op jit(solution)/shard_map/all_to_all | solution.py:126
  161.1 27.8 %all-to-all-done.1 = bf16[64,6,1024]{2,1,0:T(8,128)(2,1)} async-done(((bf16[64,6,1024]{2,1,0:T(8,128)(2,1)}), bf16[64,6,1024]{2,1,0:T(8,128)(2,1)}, u32[]{:S(2)}, u32[]{:S(2)}) %all-to-all-start.1) | async-done | bytes 786464 | tf_op jit(solution)/shard_map/all_to_all | solution.py:126
  (79 shorter events, 17.8 us)
Async XLA Ops:
  0.0 69.2 %copy-start = (bf16[1,1024,1024]{2,1,0:T(8,128)(2,1)S(1)}, bf16[1,1024,1024]{2,1,0:T(8,128)(2,1)}, u32[]{:S(2)}) copy-start(bf16[1,1024,1024]{2,1,0:T(8,128)(2,1)} %param.25) | copy-start | bytes 6291460
  3.1 9.0 %copy-start.9 = (f32[31,1024]{1,0:T(8,128)S(1)}, f32[31,1024]{1,0:T(8,128)}, u32[]{:S(2)}) copy-start(f32[31,1024]{1,0:T(8,128)} %param.19) | copy-start | bytes 380932
  6.2 6.0 %copy-start.11 = (s32[1,128,2]{1,2,0:T(2,128)S(1)}, s32[1,128,2]{1,2,0:T(2,128)}, u32[]{:S(2)}) copy-start(s32[1,128,2]{1,2,0:T(2,128)} %param.16) | copy-start | bytes 3076
  6.2 9.4 %copy-start.3 = (bf16[1,128,1024]{2,1,0:T(8,128)(2,1)S(1)}, bf16[1,128,1024]{2,1,0:T(8,128)(2,1)}, u32[]{:S(2)}) copy-start(bf16[1,128,1024]{2,1,0:T(8,128)(2,1)} %param.14) | copy-start | bytes 786436
  6.2 9.4 %copy-start.15 = (f32[1024]{0:T(1024)S(1)}, f32[1024]{0:T(1024)}, u32[]{:S(2)}) copy-start(f32[1024]{0:T(1024)} %param.21) | copy-start | bytes 12292
  6.3 9.4 %copy-start.16 = (f32[1024]{0:T(1024)S(1)}, f32[1024]{0:T(1024)}, u32[]{:S(2)}) copy-start(f32[1024]{0:T(1024)} %param.20) | copy-start | bytes 12292
  6.5 6.2 %collective-permute-start = (bf16[15,1024]{1,0:T(8,128)(2,1)S(1)}, bf16[15,1024]{1,0:T(8,128)(2,1)S(1)}, u32[]{:S(2)}, u32[]{:S(2)}) collective-permute-start(bf16[15,1024]{1,0:T(8,128)(2,1)S(1)} %get-tuple-element.23), channel_id=1, source_target_pairs={{0,8},{8,16},{16,24},{24,32},{32,40},{40,48},{48,56},{1,9},{9,17},... | collective-permute-start | bytes 92168 | tf_op jit(solution)/shard_map/ppermute | solution.py:14
  10.8 4.8 %collective-permute-start.1 = (bf16[15,1024]{1,0:T(8,128)(2,1)S(1)}, bf16[15,1024]{1,0:T(8,128)(2,1)S(1)}, u32[]{:S(2)}, u32[]{:S(2)}) collective-permute-start(bf16[15,1024]{1,0:T(8,128)(2,1)S(1)} %get-tuple-element.24), channel_id=1, source_target_pairs={{8,0},{16,8},{24,16},{32,24},{40,32},{48,40},{56,48},{9,1},{17,9},... | collective-permute-start | bytes 92168 | tf_op jit(solution)/shard_map/ppermute | solution.py:15
  15.7 5.2 %copy-start.10 = (f32[1024]{0:T(1024)S(1)}, f32[1024]{0:T(1024)}, u32[]{:S(2)}) copy-start(f32[1024]{0:T(1024)} %param.23) | copy-start | bytes 12292
  66.4 18.5 %collective-permute-start.3 = (bf16[384,1024]{1,0:T(8,128)(2,1)S(1)}, bf16[384,1024]{1,0:T(8,128)(2,1)}, u32[]{:S(2)}, u32[]{:S(2)}) collective-permute-start(bf16[384,1024]{1,0:T(8,128)(2,1)S(1)} %reshape.68), channel_id=1, source_target_pairs={{0,192},{64,0},{128,64},{192,128},{1,193},{65,1},{129,65},{193,129... | collective-permute-start | bytes 2359304 | tf_op jit(solution)/shard_map/ppermute | solution.py:108
  69.2 19.0 %collective-permute-start.2 = (bf16[384,1024]{1,0:T(8,128)(2,1)S(1)}, bf16[384,1024]{1,0:T(8,128)(2,1)}, u32[]{:S(2)}, u32[]{:S(2)}) collective-permute-start(bf16[384,1024]{1,0:T(8,128)(2,1)S(1)} %reshape.68), channel_id=1, source_target_pairs={{0,64},{64,128},{128,192},{192,0},{1,65},{65,129},{129,193},{193,1... | collective-permute-start | bytes 2359304 | tf_op jit(solution)/shard_map/ppermute | solution.py:107
  97.6 12.2 %collective-permute-start.5 = (bf16[192,1024]{1,0:T(8,128)(2,1)S(1)}, bf16[192,1024]{1,0:T(8,128)(2,1)}, u32[]{:S(2)}, u32[]{:S(2)}) collective-permute-start(bf16[192,1024]{1,0:T(8,128)(2,1)S(1)} %slice.313), channel_id=1, source_target_pairs={{0,192},{64,0},{128,64},{192,128},{1,193},{65,1},{129,65},{193,129... | collective-permute-start | bytes 1179656 | tf_op jit(solution)/shard_map/ppermute | solution.py:112
  97.9 11.9 %collective-permute-start.4 = (bf16[192,1024]{1,0:T(8,128)(2,1)S(1)}, bf16[192,1024]{1,0:T(8,128)(2,1)}, u32[]{:S(2)}, u32[]{:S(2)}) collective-permute-start(bf16[192,1024]{1,0:T(8,128)(2,1)S(1)} %slice.312), channel_id=1, source_target_pairs={{0,64},{64,128},{128,192},{192,0},{1,65},{65,129},{129,193},{193,1... | collective-permute-start | bytes 1179656 | tf_op jit(solution)/shard_map/ppermute | solution.py:112
  118.9 8.0 %copy-start.6 = (f32[384,1024]{1,0:T(8,128)S(1)}, f32[384,1024]{1,0:T(8,128)}, u32[]{:S(2)}) copy-start(f32[384,1024]{1,0:T(8,128)} %fusion.4) | copy-start | bytes 4718596
  118.9 11.2 %copy-start.5 = (f32[384,1024]{1,0:T(8,128)S(1)}, f32[384,1024]{1,0:T(8,128)}, u32[]{:S(2)}) copy-start(f32[384,1024]{1,0:T(8,128)} %fusion.2) | copy-start | bytes 4718596
  118.9 7.9 %collective-permute-start.8 = (bf16[192,1024]{1,0:T(8,128)(2,1)S(1)}, bf16[192,1024]{1,0:T(8,128)(2,1)S(1)}, u32[]{:S(2)}, u32[]{:S(2)}) collective-permute-start(bf16[192,1024]{1,0:T(8,128)(2,1)S(1)} %get-tuple-element.22), channel_id=1, source_target_pairs={{0,192},{64,0},{128,64},{192,128},{1,193},{65,1},{129,65},{193,129... | collective-permute-start | bytes 1179656 | tf_op jit(solution)/shard_map/ppermute | solution.py:119
  120.5 9.6 %collective-permute-start.6 = (bf16[192,1024]{1,0:T(8,128)(2,1)S(1)}, bf16[192,1024]{1,0:T(8,128)(2,1)S(1)}, u32[]{:S(2)}, u32[]{:S(2)}) collective-permute-start(bf16[192,1024]{1,0:T(8,128)(2,1)S(1)} %get-tuple-element.21), channel_id=1, source_target_pairs={{0,64},{64,128},{128,192},{192,0},{1,65},{65,129},{129,193},{193,1... | collective-permute-start | bytes 1179656 | tf_op jit(solution)/shard_map/ppermute | solution.py:118
  127.0 19.9 %copy-start.4 = (f32[384,1024]{1,0:T(8,128)S(1)}, f32[384,1024]{1,0:T(8,128)}, u32[]{:S(2)}) copy-start(f32[384,1024]{1,0:T(8,128)} %fusion.6) | copy-start | bytes 4718596
  127.0 16.5 %collective-permute-start.9 = (bf16[384,1024]{1,0:T(8,128)(2,1)S(1)}, bf16[384,1024]{1,0:T(8,128)(2,1)S(1)}, u32[]{:S(2)}, u32[]{:S(2)}) collective-permute-start(bf16[384,1024]{1,0:T(8,128)(2,1)S(1)} %add_convert_fusion.1), channel_id=1, source_target_pairs={{0,192},{64,0},{128,64},{192,128},{1,193},{65,1},{129,65},{193,129... | collective-permute-start | bytes 2359304 | tf_op jit(solution)/shard_map/ppermute | solution.py:123
  130.3 16.7 %collective-permute-start.7 = (bf16[384,1024]{1,0:T(8,128)(2,1)S(1)}, bf16[384,1024]{1,0:T(8,128)(2,1)S(1)}, u32[]{:S(2)}, u32[]{:S(2)}) collective-permute-start(bf16[384,1024]{1,0:T(8,128)(2,1)S(1)} %add_convert_fusion.2), channel_id=1, source_target_pairs={{0,64},{64,128},{128,192},{192,0},{1,65},{65,129},{129,193},{193,1... | collective-permute-start | bytes 2359304 | tf_op jit(solution)/shard_map/ppermute | solution.py:122
  147.3 13.5 %copy-start.8 = (bf16[1024,64]{0,1:T(8,128)(2,1)S(1)}, bf16[1024,64]{0,1:T(8,128)(2,1)}, u32[]{:S(2)}) copy-start(bf16[1024,64]{0,1:T(8,128)(2,1)} %param.24) | copy-start | bytes 393220
  148.6 12.2 %copy-start.2 = (bf16[128,1024]{1,0:T(8,128)(2,1)S(1)}, bf16[128,1024]{1,0:T(8,128)(2,1)}, u32[]{:S(2)}) copy-start(bf16[128,1024]{1,0:T(8,128)(2,1)} %copy-done.1) | copy-start | bytes 786436
  148.6 40.3 %all-to-all-start.1 = ((bf16[64,6,1024]{2,1,0:T(8,128)(2,1)}), bf16[64,6,1024]{2,1,0:T(8,128)(2,1)}, u32[]{:S(2)}, u32[]{:S(2)}) async-start(bf16[64,6,1024]{2,1,0:T(8,128)(2,1)} %reshape.69), calls=%async_computation.1 | async-start | bytes 2097152 | tf_op jit(solution)/shard_map/all_to_all | solution.py:126
  161.1 29.6 %copy-start.13 = (f32[128]{0:T(128)S(1)}, f32[128]{0:T(128)}, u32[]{:S(2)}) copy-start(f32[128]{0:T(128)} %copy-done.12) | copy-start | bytes 1540
  (4 other events, 9.9 us)

commit v4 on v3

--- a/solution.py
+++ b/solution.py
@@ -2,19 +2,6 @@
 import jax.numpy as jnp
 from jax import lax
 from jax.sharding import PartitionSpec as P
-
-
-def padded_2(x, sides, width):
-    for axis, dim in sides:
-        size, length = (lax.axis_size(axis), x.shape[dim])
-        up = [(i, (i + 1) % size) for i in range(size - 1)]
-        down = [(j, i) for i, j in up]
-        last = lax.slice_in_dim(x, length - width, length, axis=dim)
-        initial = lax.slice_in_dim(x, 0, width, axis=dim)
-        before = lax.ppermute(last, axis, up)
-        after = lax.ppermute(initial, axis, down)
-        x = jnp.concatenate([before, x, after], axis=dim)
-    return x
 
 
 def layer_norm(values, gain):
@@ -51,12 +38,23 @@
         jnp.bfloat16
     )
     reach = depth_kernel.shape[0] // 2
-    padded = padded_2(gated, (("seq", 0),), reach)
-    depth = jnp.zeros((token_count, model_width), jnp.float32)
-    for offset in range(depth_kernel.shape[0]):
-        depth = (
-            depth + padded[offset : offset + token_count].astype(jnp.float32) * depth_kernel[offset]
-        )
+    taps = depth_kernel.shape[0]
+    seq_size = lax.axis_size("seq")
+    seq_up = [(i, i + 1) for i in range(seq_size - 1)]
+    seq_down = [(j, i) for i, j in seq_up]
+    before = lax.ppermute(gated[token_count - reach :], "seq", seq_up)
+    after = lax.ppermute(gated[:reach], "seq", seq_down)
+
+    def depthwise(rows, count):
+        total = jnp.zeros((count, model_width), jnp.float32)
+        for offset in range(taps):
+            total = total + rows[offset : offset + count].astype(jnp.float32) * depth_kernel[offset]
+        return total
+
+    middle = depthwise(gated, token_count - 2 * reach)
+    head = depthwise(jnp.concatenate([before, gated[: 2 * reach]], axis=0), reach)
+    tail = depthwise(jnp.concatenate([gated[token_count - 2 * reach :], after], axis=0), reach)
+    depth = jnp.concatenate([head, middle, tail], axis=0)
     swished = jax.nn.silu(depth * bn_scale + bn_shift).astype(jnp.bfloat16)
     residual = frame_rows.astype(jnp.float32) + jnp.dot(
         swished, point_out, preferred_element_type=jnp.float32
@@ -114,14 +112,15 @@
     for_below = serve(from_below)
     for_above = serve(from_above)
     far_rows, for_below, for_above = lax.optimization_barrier((far_rows, for_below, for_above))
+    got_below = lax.ppermute(for_above.astype(jnp.bfloat16), "dp", up).astype(jnp.float32)
+    got_above = lax.ppermute(for_below.astype(jnp.bfloat16), "dp", down).astype(jnp.float32)
     for_far = serve(far_rows).astype(jnp.bfloat16)
-    far_up = lax.ppermute(for_far[:half], "dp", up).astype(jnp.float32)
-    far_down = lax.ppermute(for_far[half:], "dp", down).astype(jnp.float32)
-    send_up = for_above + jnp.concatenate([far_up, jnp.zeros_like(far_down)], axis=0)
-    send_down = for_below + jnp.concatenate([jnp.zeros_like(far_up), far_down], axis=0)
-    got_below = lax.ppermute(send_up.astype(jnp.bfloat16), "dp", up).astype(jnp.float32)
-    got_above = lax.ppermute(send_down.astype(jnp.bfloat16), "dp", down).astype(jnp.float32)
-    summed = for_own + got_below + got_above
+    hop_up = lax.ppermute(for_far[:half], "dp", up)
+    hop_down = lax.ppermute(for_far[half:], "dp", down)
+    far_got = jnp.concatenate(
+        [lax.ppermute(hop_up, "dp", up), lax.ppermute(hop_down, "dp", down)], axis=0
+    ).astype(jnp.float32)
+    summed = for_own + got_below + got_above + far_got
     served = summed.astype(jnp.bfloat16).reshape(arrived_shape)
     returned_rows = lax.all_to_all(
         served, ("seq", "expert"), split_axis=0, concat_axis=0, tiled=True

time: 192 us -> 188 us (0.979)
  waiting for transfers between devices: 64.8 us -> 57.1 us
  matrix products: 43.1 us -> 39.1 us
  starting transfers between devices: 26.9 us -> 30.3 us
  other arithmetic: 4.91 us -> 8.25 us
    ppermute x6 -> x8, waiting for transfers between devices: 25.9 us -> 18.1 us  [the longest x1 11.5 us: local(): hop_up = lax.ppermute(for_far[:half], 'dp', up)]
    dot_general x1, matrix products: 4.96 us -> 0.62 us  [local(): jnp.dot(swished, point_out, preferred_element_type=jnp.float32)]
    ppermute x6 -> x8, starting transfers between devices: 10.4 us -> 13.8 us  [the longest x1 4.36 us: local(): before = lax.ppermute(gated[token_count - reach:], 'seq', seq_up)]
    add x0 -> x3, other arithmetic: none -> 2.11 us  [depthwise(): total + rows[offset:offset + count].astype(jnp.float32) * depth_kernel[of...]
  transfers between devices with their start and end apart: 11 -> 13, of which waited for: 7 -> 6; matrix products, arithmetic and copies ran while one was open for 10% -> 16% of each run, Pallas kernels for 0% -> 0%
where the time goes in v4:
time: 188 us; the launch traced here: 187 us
  waiting for transfers between devices  57.1 us (30%)
  blocking collectives  41.8 us (22%)
  matrix products  39.1 us (21%)
  starting transfers between devices  30.3 us (16%)
  local copies, waits for them, and re-layouts  9.67 us (5%)
  other arithmetic  8.25 us (4%)
    all_to_all x1, blocking collectives, local(): lax.all_to_all(outgoing, ('seq', 'expert'), split_axis=0, concat_axis=0,...  41.8 us
    all_to_all x1, waiting for transfers between devices, local(): lax.all_to_all(served, ('seq', 'expert'), split_axis=0, concat_axis=0, ti...  27.8 us
    dot_general x4, matrix products, serve(): lax.dot_general(hidden, down_local, (((1,), (1,)), ((), ())), preferred_e...  21.7 us
    all_to_all x1, starting transfers between devices, local(): lax.all_to_all(served, ('seq', 'expert'), split_axis=0, concat_axis=0, ti...  12.2 us
    ppermute x1, waiting for transfers between devices, local(): hop_up = lax.ppermute(for_far[:half], 'dp', up)  11.5 us
    ppermute x1, waiting for transfers between devices, local(): from_above = lax.ppermute(own_rows, 'dp', down)  7.88 us
    dot_general x2, matrix products, serve(): up_part = jnp.dot(rows, up_local, preferred_element_type=jnp.float32)  7.35 us
    ppermute x1, waiting for transfers between devices, local(): lax.ppermute(hop_up, 'dp', up)  5.49 us
  transfers between devices with their start and end apart: 13, of which 6 were waited for; matrix products, arithmetic and copies ran while one was open for 16% of the time, Pallas kernels for 0%

profile of v4, /device:TPU:1, one launch (start us, length us, event | category | flops | bytes accessed | tf_op | source)
XLA Modules:
  0.0 187.4 jit_solution(13037498160244816659)
XLA Ops:
  3.1 3.1 %fusion.65 = f32[128,2048]{1,0:T(8,128)S(1)} fusion(bf16[1024,2048]{1,0:T(8,128)(2,1)} %param.18, bf16[1,128,1024]{2,1,0:T(8,128)(2,1)} %param.14, f32[1024]{0:T(1024)} %param.17, f32[128]{0:T(128)S(1)} %add_rsqrt_fusion.1, f32[128]{0:T(128)S(1)} %broadcast_multiply_fusion.1), kind=kOutput, calls=%fused_computation.91 | convolution fusion | flops 537526272 | bytes 5510144 | tf_op jit(solution)/shard_map/dot_general | solution.py:36
  6.4 4.4 %collective-permute-start = (bf16[15,1024]{1,0:T(8,128)(2,1)S(1)}, bf16[15,1024]{1,0:T(8,128)(2,1)S(1)}, u32[]{:S(2)}, u32[]{:S(2)}) collective-permute-start(bf16[15,1024]{1,0:T(8,128)(2,1)S(1)} %get-tuple-element.25), channel_id=1, source_target_pairs={{0,8},{8,16},{16,24},{24,32},{32,40},{40,48},{48,56},{1,9},{9,17},... | collective-permute-start | bytes 92168 | tf_op jit(solution)/shard_map/ppermute | solution.py:45
  12.7 1.5 multiply_add_fusion
  19.4 41.8 %all_to_all.10 = bf16[64,6,1024]{2,1,0:T(8,128)(2,1)} all-to-all(bf16[64,6,1024]{2,1,0:T(8,128)(2,1)} %reshape.67), channel_id=1, replica_groups=mesh['dp'=4,'seq'=8,'expert'=8] {'seq','expert'}, dimensions={0} | all-to-all | bytes 1572864 | tf_op jit(solution)/shard_map/all_to_all | solution.py:89
  61.2 1.4 reshape.68
  62.6 2.8 %collective-permute-start.3 = (bf16[384,1024]{1,0:T(8,128)(2,1)S(1)}, bf16[384,1024]{1,0:T(8,128)(2,1)}, u32[]{:S(2)}, u32[]{:S(2)}) collective-permute-start(bf16[384,1024]{1,0:T(8,128)(2,1)S(1)} %reshape.68), channel_id=1, source_target_pairs={{0,192},{64,0},{128,64},{192,128},{1,193},{65,1},{129,65},{193,129... | collective-permute-start | bytes 2359304 | tf_op jit(solution)/shard_map/ppermute | solution.py:106
  65.4 2.1 %fusion.22 = f32[384,1024]{1,0:T(8,128)} fusion(bf16[384,1024]{1,0:T(8,128)(2,1)S(1)} %reshape.68, bf16[1,1024,1024]{2,1,0:T(8,128)(2,1)S(1)} %copy-done), kind=kOutput, calls=%fused_computation.22 | convolution fusion | flops 805306368 | bytes 4456448 | tf_op jit(solution)/shard_map/dot_general | solution.py:94
  67.5 5.8 %fusion.6 = f32[384,1024]{1,0:T(8,128)} fusion(bf16[1,1024,1024]{2,1,0:T(8,128)(2,1)} %param.27, f32[384,1024]{1,0:T(8,128)} %fusion.22, bf16[384,1024]{1,0:T(8,128)(2,1)S(1)} %reshape.68, bf16[1,1024,1024]{2,1,0:T(8,128)(2,1)} %param.26), kind=kOutput, calls=%fused_computation.6 | convolution fusion | flops 1612972032 | bytes 8126464 | tf_op jit(solution)/shard_map/dot_general | solution.py:97
  73.3 7.9 %collective-permute-done.3 = bf16[384,1024]{1,0:T(8,128)(2,1)} collective-permute-done((bf16[384,1024]{1,0:T(8,128)(2,1)S(1)}, bf16[384,1024]{1,0:T(8,128)(2,1)}, u32[]{:S(2)}, u32[]{:S(2)}) %collective-permute-start.3) | collective-permute-done | bytes 786464 | tf_op jit(solution)/shard_map/ppermute | solution.py:106
  81.2 3.2 %collective-permute-done.2 = bf16[384,1024]{1,0:T(8,128)(2,1)} collective-permute-done((bf16[384,1024]{1,0:T(8,128)(2,1)S(1)}, bf16[384,1024]{1,0:T(8,128)(2,1)}, u32[]{:S(2)}, u32[]{:S(2)}) %collective-permute-start.2) | collective-permute-done | bytes 786464 | tf_op jit(solution)/shard_map/ppermute | solution.py:105
  85.4 4.1 %fusion.12 = f32[384,1024]{1,0:T(8,128)} fusion(bf16[384,1024]{1,0:T(8,128)(2,1)} %collective-permute-done.2, bf16[1,1024,1024]{2,1,0:T(8,128)(2,1)} %param.26), kind=kOutput, calls=%fused_computation.12 | convolution fusion | flops 805306368 | bytes 4456448 | tf_op jit(solution)/shard_map/dot_general | solution.py:95
  90.6 3.2 %fusion.10 = f32[384,1024]{1,0:T(8,128)} fusion(bf16[384,1024]{1,0:T(8,128)(2,1)} %collective-permute-done.3, bf16[1,1024,1024]{2,1,0:T(8,128)(2,1)S(1)} %copy-done.14), kind=kOutput, calls=%fused_computation.10 | convolution fusion | flops 805306368 | bytes 4456448 | tf_op jit(solution)/shard_map/dot_general | solution.py:95
  95.3 5.1 %fusion.4 = bf16[384,1024]{1,0:T(8,128)(2,1)} fusion(bf16[1,1024,1024]{2,1,0:T(8,128)(2,1)} %param.27, f32[384,1024]{1,0:T(8,128)} %fusion.12, bf16[384,1024]{1,0:T(8,128)(2,1)} %collective-permute-done.2, bf16[1,1024,1024]{2,1,0:T(8,128)(2,1)S(1)} %copy-done), kind=kOutput, calls=%fused_computation.4 | convolution fusion | flops 1612972032 | bytes 7340032 | tf_op jit(solution)/shard_map/dot_general | solution.py:97
  100.4 5.1 %fusion.2 = bf16[384,1024]{1,0:T(8,128)(2,1)} fusion(bf16[1,1024,1024]{2,1,0:T(8,128)(2,1)} %param.27, f32[384,1024]{1,0:T(8,128)} %fusion.10, bf16[384,1024]{1,0:T(8,128)(2,1)} %collective-permute-done.3, bf16[1,1024,1024]{2,1,0:T(8,128)(2,1)S(1)} %copy-done), kind=kOutput, calls=%fused_computation.2 | convolution fusion | flops 1612972032 | bytes 7340032 | tf_op jit(solution)/shard_map/dot_general | solution.py:97
  106.8 2.7 %collective-permute-start.7 = (bf16[384,1024]{1,0:T(8,128)(2,1)}, bf16[384,1024]{1,0:T(8,128)(2,1)}, u32[]{:S(2)}, u32[]{:S(2)}) collective-permute-start(bf16[384,1024]{1,0:T(8,128)(2,1)} %fusion.4), channel_id=1, source_target_pairs={{0,192},{64,0},{128,64},{192,128},{1,193},{65,1},{129,65},{193,129... | collective-permute-start | bytes 2359304 | tf_op jit(solution)/shard_map/ppermute | solution.py:116
  109.5 2.1 %fusion.16 = f32[384,1024]{1,0:T(8,128)} fusion(bf16[384,1024]{1,0:T(8,128)(2,1)S(1)} %pad_maximum_fusion, bf16[1,1024,1024]{2,1,0:T(8,128)(2,1)S(1)} %copy-done), kind=kOutput, calls=%fused_computation.16 | convolution fusion | flops 805306368 | bytes 4456448 | tf_op jit(solution)/shard_map/dot_general | solution.py:94
  111.6 5.7 %fusion.28 = bf16[384,1024]{1,0:T(8,128)(2,1)} fusion(bf16[1,1024,1024]{2,1,0:T(8,128)(2,1)} %param.27, f32[384,1024]{1,0:T(8,128)} %fusion.16, bf16[384,1024]{1,0:T(8,128)(2,1)} %copy-done.6, bf16[1,1024,1024]{2,1,0:T(8,128)(2,1)} %param.26), kind=kOutput, calls=%fused_computation.30 | convolution fusion | flops 1613365248 | bytes 7340032 | tf_op jit(solution)/shard_map/dot_general | solution.py:97
  118.7 2.7 %collective-permute-start.10 = (bf16[192,1024]{1,0:T(8,128)(2,1)S(1)}, bf16[192,1024]{1,0:T(8,128)(2,1)S(1)}, u32[]{:S(2)}, u32[]{:S(2)}) collective-permute-start(bf16[192,1024]{1,0:T(8,128)(2,1)S(1)} %get-tuple-element.22), channel_id=1, source_target_pairs={{0,192},{64,0},{128,64},{192,128},{1,193},{65,1},{129,65},{193,129... | collective-permute-start | bytes 1179656 | tf_op jit(solution)/shard_map/ppermute | solution.py:119
  121.4 11.5 %collective-permute-done.8 = bf16[192,1024]{1,0:T(8,128)(2,1)S(1)} collective-permute-done((bf16[192,1024]{1,0:T(8,128)(2,1)S(1)}, bf16[192,1024]{1,0:T(8,128)(2,1)S(1)}, u32[]{:S(2)}, u32[]{:S(2)}) %collective-permute-start.8) | collective-permute-done | bytes 393248 | tf_op jit(solution)/shard_map/ppermute | solution.py:118
  132.9 2.7 %collective-permute-start.11 = (bf16[192,1024]{1,0:T(8,128)(2,1)S(1)}, bf16[192,1024]{1,0:T(8,128)(2,1)S(1)}, u32[]{:S(2)}, u32[]{:S(2)}) collective-permute-start(bf16[192,1024]{1,0:T(8,128)(2,1)S(1)} %collective-permute-done.10), channel_id=1, source_target_pairs={{0,192},{64,0},{128,64},{192,128},{1,193},{65,1},{129,65},{193,129... | collective-permute-start | bytes 1179656 | tf_op jit(solution)/shard_map/ppermute | solution.py:121
  135.6 5.5 %collective-permute-done.9 = bf16[192,1024]{1,0:T(8,128)(2,1)S(1)} collective-permute-done((bf16[192,1024]{1,0:T(8,128)(2,1)S(1)}, bf16[192,1024]{1,0:T(8,128)(2,1)S(1)}, u32[]{:S(2)}, u32[]{:S(2)}) %collective-permute-start.9) | collective-permute-done | bytes 393248 | tf_op jit(solution)/shard_map/ppermute | solution.py:121
  141.1 1.9 %add_convert_fusion = bf16[384,1024]{1,0:T(8,128)(2,1)S(1)} fusion(bf16[384,1024]{1,0:T(8,128)(2,1)} %collective-permute-done.7, f32[384,1024]{1,0:T(8,128)S(1)} %copy-done.4, bf16[384,1024]{1,0:T(8,128)(2,1)} %copy-done.5, bf16[192,1024]{1,0:T(8,128)(2,1)S(1)} %collective-permute-done.11, bf16[192,1024]{1,0:T(8,128)(2,1)S(1)} %collective-permute-done.9), kind=kLoop, calls=%fused_computation.24 | loop fusion | flops 3932160 | bytes 4718592 | tf_op jit(solution)/shard_map/convert_element_type | solution.py:124
  144.3 12.2 %all-to-all-start.1 = ((bf16[64,6,1024]{2,1,0:T(8,128)(2,1)}), bf16[64,6,1024]{2,1,0:T(8,128)(2,1)}, u32[]{:S(2)}, u32[]{:S(2)}) async-start(bf16[64,6,1024]{2,1,0:T(8,128)(2,1)} %reshape.69), calls=%async_computation.1 | async-start | bytes 2097152 | tf_op jit(solution)/shard_map/all_to_all | solution.py:125
  156.8 27.8 %all-to-all-done.1 = bf16[64,6,1024]{2,1,0:T(8,128)(2,1)} async-done(((bf16[64,6,1024]{2,1,0:T(8,128)(2,1)}), bf16[64,6,1024]{2,1,0:T(8,128)(2,1)}, u32[]{:S(2)}, u32[]{:S(2)}) %all-to-all-start.1) | async-done | bytes 786464 | tf_op jit(solution)/shard_map/all_to_all | solution.py:125
  (85 shorter events, 19.9 us)
Async XLA Ops:
  0.0 65.4 %copy-start = (bf16[1,1024,1024]{2,1,0:T(8,128)(2,1)S(1)}, bf16[1,1024,1024]{2,1,0:T(8,128)(2,1)}, u32[]{:S(2)}) copy-start(bf16[1,1024,1024]{2,1,0:T(8,128)(2,1)} %param.25) | copy-start | bytes 6291460
  3.1 3.1 %copy-start.11 = (f32[128]{0:T(128)}, f32[128]{0:T(128)S(1)}, u32[]{:S(2)}) copy-start(f32[128]{0:T(128)S(1)} %compare_convert_fusion) | copy-start | bytes 1540
  3.1 9.0 %copy-start.8 = (f32[31,1024]{1,0:T(8,128)S(1)}, f32[31,1024]{1,0:T(8,128)}, u32[]{:S(2)}) copy-start(f32[31,1024]{1,0:T(8,128)} %param.19) | copy-start | bytes 380932
  6.2 6.0 %copy-start.10 = (s32[1,128,2]{1,2,0:T(2,128)S(1)}, s32[1,128,2]{1,2,0:T(2,128)}, u32[]{:S(2)}) copy-start(s32[1,128,2]{1,2,0:T(2,128)} %param.16) | copy-start | bytes 3076
  6.4 7.8 %collective-permute-start = (bf16[15,1024]{1,0:T(8,128)(2,1)S(1)}, bf16[15,1024]{1,0:T(8,128)(2,1)S(1)}, u32[]{:S(2)}, u32[]{:S(2)}) collective-permute-start(bf16[15,1024]{1,0:T(8,128)(2,1)S(1)} %get-tuple-element.25), channel_id=1, source_target_pairs={{0,8},{8,16},{16,24},{24,32},{32,40},{40,48},{48,56},{1,9},{9,17},... | collective-permute-start | bytes 92168 | tf_op jit(solution)/shard_map/ppermute | solution.py:45
  10.8 4.8 %collective-permute-start.1 = (bf16[15,1024]{1,0:T(8,128)(2,1)S(1)}, bf16[15,1024]{1,0:T(8,128)(2,1)S(1)}, u32[]{:S(2)}, u32[]{:S(2)}) collective-permute-start(bf16[15,1024]{1,0:T(8,128)(2,1)S(1)} %get-tuple-element.26), channel_id=1, source_target_pairs={{8,0},{16,8},{24,16},{32,24},{40,32},{48,40},{56,48},{9,1},{17,9},... | collective-permute-start | bytes 92168 | tf_op jit(solution)/shard_map/ppermute | solution.py:46
  12.7 3.3 %copy-start.13 = (bf16[1024,1024]{1,0:T(8,128)(2,1)S(1)}, bf16[1024,1024]{1,0:T(8,128)(2,1)}, u32[]{:S(2)}) copy-start(bf16[1024,1024]{1,0:T(8,128)(2,1)} %param.22) | copy-start | bytes 6291460
  62.6 18.6 %collective-permute-start.3 = (bf16[384,1024]{1,0:T(8,128)(2,1)S(1)}, bf16[384,1024]{1,0:T(8,128)(2,1)}, u32[]{:S(2)}, u32[]{:S(2)}) collective-permute-start(bf16[384,1024]{1,0:T(8,128)(2,1)S(1)} %reshape.68), channel_id=1, source_target_pairs={{0,192},{64,0},{128,64},{192,128},{1,193},{65,1},{129,65},{193,129... | collective-permute-start | bytes 2359304 | tf_op jit(solution)/shard_map/ppermute | solution.py:106
  65.4 19.0 %collective-permute-start.2 = (bf16[384,1024]{1,0:T(8,128)(2,1)S(1)}, bf16[384,1024]{1,0:T(8,128)(2,1)}, u32[]{:S(2)}, u32[]{:S(2)}) collective-permute-start(bf16[384,1024]{1,0:T(8,128)(2,1)S(1)} %reshape.68), channel_id=1, source_target_pairs={{0,64},{64,128},{128,192},{192,0},{1,65},{65,129},{129,193},{193,1... | collective-permute-start | bytes 2359304 | tf_op jit(solution)/shard_map/ppermute | solution.py:105
  85.4 5.1 %copy-start.14 = (bf16[1,1024,1024]{2,1,0:T(8,128)(2,1)S(1)}, bf16[1,1024,1024]{2,1,0:T(8,128)(2,1)}, u32[]{:S(2)}) copy-start(bf16[1,1024,1024]{2,1,0:T(8,128)(2,1)} %param.26) | copy-start | bytes 6291460
  93.8 11.7 %collective-permute-start.5 = (bf16[192,1024]{1,0:T(8,128)(2,1)S(1)}, bf16[192,1024]{1,0:T(8,128)(2,1)}, u32[]{:S(2)}, u32[]{:S(2)}) collective-permute-start(bf16[192,1024]{1,0:T(8,128)(2,1)S(1)} %slice.623), channel_id=1, source_target_pairs={{0,192},{64,0},{128,64},{192,128},{1,193},{65,1},{129,65},{193,129... | collective-permute-start | bytes 1179656 | tf_op jit(solution)/shard_map/ppermute | solution.py:110
  94.1 11.4 %collective-permute-start.4 = (bf16[192,1024]{1,0:T(8,128)(2,1)S(1)}, bf16[192,1024]{1,0:T(8,128)(2,1)}, u32[]{:S(2)}, u32[]{:S(2)}) collective-permute-start(bf16[192,1024]{1,0:T(8,128)(2,1)S(1)} %slice.622), channel_id=1, source_target_pairs={{0,64},{64,128},{128,192},{192,0},{1,65},{65,129},{129,193},{193,1... | collective-permute-start | bytes 1179656 | tf_op jit(solution)/shard_map/ppermute | solution.py:110
  106.7 28.9 %collective-permute-start.6 = (bf16[384,1024]{1,0:T(8,128)(2,1)}, bf16[384,1024]{1,0:T(8,128)(2,1)S(1)}, u32[]{:S(2)}, u32[]{:S(2)}) collective-permute-start(bf16[384,1024]{1,0:T(8,128)(2,1)} %fusion.2), channel_id=1, source_target_pairs={{0,64},{64,128},{128,192},{192,0},{1,65},{65,129},{129,193},{193,1... | collective-permute-start | bytes 2359304 | tf_op jit(solution)/shard_map/ppermute | solution.py:115
  106.8 28.8 %collective-permute-start.7 = (bf16[384,1024]{1,0:T(8,128)(2,1)}, bf16[384,1024]{1,0:T(8,128)(2,1)}, u32[]{:S(2)}, u32[]{:S(2)}) collective-permute-start(bf16[384,1024]{1,0:T(8,128)(2,1)} %fusion.4), channel_id=1, source_target_pairs={{0,192},{64,0},{128,64},{192,128},{1,193},{65,1},{129,65},{193,129... | collective-permute-start | bytes 2359304 | tf_op jit(solution)/shard_map/ppermute | solution.py:116
  117.3 23.8 %copy-start.4 = (f32[384,1024]{1,0:T(8,128)S(1)}, f32[384,1024]{1,0:T(8,128)}, u32[]{:S(2)}) copy-start(f32[384,1024]{1,0:T(8,128)} %fusion.6) | copy-start | bytes 4718596
  118.6 14.3 %collective-permute-start.8 = (bf16[192,1024]{1,0:T(8,128)(2,1)S(1)}, bf16[192,1024]{1,0:T(8,128)(2,1)S(1)}, u32[]{:S(2)}, u32[]{:S(2)}) collective-permute-start(bf16[192,1024]{1,0:T(8,128)(2,1)S(1)} %get-tuple-element.21), channel_id=1, source_target_pairs={{0,64},{64,128},{128,192},{192,0},{1,65},{65,129},{129,193},{193,1... | collective-permute-start | bytes 1179656 | tf_op jit(solution)/shard_map/ppermute | solution.py:118
  118.7 14.2 %collective-permute-start.10 = (bf16[192,1024]{1,0:T(8,128)(2,1)S(1)}, bf16[192,1024]{1,0:T(8,128)(2,1)S(1)}, u32[]{:S(2)}, u32[]{:S(2)}) collective-permute-start(bf16[192,1024]{1,0:T(8,128)(2,1)S(1)} %get-tuple-element.22), channel_id=1, source_target_pairs={{0,192},{64,0},{128,64},{192,128},{1,193},{65,1},{129,65},{193,129... | collective-permute-start | bytes 1179656 | tf_op jit(solution)/shard_map/ppermute | solution.py:119
  132.9 8.2 %collective-permute-start.9 = (bf16[192,1024]{1,0:T(8,128)(2,1)S(1)}, bf16[192,1024]{1,0:T(8,128)(2,1)S(1)}, u32[]{:S(2)}, u32[]{:S(2)}) collective-permute-start(bf16[192,1024]{1,0:T(8,128)(2,1)S(1)} %collective-permute-done.8), channel_id=1, source_target_pairs={{0,64},{64,128},{128,192},{192,0},{1,65},{65,129},{129,193},{193,1... | collective-permute-start | bytes 1179656 | tf_op jit(solution)/shard_map/ppermute | solution.py:121
  132.9 8.2 %collective-permute-start.11 = (bf16[192,1024]{1,0:T(8,128)(2,1)S(1)}, bf16[192,1024]{1,0:T(8,128)(2,1)S(1)}, u32[]{:S(2)}, u32[]{:S(2)}) collective-permute-start(bf16[192,1024]{1,0:T(8,128)(2,1)S(1)} %collective-permute-done.10), channel_id=1, source_target_pairs={{0,192},{64,0},{128,64},{192,128},{1,193},{65,1},{129,65},{193,129... | collective-permute-start | bytes 1179656 | tf_op jit(solution)/shard_map/ppermute | solution.py:121
  135.6 5.5 %copy-start.5 = (bf16[384,1024]{1,0:T(8,128)(2,1)}, bf16[384,1024]{1,0:T(8,128)(2,1)S(1)}, u32[]{:S(2)}) copy-start(bf16[384,1024]{1,0:T(8,128)(2,1)S(1)} %collective-permute-done.6) | copy-start | bytes 2359300
  143.0 13.5 %copy-start.7 = (bf16[1024,64]{0,1:T(8,128)(2,1)S(1)}, bf16[1024,64]{0,1:T(8,128)(2,1)}, u32[]{:S(2)}) copy-start(bf16[1024,64]{0,1:T(8,128)(2,1)} %param.24) | copy-start | bytes 393220
  144.3 12.2 %copy-start.2 = (bf16[128,1024]{1,0:T(8,128)(2,1)S(1)}, bf16[128,1024]{1,0:T(8,128)(2,1)}, u32[]{:S(2)}) copy-start(bf16[128,1024]{1,0:T(8,128)(2,1)} %copy-done.1) | copy-start | bytes 786436
  144.3 40.3 %all-to-all-start.1 = ((bf16[64,6,1024]{2,1,0:T(8,128)(2,1)}), bf16[64,6,1024]{2,1,0:T(8,128)(2,1)}, u32[]{:S(2)}, u32[]{:S(2)}) async-start(bf16[64,6,1024]{2,1,0:T(8,128)(2,1)} %reshape.69), calls=%async_computation.1 | async-start | bytes 2097152 | tf_op jit(solution)/shard_map/all_to_all | solution.py:125
  156.8 29.6 %copy-start.12 = (f32[128]{0:T(128)S(1)}, f32[128]{0:T(128)}, u32[]{:S(2)}) copy-start(f32[128]{0:T(128)} %copy-done.11) | copy-start | bytes 1540
  (6 other events, 9.8 us)

commit v5 on v4

--- a/solution.py
+++ b/solution.py
@@ -82,13 +82,14 @@
     outgoing = lax.dot_general(
         slot_one + slot_two, moe_in, (((0,), (0,)), ((), ())), preferred_element_type=jnp.float32
     ).astype(jnp.bfloat16)
-    outgoing = outgoing.reshape(expert_count, capacity, model_width)
+    lanes = 128
+    outgoing = outgoing.reshape(expert_count, capacity * model_width // lanes, lanes)
     gate_local = gate_weight[0]
     up_local = up_weight[0]
     down_local = down_weight[0]
     arrived = lax.all_to_all(outgoing, ("seq", "expert"), split_axis=0, concat_axis=0, tiled=True)
     arrived_shape = arrived.shape
-    own_rows = arrived.reshape(-1, arrived_shape[2])
+    own_rows = arrived.reshape(-1, model_width)
 
     def serve(rows):
         gate_part = jnp.dot(rows, gate_local, preferred_element_type=jnp.float32)

time: 188 us -> 178 us (0.947)
  blocking collectives: 41.8 us -> 36.4 us
  waiting for transfers between devices: 57.1 us -> 53.3 us
  starting transfers between devices: 30.3 us -> 28.2 us
    all_to_all x1, blocking collectives: 41.8 us -> 36.4 us  [local(): lax.all_to_all(outgoing, ('seq', 'expert'), split_axis=0, concat_axis=0,...]
    all_to_all x1, waiting for transfers between devices: 27.8 us -> 22.7 us  [local(): lax.all_to_all(served, ('seq', 'expert'), split_axis=0, concat_axis=0, ti...]
    all_to_all x1, starting transfers between devices: 12.2 us -> 10.1 us  [local(): lax.all_to_all(served, ('seq', 'expert'), split_axis=0, concat_axis=0, ti...]
  transfers between devices with their start and end apart: 13 -> 13, of which waited for: 6 -> 6; matrix products, arithmetic and copies ran while one was open for 16% -> 17% of each run, Pallas kernels for 0% -> 0%
where the time goes in v5:
time: 178 us; the launch traced here: 177 us
  waiting for transfers between devices  53.3 us (30%)
  matrix products  40 us (22%)
  blocking collectives  36.4 us (20%)
  starting transfers between devices  28.2 us (16%)
  local copies, waits for them, and re-layouts  9.91 us (6%)
  other arithmetic  8.25 us (5%)
    all_to_all x1, blocking collectives, local(): lax.all_to_all(outgoing, ('seq', 'expert'), split_axis=0, concat_axis=0,...  36.4 us
    all_to_all x1, waiting for transfers between devices, local(): lax.all_to_all(served, ('seq', 'expert'), split_axis=0, concat_axis=0, ti...  22.7 us
    dot_general x4, matrix products, serve(): lax.dot_general(hidden, down_local, (((1,), (1,)), ((), ())), preferred_e...  21.7 us
    ppermute x1, waiting for transfers between devices, local(): hop_up = lax.ppermute(for_far[:half], 'dp', up)  12 us
    all_to_all x1, starting transfers between devices, local(): lax.all_to_all(served, ('seq', 'expert'), split_axis=0, concat_axis=0, ti...  10.1 us
    ppermute x1, waiting for transfers between devices, local(): from_above = lax.ppermute(own_rows, 'dp', down)  8.33 us
    dot_general x2, matrix products, serve(): up_part = jnp.dot(rows, up_local, preferred_element_type=jnp.float32)  7.35 us
    ppermute x1, waiting for transfers between devices, local(): lax.ppermute(hop_up, 'dp', up)  5.93 us
  transfers between devices with their start and end apart: 13, of which 6 were waited for; matrix products, arithmetic and copies ran while one was open for 17% of the time, Pallas kernels for 0%

profile of v5, /device:TPU:1, one launch (start us, length us, event | category | flops | bytes accessed | tf_op | source)
XLA Modules:
  0.0 177.3 jit_solution(2385720827061065435)
XLA Ops:
  3.1 3.1 %fusion.65 = f32[128,2048]{1,0:T(8,128)S(1)} fusion(bf16[1024,2048]{1,0:T(8,128)(2,1)} %param.18, bf16[1,128,1024]{2,1,0:T(8,128)(2,1)} %param.14, f32[1024]{0:T(1024)} %param.17, f32[128]{0:T(128)S(1)} %add_rsqrt_fusion.1, f32[128]{0:T(128)S(1)} %broadcast_multiply_fusion.1), kind=kOutput, calls=%fused_computation.91 | convolution fusion | flops 537526272 | bytes 5510144 | tf_op jit(solution)/shard_map/dot_general | solution.py:36
  6.4 4.4 %collective-permute-start = (bf16[15,1024]{1,0:T(8,128)(2,1)S(1)}, bf16[15,1024]{1,0:T(8,128)(2,1)S(1)}, u32[]{:S(2)}, u32[]{:S(2)}) collective-permute-start(bf16[15,1024]{1,0:T(8,128)(2,1)S(1)} %get-tuple-element.25), channel_id=1, source_target_pairs={{0,8},{8,16},{16,24},{24,32},{32,40},{40,48},{48,56},{1,9},{9,17},... | collective-permute-start | bytes 92168 | tf_op jit(solution)/shard_map/ppermute | solution.py:45
  12.7 1.5 multiply_add_fusion
  20.5 36.4 %all_to_all.10 = bf16[64,48,128]{2,1,0:T(8,128)(2,1)} all-to-all(bf16[64,48,128]{2,1,0:T(8,128)(2,1)S(1)} %reshape.67), channel_id=1, replica_groups=mesh['dp'=4,'seq'=8,'expert'=8] {'seq','expert'}, dimensions={0} | all-to-all | bytes 1572864 | tf_op jit(solution)/shard_map/all_to_all | solution.py:90
  56.9 1.4 reshape.68
  58.4 2.8 %collective-permute-start.3 = (bf16[384,1024]{1,0:T(8,128)(2,1)S(1)}, bf16[384,1024]{1,0:T(8,128)(2,1)}, u32[]{:S(2)}, u32[]{:S(2)}) collective-permute-start(bf16[384,1024]{1,0:T(8,128)(2,1)S(1)} %reshape.68), channel_id=1, source_target_pairs={{0,192},{64,0},{128,64},{192,128},{1,193},{65,1},{129,65},{193,129... | collective-permute-start | bytes 2359304 | tf_op jit(solution)/shard_map/ppermute | solution.py:107
  61.2 2.1 %fusion.22 = f32[384,1024]{1,0:T(8,128)} fusion(bf16[384,1024]{1,0:T(8,128)(2,1)S(1)} %reshape.68, bf16[1,1024,1024]{2,1,0:T(8,128)(2,1)S(1)} %copy-done), kind=kOutput, calls=%fused_computation.22 | convolution fusion | flops 805306368 | bytes 4456448 | tf_op jit(solution)/shard_map/dot_general | solution.py:95
  63.3 5.8 %fusion.6 = f32[384,1024]{1,0:T(8,128)} fusion(bf16[1,1024,1024]{2,1,0:T(8,128)(2,1)} %param.27, f32[384,1024]{1,0:T(8,128)} %fusion.22, bf16[384,1024]{1,0:T(8,128)(2,1)S(1)} %reshape.68, bf16[1,1024,1024]{2,1,0:T(8,128)(2,1)} %param.26), kind=kOutput, calls=%fused_computation.6 | convolution fusion | flops 1612972032 | bytes 8126464 | tf_op jit(solution)/shard_map/dot_general | solution.py:98
  69.0 8.3 %collective-permute-done.3 = bf16[384,1024]{1,0:T(8,128)(2,1)} collective-permute-done((bf16[384,1024]{1,0:T(8,128)(2,1)S(1)}, bf16[384,1024]{1,0:T(8,128)(2,1)}, u32[]{:S(2)}, u32[]{:S(2)}) %collective-permute-start.3) | collective-permute-done | bytes 786464 | tf_op jit(solution)/shard_map/ppermute | solution.py:107
  77.4 3.2 %collective-permute-done.2 = bf16[384,1024]{1,0:T(8,128)(2,1)} collective-permute-done((bf16[384,1024]{1,0:T(8,128)(2,1)S(1)}, bf16[384,1024]{1,0:T(8,128)(2,1)}, u32[]{:S(2)}, u32[]{:S(2)}) %collective-permute-start.2) | collective-permute-done | bytes 786464 | tf_op jit(solution)/shard_map/ppermute | solution.py:106
  81.6 4.1 %fusion.12 = f32[384,1024]{1,0:T(8,128)} fusion(bf16[384,1024]{1,0:T(8,128)(2,1)} %collective-permute-done.2, bf16[1,1024,1024]{2,1,0:T(8,128)(2,1)} %param.26), kind=kOutput, calls=%fused_computation.12 | convolution fusion | flops 805306368 | bytes 4456448 | tf_op jit(solution)/shard_map/dot_general | solution.py:96
  86.8 3.2 %fusion.10 = f32[384,1024]{1,0:T(8,128)} fusion(bf16[384,1024]{1,0:T(8,128)(2,1)} %collective-permute-done.3, bf16[1,1024,1024]{2,1,0:T(8,128)(2,1)S(1)} %copy-done.14), kind=kOutput, calls=%fused_computation.10 | convolution fusion | flops 805306368 | bytes 4456448 | tf_op jit(solution)/shard_map/dot_general | solution.py:96
  91.5 5.1 %fusion.4 = bf16[384,1024]{1,0:T(8,128)(2,1)} fusion(bf16[1,1024,1024]{2,1,0:T(8,128)(2,1)} %param.27, f32[384,1024]{1,0:T(8,128)} %fusion.12, bf16[384,1024]{1,0:T(8,128)(2,1)} %collective-permute-done.2, bf16[1,1024,1024]{2,1,0:T(8,128)(2,1)S(1)} %copy-done), kind=kOutput, calls=%fused_computation.4 | convolution fusion | flops 1612972032 | bytes 7340032 | tf_op jit(solution)/shard_map/dot_general | solution.py:98
  96.6 5.1 %fusion.2 = bf16[384,1024]{1,0:T(8,128)(2,1)} fusion(bf16[1,1024,1024]{2,1,0:T(8,128)(2,1)} %param.27, f32[384,1024]{1,0:T(8,128)} %fusion.10, bf16[384,1024]{1,0:T(8,128)(2,1)} %collective-permute-done.3, bf16[1,1024,1024]{2,1,0:T(8,128)(2,1)S(1)} %copy-done), kind=kOutput, calls=%fused_computation.2 | convolution fusion | flops 1612972032 | bytes 7340032 | tf_op jit(solution)/shard_map/dot_general | solution.py:98
  103.0 2.7 %collective-permute-start.7 = (bf16[384,1024]{1,0:T(8,128)(2,1)}, bf16[384,1024]{1,0:T(8,128)(2,1)}, u32[]{:S(2)}, u32[]{:S(2)}) collective-permute-start(bf16[384,1024]{1,0:T(8,128)(2,1)} %fusion.4), channel_id=1, source_target_pairs={{0,192},{64,0},{128,64},{192,128},{1,193},{65,1},{129,65},{193,129... | collective-permute-start | bytes 2359304 | tf_op jit(solution)/shard_map/ppermute | solution.py:117
  105.7 2.1 %fusion.16 = f32[384,1024]{1,0:T(8,128)} fusion(bf16[384,1024]{1,0:T(8,128)(2,1)S(1)} %pad_maximum_fusion, bf16[1,1024,1024]{2,1,0:T(8,128)(2,1)S(1)} %copy-done), kind=kOutput, calls=%fused_computation.16 | convolution fusion | flops 805306368 | bytes 4456448 | tf_op jit(solution)/shard_map/dot_general | solution.py:95
  107.8 5.7 %fusion.28 = bf16[384,1024]{1,0:T(8,128)(2,1)} fusion(bf16[1,1024,1024]{2,1,0:T(8,128)(2,1)} %param.27, f32[384,1024]{1,0:T(8,128)} %fusion.16, bf16[384,1024]{1,0:T(8,128)(2,1)} %copy-done.6, bf16[1,1024,1024]{2,1,0:T(8,128)(2,1)} %param.26), kind=kOutput, calls=%fused_computation.30 | convolution fusion | flops 1613365248 | bytes 7340032 | tf_op jit(solution)/shard_map/dot_general | solution.py:98
  114.9 2.7 %collective-permute-start.10 = (bf16[192,1024]{1,0:T(8,128)(2,1)S(1)}, bf16[192,1024]{1,0:T(8,128)(2,1)S(1)}, u32[]{:S(2)}, u32[]{:S(2)}) collective-permute-start(bf16[192,1024]{1,0:T(8,128)(2,1)S(1)} %get-tuple-element.22), channel_id=1, source_target_pairs={{0,192},{64,0},{128,64},{192,128},{1,193},{65,1},{129,65},{193,129... | collective-permute-start | bytes 1179656 | tf_op jit(solution)/shard_map/ppermute | solution.py:120
  117.6 12.0 %collective-permute-done.8 = bf16[192,1024]{1,0:T(8,128)(2,1)S(1)} collective-permute-done((bf16[192,1024]{1,0:T(8,128)(2,1)S(1)}, bf16[192,1024]{1,0:T(8,128)(2,1)S(1)}, u32[]{:S(2)}, u32[]{:S(2)}) %collective-permute-start.8) | collective-permute-done | bytes 393248 | tf_op jit(solution)/shard_map/ppermute | solution.py:119
  129.5 2.7 %collective-permute-start.11 = (bf16[192,1024]{1,0:T(8,128)(2,1)S(1)}, bf16[192,1024]{1,0:T(8,128)(2,1)S(1)}, u32[]{:S(2)}, u32[]{:S(2)}) collective-permute-start(bf16[192,1024]{1,0:T(8,128)(2,1)S(1)} %collective-permute-done.10), channel_id=1, source_target_pairs={{0,192},{64,0},{128,64},{192,128},{1,193},{65,1},{129,65},{193,129... | collective-permute-start | bytes 1179656 | tf_op jit(solution)/shard_map/ppermute | solution.py:122
  132.2 5.9 %collective-permute-done.9 = bf16[192,1024]{1,0:T(8,128)(2,1)S(1)} collective-permute-done((bf16[192,1024]{1,0:T(8,128)(2,1)S(1)}, bf16[192,1024]{1,0:T(8,128)(2,1)S(1)}, u32[]{:S(2)}, u32[]{:S(2)}) %collective-permute-start.9) | collective-permute-done | bytes 393248 | tf_op jit(solution)/shard_map/ppermute | solution.py:122
  138.2 1.9 %add_convert_fusion = bf16[384,1024]{1,0:T(8,128)(2,1)S(1)} fusion(bf16[384,1024]{1,0:T(8,128)(2,1)} %collective-permute-done.7, f32[384,1024]{1,0:T(8,128)S(1)} %copy-done.4, bf16[384,1024]{1,0:T(8,128)(2,1)} %copy-done.5, bf16[192,1024]{1,0:T(8,128)(2,1)S(1)} %collective-permute-done.11, bf16[192,1024]{1,0:T(8,128)(2,1)S(1)} %collective-permute-done.9), kind=kLoop, calls=%fused_computation.24 | loop fusion | flops 3932160 | bytes 4718592 | tf_op jit(solution)/shard_map/convert_element_type | solution.py:125
  141.4 10.1 %all-to-all-start.1 = ((bf16[64,48,128]{2,1,0:T(8,128)(2,1)}), bf16[64,48,128]{2,1,0:T(8,128)(2,1)}, u32[]{:S(2)}, u32[]{:S(2)}) async-start(bf16[64,48,128]{2,1,0:T(8,128)(2,1)} %reshape.69), calls=%async_computation.1 | async-start | bytes 1572864 | tf_op jit(solution)/shard_map/all_to_all | solution.py:126
  151.8 22.7 %all-to-all-done.1 = bf16[64,48,128]{2,1,0:T(8,128)(2,1)} async-done(((bf16[64,48,128]{2,1,0:T(8,128)(2,1)}), bf16[64,48,128]{2,1,0:T(8,128)(2,1)}, u32[]{:S(2)}, u32[]{:S(2)}) %all-to-all-start.1) | async-done | bytes 786464 | tf_op jit(solution)/shard_map/all_to_all | solution.py:126
  (85 shorter events, 21.0 us)
Async XLA Ops:
  0.0 61.2 %copy-start = (bf16[1,1024,1024]{2,1,0:T(8,128)(2,1)S(1)}, bf16[1,1024,1024]{2,1,0:T(8,128)(2,1)}, u32[]{:S(2)}) copy-start(bf16[1,1024,1024]{2,1,0:T(8,128)(2,1)} %param.25) | copy-start | bytes 6291460
  3.1 3.1 %copy-start.11 = (f32[128]{0:T(128)}, f32[128]{0:T(128)S(1)}, u32[]{:S(2)}) copy-start(f32[128]{0:T(128)S(1)} %compare_convert_fusion) | copy-start | bytes 1540
  3.1 9.0 %copy-start.8 = (f32[31,1024]{1,0:T(8,128)S(1)}, f32[31,1024]{1,0:T(8,128)}, u32[]{:S(2)}) copy-start(f32[31,1024]{1,0:T(8,128)} %param.19) | copy-start | bytes 380932
  6.2 6.0 %copy-start.10 = (s32[1,128,2]{1,2,0:T(2,128)S(1)}, s32[1,128,2]{1,2,0:T(2,128)}, u32[]{:S(2)}) copy-start(s32[1,128,2]{1,2,0:T(2,128)} %param.16) | copy-start | bytes 3076
  6.4 7.8 %collective-permute-start = (bf16[15,1024]{1,0:T(8,128)(2,1)S(1)}, bf16[15,1024]{1,0:T(8,128)(2,1)S(1)}, u32[]{:S(2)}, u32[]{:S(2)}) collective-permute-start(bf16[15,1024]{1,0:T(8,128)(2,1)S(1)} %get-tuple-element.25), channel_id=1, source_target_pairs={{0,8},{8,16},{16,24},{24,32},{32,40},{40,48},{48,56},{1,9},{9,17},... | collective-permute-start | bytes 92168 | tf_op jit(solution)/shard_map/ppermute | solution.py:45
  10.8 4.8 %collective-permute-start.1 = (bf16[15,1024]{1,0:T(8,128)(2,1)S(1)}, bf16[15,1024]{1,0:T(8,128)(2,1)S(1)}, u32[]{:S(2)}, u32[]{:S(2)}) collective-permute-start(bf16[15,1024]{1,0:T(8,128)(2,1)S(1)} %get-tuple-element.26), channel_id=1, source_target_pairs={{8,0},{16,8},{24,16},{32,24},{40,32},{48,40},{56,48},{9,1},{17,9},... | collective-permute-start | bytes 92168 | tf_op jit(solution)/shard_map/ppermute | solution.py:46
  12.7 3.3 %copy-start.13 = (bf16[1024,1024]{1,0:T(8,128)(2,1)S(1)}, bf16[1024,1024]{1,0:T(8,128)(2,1)}, u32[]{:S(2)}) copy-start(bf16[1024,1024]{1,0:T(8,128)(2,1)} %param.22) | copy-start | bytes 6291460
  58.4 19.0 %collective-permute-start.3 = (bf16[384,1024]{1,0:T(8,128)(2,1)S(1)}, bf16[384,1024]{1,0:T(8,128)(2,1)}, u32[]{:S(2)}, u32[]{:S(2)}) collective-permute-start(bf16[384,1024]{1,0:T(8,128)(2,1)S(1)} %reshape.68), channel_id=1, source_target_pairs={{0,192},{64,0},{128,64},{192,128},{1,193},{65,1},{129,65},{193,129... | collective-permute-start | bytes 2359304 | tf_op jit(solution)/shard_map/ppermute | solution.py:107
  61.2 19.4 %collective-permute-start.2 = (bf16[384,1024]{1,0:T(8,128)(2,1)S(1)}, bf16[384,1024]{1,0:T(8,128)(2,1)}, u32[]{:S(2)}, u32[]{:S(2)}) collective-permute-start(bf16[384,1024]{1,0:T(8,128)(2,1)S(1)} %reshape.68), channel_id=1, source_target_pairs={{0,64},{64,128},{128,192},{192,0},{1,65},{65,129},{129,193},{193,1... | collective-permute-start | bytes 2359304 | tf_op jit(solution)/shard_map/ppermute | solution.py:106
  81.6 5.1 %copy-start.14 = (bf16[1,1024,1024]{2,1,0:T(8,128)(2,1)S(1)}, bf16[1,1024,1024]{2,1,0:T(8,128)(2,1)}, u32[]{:S(2)}) copy-start(bf16[1,1024,1024]{2,1,0:T(8,128)(2,1)} %param.26) | copy-start | bytes 6291460
  90.0 11.7 %collective-permute-start.5 = (bf16[192,1024]{1,0:T(8,128)(2,1)S(1)}, bf16[192,1024]{1,0:T(8,128)(2,1)}, u32[]{:S(2)}, u32[]{:S(2)}) collective-permute-start(bf16[192,1024]{1,0:T(8,128)(2,1)S(1)} %slice.623), channel_id=1, source_target_pairs={{0,192},{64,0},{128,64},{192,128},{1,193},{65,1},{129,65},{193,129... | collective-permute-start | bytes 1179656 | tf_op jit(solution)/shard_map/ppermute | solution.py:111
  90.3 11.4 %collective-permute-start.4 = (bf16[192,1024]{1,0:T(8,128)(2,1)S(1)}, bf16[192,1024]{1,0:T(8,128)(2,1)}, u32[]{:S(2)}, u32[]{:S(2)}) collective-permute-start(bf16[192,1024]{1,0:T(8,128)(2,1)S(1)} %slice.622), channel_id=1, source_target_pairs={{0,64},{64,128},{128,192},{192,0},{1,65},{65,129},{129,193},{193,1... | collective-permute-start | bytes 1179656 | tf_op jit(solution)/shard_map/ppermute | solution.py:111
  102.9 29.3 %collective-permute-start.6 = (bf16[384,1024]{1,0:T(8,128)(2,1)}, bf16[384,1024]{1,0:T(8,128)(2,1)S(1)}, u32[]{:S(2)}, u32[]{:S(2)}) collective-permute-start(bf16[384,1024]{1,0:T(8,128)(2,1)} %fusion.2), channel_id=1, source_target_pairs={{0,64},{64,128},{128,192},{192,0},{1,65},{65,129},{129,193},{193,1... | collective-permute-start | bytes 2359304 | tf_op jit(solution)/shard_map/ppermute | solution.py:116
  103.0 29.2 %collective-permute-start.7 = (bf16[384,1024]{1,0:T(8,128)(2,1)}, bf16[384,1024]{1,0:T(8,128)(2,1)}, u32[]{:S(2)}, u32[]{:S(2)}) collective-permute-start(bf16[384,1024]{1,0:T(8,128)(2,1)} %fusion.4), channel_id=1, source_target_pairs={{0,192},{64,0},{128,64},{192,128},{1,193},{65,1},{129,65},{193,129... | collective-permute-start | bytes 2359304 | tf_op jit(solution)/shard_map/ppermute | solution.py:117
  113.5 24.7 %copy-start.4 = (f32[384,1024]{1,0:T(8,128)S(1)}, f32[384,1024]{1,0:T(8,128)}, u32[]{:S(2)}) copy-start(f32[384,1024]{1,0:T(8,128)} %fusion.6) | copy-start | bytes 4718596
  114.8 14.7 %collective-permute-start.8 = (bf16[192,1024]{1,0:T(8,128)(2,1)S(1)}, bf16[192,1024]{1,0:T(8,128)(2,1)S(1)}, u32[]{:S(2)}, u32[]{:S(2)}) collective-permute-start(bf16[192,1024]{1,0:T(8,128)(2,1)S(1)} %get-tuple-element.21), channel_id=1, source_target_pairs={{0,64},{64,128},{128,192},{192,0},{1,65},{65,129},{129,193},{193,1... | collective-permute-start | bytes 1179656 | tf_op jit(solution)/shard_map/ppermute | solution.py:119
  114.9 14.6 %collective-permute-start.10 = (bf16[192,1024]{1,0:T(8,128)(2,1)S(1)}, bf16[192,1024]{1,0:T(8,128)(2,1)S(1)}, u32[]{:S(2)}, u32[]{:S(2)}) collective-permute-start(bf16[192,1024]{1,0:T(8,128)(2,1)S(1)} %get-tuple-element.22), channel_id=1, source_target_pairs={{0,192},{64,0},{128,64},{192,128},{1,193},{65,1},{129,65},{193,129... | collective-permute-start | bytes 1179656 | tf_op jit(solution)/shard_map/ppermute | solution.py:120
  129.5 8.6 %collective-permute-start.9 = (bf16[192,1024]{1,0:T(8,128)(2,1)S(1)}, bf16[192,1024]{1,0:T(8,128)(2,1)S(1)}, u32[]{:S(2)}, u32[]{:S(2)}) collective-permute-start(bf16[192,1024]{1,0:T(8,128)(2,1)S(1)} %collective-permute-done.8), channel_id=1, source_target_pairs={{0,64},{64,128},{128,192},{192,0},{1,65},{65,129},{129,193},{193,1... | collective-permute-start | bytes 1179656 | tf_op jit(solution)/shard_map/ppermute | solution.py:122
  129.5 8.6 %collective-permute-start.11 = (bf16[192,1024]{1,0:T(8,128)(2,1)S(1)}, bf16[192,1024]{1,0:T(8,128)(2,1)S(1)}, u32[]{:S(2)}, u32[]{:S(2)}) collective-permute-start(bf16[192,1024]{1,0:T(8,128)(2,1)S(1)} %collective-permute-done.10), channel_id=1, source_target_pairs={{0,192},{64,0},{128,64},{192,128},{1,193},{65,1},{129,65},{193,129... | collective-permute-start | bytes 1179656 | tf_op jit(solution)/shard_map/ppermute | solution.py:122
  132.2 5.9 %copy-start.5 = (bf16[384,1024]{1,0:T(8,128)(2,1)}, bf16[384,1024]{1,0:T(8,128)(2,1)S(1)}, u32[]{:S(2)}) copy-start(bf16[384,1024]{1,0:T(8,128)(2,1)S(1)} %collective-permute-done.6) | copy-start | bytes 2359300
  140.1 11.4 %copy-start.7 = (bf16[1024,64]{0,1:T(8,128)(2,1)S(1)}, bf16[1024,64]{0,1:T(8,128)(2,1)}, u32[]{:S(2)}) copy-start(bf16[1024,64]{0,1:T(8,128)(2,1)} %param.24) | copy-start | bytes 393220
  141.4 10.1 %copy-start.2 = (bf16[128,1024]{1,0:T(8,128)(2,1)S(1)}, bf16[128,1024]{1,0:T(8,128)(2,1)}, u32[]{:S(2)}) copy-start(bf16[128,1024]{1,0:T(8,128)(2,1)} %copy-done.1) | copy-start | bytes 786436
  141.4 33.0 %all-to-all-start.1 = ((bf16[64,48,128]{2,1,0:T(8,128)(2,1)}), bf16[64,48,128]{2,1,0:T(8,128)(2,1)}, u32[]{:S(2)}, u32[]{:S(2)}) async-start(bf16[64,48,128]{2,1,0:T(8,128)(2,1)} %reshape.69), calls=%async_computation.1 | async-start | bytes 1572864 | tf_op jit(solution)/shard_map/all_to_all | solution.py:126
  151.8 24.5 %copy-start.12 = (f32[128]{0:T(128)S(1)}, f32[128]{0:T(128)}, u32[]{:S(2)}) copy-start(f32[128]{0:T(128)} %copy-done.11) | copy-start | bytes 1540
  (6 other events, 9.8 us)

commit v6 on v5

--- a/solution.py
+++ b/solution.py
@@ -103,13 +103,17 @@
     up = [(i, (i + 1) % size) for i in range(size)]
     down = [(i, (i - 1) % size) for i in range(size)]
     half = own_rows.shape[0] // 2
-    from_below = lax.ppermute(own_rows, "dp", up)
-    from_above = lax.ppermute(own_rows, "dp", down)
+    below_first = lax.ppermute(own_rows[:half], "dp", up)
+    above_second = lax.ppermute(own_rows[half:], "dp", down)
+    below_second = lax.ppermute(own_rows[half:], "dp", up)
+    above_first = lax.ppermute(own_rows[:half], "dp", down)
     for_own = serve(own_rows)
-    for_own, from_below, from_above = lax.optimization_barrier((for_own, from_below, from_above))
+    for_own, below_first, above_second = lax.optimization_barrier((for_own, below_first, above_second))
     far_rows = jnp.concatenate(
-        [lax.ppermute(from_below[:half], "dp", up), lax.ppermute(from_above[half:], "dp", down)], axis=0
+        [lax.ppermute(below_first, "dp", up), lax.ppermute(above_second, "dp", down)], axis=0
     )
+    from_below = jnp.concatenate([below_first, below_second], axis=0)
+    from_above = jnp.concatenate([above_first, above_second], axis=0)
     for_below = serve(from_below)
     for_above = serve(from_above)
     far_rows, for_below, for_above = lax.optimization_barrier((far_rows, for_below, for_above))

time: 178 us -> 179 us (level)
  waiting for transfers between devices: 53.3 us -> 44.5 us
  local copies, waits for them, and re-layouts: 9.91 us -> 17.8 us
  starting transfers between devices: 28.2 us -> 32.2 us
    ppermute x4 -> x6, waiting for transfers between devices: 11.6 us -> 1.63 us  [the longest x1 1.61 us: local(): above_second = lax.ppermute(own_rows[half:], 'dp', down)]
    unnamed x34 -> x40, local copies, waits for them, and re-layouts: 0.78 us -> 5.36 us
    ppermute x4 -> x6, starting transfers between devices: 4.28 us -> 8.83 us  [the longest x1 2.74 us: local(): above_first = lax.ppermute(own_rows[:half], 'dp', down)]
    slice x2 -> x3, local copies, waits for them, and re-layouts: 2.04 us -> 4.76 us  [the longest x2 2.85 us: local(): above_second = lax.ppermute(own_rows[half:], 'dp', down)]
  transfers between devices with their start and end apart: 13 -> 15, of which waited for: 6 -> 5; matrix products, arithmetic and copies ran while one was open for 17% -> 25% of each run, Pallas kernels for 0% -> 0%
where the time goes in v6:
time: 179 us; the launch traced here: 178 us
  waiting for transfers between devices  44.5 us (25%)
  matrix products  39 us (22%)
  blocking collectives  36.5 us (20%)
  starting transfers between devices  32.2 us (18%)
  local copies, waits for them, and re-layouts  17.8 us (10%)
  other arithmetic  7.13 us (4%)
    all_to_all x1, blocking collectives, local(): lax.all_to_all(outgoing, ('seq', 'expert'), split_axis=0, concat_axis=0,...  36.5 us
    all_to_all x1, waiting for transfers between devices, local(): lax.all_to_all(served, ('seq', 'expert'), split_axis=0, concat_axis=0, ti...  22.7 us
    dot_general x4, matrix products, serve(): lax.dot_general(hidden, down_local, (((1,), (1,)), ((), ())), preferred_e...  21.7 us
    ppermute x1, waiting for transfers between devices, local(): hop_up = lax.ppermute(for_far[:half], 'dp', up)  12.5 us
    all_to_all x1, starting transfers between devices, local(): lax.all_to_all(served, ('seq', 'expert'), split_axis=0, concat_axis=0, ti...  9.53 us
    ppermute x1, waiting for transfers between devices, local(): lax.ppermute(hop_up, 'dp', up)  6.5 us
    dot_general x2, matrix products, serve(): up_part = jnp.dot(rows, up_local, preferred_element_type=jnp.float32)  6.07 us
    dot_general x2, matrix products, serve(): gate_part = jnp.dot(rows, gate_local, preferred_element_type=jnp.float32)  5.43 us
  transfers between devices with their start and end apart: 15, of which 5 were waited for; matrix products, arithmetic and copies ran while one was open for 25% of the time, Pallas kernels for 0%

profile of v6, /device:TPU:1, one launch (start us, length us, event | category | flops | bytes accessed | tf_op | source)
XLA Modules:
  0.0 178.3 jit_solution(2708635667075136933)
XLA Ops:
  3.1 3.1 %fusion.65 = f32[128,2048]{1,0:T(8,128)S(1)} fusion(bf16[1024,2048]{1,0:T(8,128)(2,1)} %param.18, bf16[1,128,1024]{2,1,0:T(8,128)(2,1)} %param.14, f32[1024]{0:T(1024)} %param.17, f32[128]{0:T(128)S(1)} %add_rsqrt_fusion.1, f32[128]{0:T(128)S(1)} %broadcast_multiply_fusion.1), kind=kOutput, calls=%fused_computation.91 | convolution fusion | flops 537526272 | bytes 5510144 | tf_op jit(solution)/shard_map/dot_general | solution.py:36
  6.4 4.4 %collective-permute-start = (bf16[15,1024]{1,0:T(8,128)(2,1)S(1)}, bf16[15,1024]{1,0:T(8,128)(2,1)S(1)}, u32[]{:S(2)}, u32[]{:S(2)}) collective-permute-start(bf16[15,1024]{1,0:T(8,128)(2,1)S(1)} %get-tuple-element.27), channel_id=1, source_target_pairs={{0,8},{8,16},{16,24},{24,32},{32,40},{40,48},{48,56},{1,9},{9,17},... | collective-permute-start | bytes 92168 | tf_op jit(solution)/shard_map/ppermute | solution.py:45
  19.4 36.5 %all_to_all.10 = bf16[64,48,128]{2,1,0:T(8,128)(2,1)S(1)} all-to-all(bf16[64,48,128]{2,1,0:T(8,128)(2,1)} %reshape.69), channel_id=1, replica_groups=mesh['dp'=4,'seq'=8,'expert'=8] {'seq','expert'}, dimensions={0} | all-to-all | bytes 1572864 | tf_op jit(solution)/shard_map/all_to_all | solution.py:90
  58.7 2.7 %collective-permute-start.7 = (bf16[192,1024]{1,0:T(8,128)(2,1)}, bf16[192,1024]{1,0:T(8,128)(2,1)}, u32[]{:S(2)}, u32[]{:S(2)}) collective-permute-start(bf16[192,1024]{1,0:T(8,128)(2,1)} %slice.631), channel_id=1, source_target_pairs={{0,192},{64,0},{128,64},{192,128},{1,193},{65,1},{129,65},{193,129... | collective-permute-start | bytes 1179656 | tf_op jit(solution)/shard_map/ppermute | solution.py:109
  61.5 1.9 %slice.633 = bf16[192,1024]{1,0:T(8,128)(2,1)} reshape(bf16[32,48,128]{2,1,0:T(8,128)(2,1)} %get-tuple-element.23) | data formatting | bytes 786432 | tf_op jit(solution)/shard_map/slice | solution.py:107
  63.4 2.7 %collective-permute-start.3 = (bf16[192,1024]{1,0:T(8,128)(2,1)}, bf16[192,1024]{1,0:T(8,128)(2,1)}, u32[]{:S(2)}, u32[]{:S(2)}) collective-permute-start(bf16[192,1024]{1,0:T(8,128)(2,1)} %slice.633), channel_id=1, source_target_pairs={{0,192},{64,0},{128,64},{192,128},{1,193},{65,1},{129,65},{193,129... | collective-permute-start | bytes 1179656 | tf_op jit(solution)/shard_map/ppermute | solution.py:107
  67.3 3.3 %fusion.22 = f32[384,1024]{1,0:T(8,128)} fusion(bf16[384,1024]{1,0:T(8,128)(2,1)} %reshape.70, bf16[1,1024,1024]{2,1,0:T(8,128)(2,1)S(1)} %copy-done), kind=kOutput, calls=%fused_computation.22 | convolution fusion | flops 805306368 | bytes 4456448 | tf_op jit(solution)/shard_map/dot_general | solution.py:95
  70.6 5.8 %fusion.6 = f32[384,1024]{1,0:T(8,128)} fusion(bf16[1,1024,1024]{2,1,0:T(8,128)(2,1)} %param.27, f32[384,1024]{1,0:T(8,128)} %fusion.22, bf16[384,1024]{1,0:T(8,128)(2,1)S(1)} %copy-done.7, bf16[1,1024,1024]{2,1,0:T(8,128)(2,1)} %param.26), kind=kOutput, calls=%fused_computation.6 | convolution fusion | flops 1612972032 | bytes 8126464 | tf_op jit(solution)/shard_map/dot_general | solution.py:98
  78.8 2.7 %collective-permute-start.5 = (bf16[192,1024]{1,0:T(8,128)(2,1)}, bf16[192,1024]{1,0:T(8,128)(2,1)S(1)}, u32[]{:S(2)}, u32[]{:S(2)}) collective-permute-start(bf16[192,1024]{1,0:T(8,128)(2,1)} %collective-permute-done.3), channel_id=1, source_target_pairs={{0,192},{64,0},{128,64},{192,128},{1,193},{65,1},{129,65},{193,129... | collective-permute-start | bytes 1179656 | tf_op jit(solution)/shard_map/ppermute | solution.py:113
  83.2 1.9 %constant_dynamic-update-slice_fusion.1 = (bf16[384,1024]{1,0:T(8,128)(2,1)S(1)}, bf16[384,1024]{1,0:T(8,128)(2,1)}) fusion(bf16[192,1024]{1,0:T(8,128)(2,1)} %collective-permute-done.2, bf16[384,1024]{1,0:T(8,128)(2,1)} %constant_dynamic-update-slice_fusion.3, bf16[192,1024]{1,0:T(8,128)(2,1)} %collective-permute-done.3), kind=kLoop, calls=%fused_computation.175 | loop fusion | bytes 1572864
  87.0 2.1 %fusion.12 = f32[384,1024]{1,0:T(8,128)} fusion(bf16[384,1024]{1,0:T(8,128)(2,1)S(1)} %constant_dynamic-update-slice_fusion, bf16[1,1024,1024]{2,1,0:T(8,128)(2,1)S(1)} %copy-done.16), kind=kOutput, calls=%fused_computation.12 | convolution fusion | flops 805306368 | bytes 4456448 | tf_op jit(solution)/shard_map/dot_general | solution.py:96
  89.1 5.1 %fusion.4 = bf16[384,1024]{1,0:T(8,128)(2,1)} fusion(bf16[1,1024,1024]{2,1,0:T(8,128)(2,1)} %param.27, f32[384,1024]{1,0:T(8,128)} %fusion.12, bf16[384,1024]{1,0:T(8,128)(2,1)} %copy-done.8, bf16[1,1024,1024]{2,1,0:T(8,128)(2,1)S(1)} %copy-done), kind=kOutput, calls=%fused_computation.4 | convolution fusion | flops 1612972032 | bytes 7340032 | tf_op jit(solution)/shard_map/dot_general | solution.py:98
  94.2 4.0 %fusion.10 = f32[384,1024]{1,0:T(8,128)} fusion(bf16[384,1024]{1,0:T(8,128)(2,1)} %get-tuple-element.69, bf16[1,1024,1024]{2,1,0:T(8,128)(2,1)} %param.26), kind=kOutput, calls=%fused_computation.10 | convolution fusion | flops 805306368 | bytes 4456448 | tf_op jit(solution)/shard_map/dot_general | solution.py:96
  98.2 5.1 %fusion.2 = bf16[384,1024]{1,0:T(8,128)(2,1)} fusion(bf16[1,1024,1024]{2,1,0:T(8,128)(2,1)} %param.27, f32[384,1024]{1,0:T(8,128)} %fusion.10, bf16[384,1024]{1,0:T(8,128)(2,1)} %get-tuple-element.69, bf16[1,1024,1024]{2,1,0:T(8,128)(2,1)S(1)} %copy-done), kind=kOutput, calls=%fused_computation.2 | convolution fusion | flops 1612972032 | bytes 7340032 | tf_op jit(solution)/shard_map/dot_general | solution.py:98
  103.5 2.7 %collective-permute-start.9 = (bf16[384,1024]{1,0:T(8,128)(2,1)}, bf16[384,1024]{1,0:T(8,128)(2,1)}, u32[]{:S(2)}, u32[]{:S(2)}) collective-permute-start(bf16[384,1024]{1,0:T(8,128)(2,1)} %fusion.4), channel_id=1, source_target_pairs={{0,192},{64,0},{128,64},{192,128},{1,193},{65,1},{129,65},{193,129... | collective-permute-start | bytes 2359304 | tf_op jit(solution)/shard_map/ppermute | solution.py:121
  106.1 2.1 %fusion.16 = f32[384,1024]{1,0:T(8,128)} fusion(bf16[384,1024]{1,0:T(8,128)(2,1)S(1)} %pad_maximum_fusion, bf16[1,1024,1024]{2,1,0:T(8,128)(2,1)S(1)} %copy-done), kind=kOutput, calls=%fused_computation.16 | convolution fusion | flops 805306368 | bytes 4456448 | tf_op jit(solution)/shard_map/dot_general | solution.py:95
  108.2 5.7 %fusion.28 = bf16[384,1024]{1,0:T(8,128)(2,1)} fusion(bf16[1,1024,1024]{2,1,0:T(8,128)(2,1)} %param.27, f32[384,1024]{1,0:T(8,128)} %fusion.16, bf16[384,1024]{1,0:T(8,128)(2,1)} %copy-done.6, bf16[1,1024,1024]{2,1,0:T(8,128)(2,1)} %param.26), kind=kOutput, calls=%fused_computation.30 | convolution fusion | flops 1613365248 | bytes 7340032 | tf_op jit(solution)/shard_map/dot_general | solution.py:98
  115.3 2.7 %collective-permute-start.12 = (bf16[192,1024]{1,0:T(8,128)(2,1)S(1)}, bf16[192,1024]{1,0:T(8,128)(2,1)S(1)}, u32[]{:S(2)}, u32[]{:S(2)}) collective-permute-start(bf16[192,1024]{1,0:T(8,128)(2,1)S(1)} %get-tuple-element.22), channel_id=1, source_target_pairs={{0,192},{64,0},{128,64},{192,128},{1,193},{65,1},{129,65},{193,129... | collective-permute-start | bytes 1179656 | tf_op jit(solution)/shard_map/ppermute | solution.py:124
  118.0 12.5 %collective-permute-done.10 = bf16[192,1024]{1,0:T(8,128)(2,1)S(1)} collective-permute-done((bf16[192,1024]{1,0:T(8,128)(2,1)S(1)}, bf16[192,1024]{1,0:T(8,128)(2,1)S(1)}, u32[]{:S(2)}, u32[]{:S(2)}) %collective-permute-start.10) | collective-permute-done | bytes 393248 | tf_op jit(solution)/shard_map/ppermute | solution.py:123
  130.6 2.7 %collective-permute-start.13 = (bf16[192,1024]{1,0:T(8,128)(2,1)S(1)}, bf16[192,1024]{1,0:T(8,128)(2,1)S(1)}, u32[]{:S(2)}, u32[]{:S(2)}) collective-permute-start(bf16[192,1024]{1,0:T(8,128)(2,1)S(1)} %collective-permute-done.12), channel_id=1, source_target_pairs={{0,192},{64,0},{128,64},{192,128},{1,193},{65,1},{129,65},{193,129... | collective-permute-start | bytes 1179656 | tf_op jit(solution)/shard_map/ppermute | solution.py:126
  133.2 6.5 %collective-permute-done.11 = bf16[192,1024]{1,0:T(8,128)(2,1)S(1)} collective-permute-done((bf16[192,1024]{1,0:T(8,128)(2,1)S(1)}, bf16[192,1024]{1,0:T(8,128)(2,1)S(1)}, u32[]{:S(2)}, u32[]{:S(2)}) %collective-permute-start.11) | collective-permute-done | bytes 393248 | tf_op jit(solution)/shard_map/ppermute | solution.py:126
  139.8 1.9 %add_convert_fusion = bf16[384,1024]{1,0:T(8,128)(2,1)S(1)} fusion(bf16[384,1024]{1,0:T(8,128)(2,1)} %collective-permute-done.9, f32[384,1024]{1,0:T(8,128)S(1)} %copy-done.4, bf16[384,1024]{1,0:T(8,128)(2,1)} %copy-done.5, bf16[192,1024]{1,0:T(8,128)(2,1)S(1)} %collective-permute-done.13, bf16[192,1024]{1,0:T(8,128)(2,1)S(1)} %collective-permute-done.11), kind=kLoop, calls=%fused_computation.24 | loop fusion | flops 3932160 | bytes 4718592 | tf_op jit(solution)/shard_map/convert_element_type | solution.py:129
  143.0 9.5 %all-to-all-start.1 = ((bf16[64,48,128]{2,1,0:T(8,128)(2,1)}), bf16[64,48,128]{2,1,0:T(8,128)(2,1)}, u32[]{:S(2)}, u32[]{:S(2)}) async-start(bf16[64,48,128]{2,1,0:T(8,128)(2,1)} %reshape.71), calls=%async_computation.1 | async-start | bytes 1572864 | tf_op jit(solution)/shard_map/all_to_all | solution.py:130
  152.8 22.7 %all-to-all-done.1 = bf16[64,48,128]{2,1,0:T(8,128)(2,1)} async-done(((bf16[64,48,128]{2,1,0:T(8,128)(2,1)}), bf16[64,48,128]{2,1,0:T(8,128)(2,1)}, u32[]{:S(2)}, u32[]{:S(2)}) %all-to-all-start.1) | async-done | bytes 786464 | tf_op jit(solution)/shard_map/all_to_all | solution.py:130
  (97 shorter events, 26.9 us)
Async XLA Ops:
  0.0 67.3 %copy-start = (bf16[1,1024,1024]{2,1,0:T(8,128)(2,1)S(1)}, bf16[1,1024,1024]{2,1,0:T(8,128)(2,1)}, u32[]{:S(2)}) copy-start(bf16[1,1024,1024]{2,1,0:T(8,128)(2,1)} %param.25) | copy-start | bytes 6291460
  3.1 9.0 %copy-start.10 = (f32[31,1024]{1,0:T(8,128)S(1)}, f32[31,1024]{1,0:T(8,128)}, u32[]{:S(2)}) copy-start(f32[31,1024]{1,0:T(8,128)} %param.19) | copy-start | bytes 380932
  6.2 6.0 %copy-start.12 = (s32[1,128,2]{1,2,0:T(2,128)S(1)}, s32[1,128,2]{1,2,0:T(2,128)}, u32[]{:S(2)}) copy-start(s32[1,128,2]{1,2,0:T(2,128)} %param.16) | copy-start | bytes 3076
  6.4 7.8 %collective-permute-start = (bf16[15,1024]{1,0:T(8,128)(2,1)S(1)}, bf16[15,1024]{1,0:T(8,128)(2,1)S(1)}, u32[]{:S(2)}, u32[]{:S(2)}) collective-permute-start(bf16[15,1024]{1,0:T(8,128)(2,1)S(1)} %get-tuple-element.27), channel_id=1, source_target_pairs={{0,8},{8,16},{16,24},{24,32},{32,40},{40,48},{48,56},{1,9},{9,17},... | collective-permute-start | bytes 92168 | tf_op jit(solution)/shard_map/ppermute | solution.py:45
  10.8 4.8 %collective-permute-start.1 = (bf16[15,1024]{1,0:T(8,128)(2,1)S(1)}, bf16[15,1024]{1,0:T(8,128)(2,1)S(1)}, u32[]{:S(2)}, u32[]{:S(2)}) collective-permute-start(bf16[15,1024]{1,0:T(8,128)(2,1)S(1)} %get-tuple-element.28), channel_id=1, source_target_pairs={{8,0},{16,8},{24,16},{32,24},{40,32},{48,40},{56,48},{9,1},{17,9},... | collective-permute-start | bytes 92168 | tf_op jit(solution)/shard_map/ppermute | solution.py:46
  58.7 22.7 %collective-permute-start.7 = (bf16[192,1024]{1,0:T(8,128)(2,1)}, bf16[192,1024]{1,0:T(8,128)(2,1)}, u32[]{:S(2)}, u32[]{:S(2)}) collective-permute-start(bf16[192,1024]{1,0:T(8,128)(2,1)} %slice.631), channel_id=1, source_target_pairs={{0,192},{64,0},{128,64},{192,128},{1,193},{65,1},{129,65},{193,129... | collective-permute-start | bytes 1179656 | tf_op jit(solution)/shard_map/ppermute | solution.py:109
  61.5 14.9 %collective-permute-start.2 = (bf16[192,1024]{1,0:T(8,128)(2,1)}, bf16[192,1024]{1,0:T(8,128)(2,1)}, u32[]{:S(2)}, u32[]{:S(2)}) collective-permute-start(bf16[192,1024]{1,0:T(8,128)(2,1)} %slice.631), channel_id=1, source_target_pairs={{0,64},{64,128},{128,192},{192,0},{1,65},{65,129},{129,193},{193,1... | collective-permute-start | bytes 1179656 | tf_op jit(solution)/shard_map/ppermute | solution.py:106
  63.4 21.7 %collective-permute-start.6 = (bf16[192,1024]{1,0:T(8,128)(2,1)}, bf16[192,1024]{1,0:T(8,128)(2,1)}, u32[]{:S(2)}, u32[]{:S(2)}) collective-permute-start(bf16[192,1024]{1,0:T(8,128)(2,1)} %slice.633), channel_id=1, source_target_pairs={{0,64},{64,128},{128,192},{192,0},{1,65},{65,129},{129,193},{193,1... | collective-permute-start | bytes 1179656 | tf_op jit(solution)/shard_map/ppermute | solution.py:108
  63.4 14.6 %collective-permute-start.3 = (bf16[192,1024]{1,0:T(8,128)(2,1)}, bf16[192,1024]{1,0:T(8,128)(2,1)}, u32[]{:S(2)}, u32[]{:S(2)}) collective-permute-start(bf16[192,1024]{1,0:T(8,128)(2,1)} %slice.633), channel_id=1, source_target_pairs={{0,192},{64,0},{128,64},{192,128},{1,193},{65,1},{129,65},{193,129... | collective-permute-start | bytes 1179656 | tf_op jit(solution)/shard_map/ppermute | solution.py:107
  76.4 10.7 %copy-start.16 = (bf16[1,1024,1024]{2,1,0:T(8,128)(2,1)S(1)}, bf16[1,1024,1024]{2,1,0:T(8,128)(2,1)}, u32[]{:S(2)}) copy-start(bf16[1,1024,1024]{2,1,0:T(8,128)(2,1)} %param.26) | copy-start | bytes 6291460
  78.0 25.3 %collective-permute-start.4 = (bf16[192,1024]{1,0:T(8,128)(2,1)}, bf16[192,1024]{1,0:T(8,128)(2,1)S(1)}, u32[]{:S(2)}, u32[]{:S(2)}) collective-permute-start(bf16[192,1024]{1,0:T(8,128)(2,1)} %collective-permute-done.2), channel_id=1, source_target_pairs={{0,64},{64,128},{128,192},{192,0},{1,65},{65,129},{129,193},{193,1... | collective-permute-start | bytes 1179656 | tf_op jit(solution)/shard_map/ppermute | solution.py:113
  78.8 24.5 %collective-permute-start.5 = (bf16[192,1024]{1,0:T(8,128)(2,1)}, bf16[192,1024]{1,0:T(8,128)(2,1)S(1)}, u32[]{:S(2)}, u32[]{:S(2)}) collective-permute-start(bf16[192,1024]{1,0:T(8,128)(2,1)} %collective-permute-done.3), channel_id=1, source_target_pairs={{0,192},{64,0},{128,64},{192,128},{1,193},{65,1},{129,65},{193,129... | collective-permute-start | bytes 1179656 | tf_op jit(solution)/shard_map/ppermute | solution.py:113
  103.4 29.9 %collective-permute-start.8 = (bf16[384,1024]{1,0:T(8,128)(2,1)}, bf16[384,1024]{1,0:T(8,128)(2,1)S(1)}, u32[]{:S(2)}, u32[]{:S(2)}) collective-permute-start(bf16[384,1024]{1,0:T(8,128)(2,1)} %fusion.2), channel_id=1, source_target_pairs={{0,64},{64,128},{128,192},{192,0},{1,65},{65,129},{129,193},{193,1... | collective-permute-start | bytes 2359304 | tf_op jit(solution)/shard_map/ppermute | solution.py:120
  103.5 29.8 %collective-permute-start.9 = (bf16[384,1024]{1,0:T(8,128)(2,1)}, bf16[384,1024]{1,0:T(8,128)(2,1)}, u32[]{:S(2)}, u32[]{:S(2)}) collective-permute-start(bf16[384,1024]{1,0:T(8,128)(2,1)} %fusion.4), channel_id=1, source_target_pairs={{0,192},{64,0},{128,64},{192,128},{1,193},{65,1},{129,65},{193,129... | collective-permute-start | bytes 2359304 | tf_op jit(solution)/shard_map/ppermute | solution.py:121
  114.0 25.8 %copy-start.4 = (f32[384,1024]{1,0:T(8,128)S(1)}, f32[384,1024]{1,0:T(8,128)}, u32[]{:S(2)}) copy-start(f32[384,1024]{1,0:T(8,128)} %fusion.6) | copy-start | bytes 4718596
  115.3 15.3 %collective-permute-start.10 = (bf16[192,1024]{1,0:T(8,128)(2,1)S(1)}, bf16[192,1024]{1,0:T(8,128)(2,1)S(1)}, u32[]{:S(2)}, u32[]{:S(2)}) collective-permute-start(bf16[192,1024]{1,0:T(8,128)(2,1)S(1)} %get-tuple-element.21), channel_id=1, source_target_pairs={{0,64},{64,128},{128,192},{192,0},{1,65},{65,129},{129,193},{193,1... | collective-permute-start | bytes 1179656 | tf_op jit(solution)/shard_map/ppermute | solution.py:123
  115.3 15.2 %collective-permute-start.12 = (bf16[192,1024]{1,0:T(8,128)(2,1)S(1)}, bf16[192,1024]{1,0:T(8,128)(2,1)S(1)}, u32[]{:S(2)}, u32[]{:S(2)}) collective-permute-start(bf16[192,1024]{1,0:T(8,128)(2,1)S(1)} %get-tuple-element.22), channel_id=1, source_target_pairs={{0,192},{64,0},{128,64},{192,128},{1,193},{65,1},{129,65},{193,129... | collective-permute-start | bytes 1179656 | tf_op jit(solution)/shard_map/ppermute | solution.py:124
  130.6 9.2 %collective-permute-start.11 = (bf16[192,1024]{1,0:T(8,128)(2,1)S(1)}, bf16[192,1024]{1,0:T(8,128)(2,1)S(1)}, u32[]{:S(2)}, u32[]{:S(2)}) collective-permute-start(bf16[192,1024]{1,0:T(8,128)(2,1)S(1)} %collective-permute-done.10), channel_id=1, source_target_pairs={{0,64},{64,128},{128,192},{192,0},{1,65},{65,129},{129,193},{193,1... | collective-permute-start | bytes 1179656 | tf_op jit(solution)/shard_map/ppermute | solution.py:126
  130.6 9.2 %collective-permute-start.13 = (bf16[192,1024]{1,0:T(8,128)(2,1)S(1)}, bf16[192,1024]{1,0:T(8,128)(2,1)S(1)}, u32[]{:S(2)}, u32[]{:S(2)}) collective-permute-start(bf16[192,1024]{1,0:T(8,128)(2,1)S(1)} %collective-permute-done.12), channel_id=1, source_target_pairs={{0,192},{64,0},{128,64},{192,128},{1,193},{65,1},{129,65},{193,129... | collective-permute-start | bytes 1179656 | tf_op jit(solution)/shard_map/ppermute | solution.py:126
  133.2 6.5 %copy-start.5 = (bf16[384,1024]{1,0:T(8,128)(2,1)}, bf16[384,1024]{1,0:T(8,128)(2,1)S(1)}, u32[]{:S(2)}) copy-start(bf16[384,1024]{1,0:T(8,128)(2,1)S(1)} %collective-permute-done.8) | copy-start | bytes 2359300
  141.7 10.8 %copy-start.9 = (bf16[1024,64]{0,1:T(8,128)(2,1)S(1)}, bf16[1024,64]{0,1:T(8,128)(2,1)}, u32[]{:S(2)}) copy-start(bf16[1024,64]{0,1:T(8,128)(2,1)} %param.24) | copy-start | bytes 393220
  143.0 9.6 %copy-start.2 = (bf16[128,1024]{1,0:T(8,128)(2,1)S(1)}, bf16[128,1024]{1,0:T(8,128)(2,1)}, u32[]{:S(2)}) copy-start(bf16[128,1024]{1,0:T(8,128)(2,1)} %copy-done.1) | copy-start | bytes 786436
  143.0 32.5 %all-to-all-start.1 = ((bf16[64,48,128]{2,1,0:T(8,128)(2,1)}), bf16[64,48,128]{2,1,0:T(8,128)(2,1)}, u32[]{:S(2)}, u32[]{:S(2)}) async-start(bf16[64,48,128]{2,1,0:T(8,128)(2,1)} %reshape.71), calls=%async_computation.1 | async-start | bytes 1572864 | tf_op jit(solution)/shard_map/all_to_all | solution.py:130
  152.7 24.5 %copy-start.14 = (f32[128]{0:T(128)S(1)}, f32[128]{0:T(128)}, u32[]{:S(2)}) copy-start(f32[128]{0:T(128)} %copy-done.13) | copy-start | bytes 1540
  (10 other events, 20.4 us)

commit v7 on v5

--- a/solution.py
+++ b/solution.py
@@ -30,20 +30,26 @@
     frame_rows = frames[0]
     token_count = frame_rows.shape[0]
     model_width = frame_rows.shape[1]
-    position = lax.axis_index("seq") * token_count + jnp.arange(token_count, dtype=jnp.int32)
-    frame_mask = (position < lengths[0]).astype(jnp.float32)[:, None]
-    conv_in = layer_norm(frame_rows, norm_conv).astype(jnp.bfloat16)
-    lifted = jnp.dot(conv_in, point_in, preferred_element_type=jnp.float32)
-    gated = (lifted[:, :model_width] * jax.nn.sigmoid(lifted[:, model_width:]) * frame_mask).astype(
-        jnp.bfloat16
-    )
     reach = depth_kernel.shape[0] // 2
     taps = depth_kernel.shape[0]
     seq_size = lax.axis_size("seq")
     seq_up = [(i, i + 1) for i in range(seq_size - 1)]
     seq_down = [(j, i) for i, j in seq_up]
-    before = lax.ppermute(gated[token_count - reach :], "seq", seq_up)
-    after = lax.ppermute(gated[:reach], "seq", seq_down)
+    before = lax.ppermute(frame_rows[token_count - reach :], "seq", seq_up)
+    after = lax.ppermute(frame_rows[:reach], "seq", seq_down)
+    position = lax.axis_index("seq") * token_count + jnp.arange(token_count, dtype=jnp.int32)
+    frame_mask = (position < lengths[0]).astype(jnp.float32)[:, None]
+    wide_position = lax.axis_index("seq") * token_count - reach + jnp.arange(
+        token_count + 2 * reach, dtype=jnp.int32
+    )
+    wide_mask = ((wide_position >= 0) & (wide_position < lengths[0])).astype(jnp.float32)[:, None]
+    own_in = layer_norm(frame_rows, norm_conv).astype(jnp.bfloat16)
+    edge_in = layer_norm(jnp.concatenate([before, after], axis=0), norm_conv).astype(jnp.bfloat16)
+    conv_in = jnp.concatenate([edge_in[:reach], own_in, edge_in[reach:]], axis=0)
+    lifted = jnp.dot(conv_in, point_in, preferred_element_type=jnp.float32)
+    gated = (lifted[:, :model_width] * jax.nn.sigmoid(lifted[:, model_width:]) * wide_mask).astype(
+        jnp.bfloat16
+    )
 
     def depthwise(rows, count):
         total = jnp.zeros((count, model_width), jnp.float32)
@@ -51,10 +57,7 @@
             total = total + rows[offset : offset + count].astype(jnp.float32) * depth_kernel[offset]
         return total
 
-    middle = depthwise(gated, token_count - 2 * reach)
-    head = depthwise(jnp.concatenate([before, gated[: 2 * reach]], axis=0), reach)
-    tail = depthwise(jnp.concatenate([gated[token_count - 2 * reach :], after], axis=0), reach)
-    depth = jnp.concatenate([head, middle, tail], axis=0)
+    depth = depthwise(gated, token_count)
     swished = jax.nn.silu(depth * bn_scale + bn_shift).astype(jnp.bfloat16)
     residual = frame_rows.astype(jnp.float32) + jnp.dot(
         swished, point_out, preferred_element_type=jnp.float32

time: 178 us -> 185 us (1.039)
  local copies, waits for them, and re-layouts: 9.91 us -> 14.7 us
  matrix products: 40 us -> 42.1 us
    slice x2, local copies, waits for them, and re-layouts: 0.1 us -> 2.53 us  [depthwise(): depth_kernel[offset]]
    add x3 -> x0, other arithmetic: 2.11 us -> none  [depthwise(): total + rows[offset:offset + count].astype(jnp.float32) * depth_kernel[of...]
    dot_general x1, matrix products: 0.62 us -> 2.59 us  [local(): jnp.dot(swished, point_out, preferred_element_type=jnp.float32)]
  transfers between devices with their start and end apart: 13 -> 13, of which waited for: 6 -> 5; matrix products, arithmetic and copies ran while one was open for 17% -> 19% of each run, Pallas kernels for 0% -> 0%
where the time goes in v7:
time: 185 us; the launch traced here: 184 us
  waiting for transfers between devices  51.6 us (28%)
  matrix products  42.1 us (23%)
  blocking collectives  37.3 us (20%)
  starting transfers between devices  28.2 us (15%)
  local copies, waits for them, and re-layouts  14.7 us (8%)
  other arithmetic  9.07 us (5%)
    all_to_all x1, blocking collectives, local(): lax.all_to_all(outgoing, ('seq', 'expert'), split_axis=0, concat_axis=0,...  37.3 us
    all_to_all x1, waiting for transfers between devices, local(): lax.all_to_all(served, ('seq', 'expert'), split_axis=0, concat_axis=0, ti...  22.1 us
    dot_general x4, matrix products, serve(): lax.dot_general(hidden, down_local, (((1,), (1,)), ((), ())), preferred_e...  21.6 us
    ppermute x1, waiting for transfers between devices, local(): hop_up = lax.ppermute(for_far[:half], 'dp', up)  12 us
    all_to_all x1, starting transfers between devices, local(): lax.all_to_all(served, ('seq', 'expert'), split_axis=0, concat_axis=0, ti...  10.1 us
    ppermute x1, waiting for transfers between devices, local(): from_above = lax.ppermute(own_rows, 'dp', down)  8.33 us
    dot_general x2, matrix products, serve(): up_part = jnp.dot(rows, up_local, preferred_element_type=jnp.float32)  7.38 us
    ppermute x1, waiting for transfers between devices, local(): lax.ppermute(hop_up, 'dp', up)  5.93 us
  transfers between devices with their start and end apart: 13, of which 5 were waited for; matrix products, arithmetic and copies ran while one was open for 19% of the time, Pallas kernels for 0%

profile of v7, /device:TPU:1, one launch (start us, length us, event | category | flops | bytes accessed | tf_op | source)
XLA Modules:
  0.0 183.9 jit_solution(2599882930090428931)
XLA Ops:
  1.0 4.4 %collective-permute-start = (bf16[15,1024]{1,0:T(8,128)(2,1)S(1)}, bf16[15,1024]{1,0:T(8,128)(2,1)S(1)}, u32[]{:S(2)}, u32[]{:S(2)}) collective-permute-start(bf16[15,1024]{1,0:T(8,128)(2,1)S(1)} %get-tuple-element.23), channel_id=1, source_target_pairs={{0,8},{8,16},{16,24},{24,32},{32,40},{40,48},{48,56},{1,9},{9,17},... | collective-permute-start | bytes 92168 | tf_op jit(solution)/shard_map/ppermute | solution.py:38
  15.7 3.2 %fusion.64 = f32[158,2048]{1,0:T(8,128)S(1)} fusion(bf16[1024,2048]{1,0:T(8,128)(2,1)} %param.18, bf16[15,1024]{1,0:T(8,128)(2,1)S(1)} %get-tuple-element.57, bf16[128,1024]{1,0:T(8,128)(2,1)S(1)} %fusion.63, bf16[15,1024]{1,0:T(8,128)(2,1)S(1)} %get-tuple-element.56), kind=kOutput, calls=%fused_computation.62 | convolution fusion | flops 663670784 | bytes 5812224 | tf_op jit(solution)/shard_map/dot_general | solution.py:49
  19.8 2.6 %fusion.100 = (f32[128]{0:T(128)S(1)}, f32[128,1024]{1,0:T(8,128)S(1)}) fusion(bf16[1024,1024]{1,0:T(8,128)(2,1)S(1)} %copy-done.11, bf16[158,1024]{1,0:T(8,128)(2,1)S(1)} %fusion.58, f32[1024]{0:T(1024)S(1)} %copy-done.13, f32[1024]{0:T(1024)S(1)} %copy-done.14, f32[1024]{0:T(1024)S(1)} %bitcast.143, f32[1024]{0:T(1024)S(1)} %bitcast.144, ...), kind=kOutput, calls=%fused_computation.124 | convolution fusion | flops 281804672 | bytes 11145728 | tf_op jit(solution)/shard_map/dot_general | solution.py:62
  26.3 37.3 %all_to_all.10 = bf16[64,48,128]{2,1,0:T(8,128)(2,1)} all-to-all(bf16[64,48,128]{2,1,0:T(8,128)(2,1)S(1)} %reshape.89), channel_id=1, replica_groups=mesh['dp'=4,'seq'=8,'expert'=8] {'seq','expert'}, dimensions={0} | all-to-all | bytes 1572864 | tf_op jit(solution)/shard_map/all_to_all | solution.py:93
  63.6 1.4 reshape.90
  65.0 2.8 %collective-permute-start.3 = (bf16[384,1024]{1,0:T(8,128)(2,1)S(1)}, bf16[384,1024]{1,0:T(8,128)(2,1)}, u32[]{:S(2)}, u32[]{:S(2)}) collective-permute-start(bf16[384,1024]{1,0:T(8,128)(2,1)S(1)} %reshape.90), channel_id=1, source_target_pairs={{0,192},{64,0},{128,64},{192,128},{1,193},{65,1},{129,65},{193,129... | collective-permute-start | bytes 2359304 | tf_op jit(solution)/shard_map/ppermute | solution.py:110
  67.8 2.1 %fusion.22 = f32[384,1024]{1,0:T(8,128)} fusion(bf16[384,1024]{1,0:T(8,128)(2,1)S(1)} %reshape.90, bf16[1,1024,1024]{2,1,0:T(8,128)(2,1)S(1)} %copy-done), kind=kOutput, calls=%fused_computation.22 | convolution fusion | flops 805306368 | bytes 4456448 | tf_op jit(solution)/shard_map/dot_general | solution.py:98
  70.0 5.7 %fusion.6 = f32[384,1024]{1,0:T(8,128)} fusion(bf16[1,1024,1024]{2,1,0:T(8,128)(2,1)} %param.27, f32[384,1024]{1,0:T(8,128)} %fusion.22, bf16[384,1024]{1,0:T(8,128)(2,1)S(1)} %reshape.90, bf16[1,1024,1024]{2,1,0:T(8,128)(2,1)} %param.26), kind=kOutput, calls=%fused_computation.6 | convolution fusion | flops 1612972032 | bytes 8126464 | tf_op jit(solution)/shard_map/dot_general | solution.py:101
  75.7 8.3 %collective-permute-done.3 = bf16[384,1024]{1,0:T(8,128)(2,1)} collective-permute-done((bf16[384,1024]{1,0:T(8,128)(2,1)S(1)}, bf16[384,1024]{1,0:T(8,128)(2,1)}, u32[]{:S(2)}, u32[]{:S(2)}) %collective-permute-start.3) | collective-permute-done | bytes 786464 | tf_op jit(solution)/shard_map/ppermute | solution.py:110
  84.0 3.2 %collective-permute-done.2 = bf16[384,1024]{1,0:T(8,128)(2,1)} collective-permute-done((bf16[384,1024]{1,0:T(8,128)(2,1)S(1)}, bf16[384,1024]{1,0:T(8,128)(2,1)}, u32[]{:S(2)}, u32[]{:S(2)}) %collective-permute-start.2) | collective-permute-done | bytes 786464 | tf_op jit(solution)/shard_map/ppermute | solution.py:109
  88.3 4.1 %fusion.12 = f32[384,1024]{1,0:T(8,128)} fusion(bf16[384,1024]{1,0:T(8,128)(2,1)} %collective-permute-done.2, bf16[1,1024,1024]{2,1,0:T(8,128)(2,1)} %param.26), kind=kOutput, calls=%fused_computation.12 | convolution fusion | flops 805306368 | bytes 4456448 | tf_op jit(solution)/shard_map/dot_general | solution.py:99
  93.4 3.3 %fusion.10 = f32[384,1024]{1,0:T(8,128)} fusion(bf16[384,1024]{1,0:T(8,128)(2,1)} %collective-permute-done.3, bf16[1,1024,1024]{2,1,0:T(8,128)(2,1)S(1)} %copy-done.12), kind=kOutput, calls=%fused_computation.10 | convolution fusion | flops 805306368 | bytes 4456448 | tf_op jit(solution)/shard_map/dot_general | solution.py:99
  98.2 5.1 %fusion.4 = bf16[384,1024]{1,0:T(8,128)(2,1)} fusion(bf16[1,1024,1024]{2,1,0:T(8,128)(2,1)} %param.27, f32[384,1024]{1,0:T(8,128)} %fusion.12, bf16[384,1024]{1,0:T(8,128)(2,1)} %collective-permute-done.2, bf16[1,1024,1024]{2,1,0:T(8,128)(2,1)S(1)} %copy-done), kind=kOutput, calls=%fused_computation.4 | convolution fusion | flops 1612972032 | bytes 7340032 | tf_op jit(solution)/shard_map/dot_general | solution.py:101
  103.3 5.1 %fusion.2 = bf16[384,1024]{1,0:T(8,128)(2,1)} fusion(bf16[1,1024,1024]{2,1,0:T(8,128)(2,1)} %param.27, f32[384,1024]{1,0:T(8,128)} %fusion.10, bf16[384,1024]{1,0:T(8,128)(2,1)} %collective-permute-done.3, bf16[1,1024,1024]{2,1,0:T(8,128)(2,1)S(1)} %copy-done), kind=kOutput, calls=%fused_computation.2 | convolution fusion | flops 1612972032 | bytes 7340032 | tf_op jit(solution)/shard_map/dot_general | solution.py:101
  109.7 2.7 %collective-permute-start.7 = (bf16[384,1024]{1,0:T(8,128)(2,1)}, bf16[384,1024]{1,0:T(8,128)(2,1)S(1)}, u32[]{:S(2)}, u32[]{:S(2)}) collective-permute-start(bf16[384,1024]{1,0:T(8,128)(2,1)} %fusion.4), channel_id=1, source_target_pairs={{0,192},{64,0},{128,64},{192,128},{1,193},{65,1},{129,65},{193,129... | collective-permute-start | bytes 2359304 | tf_op jit(solution)/shard_map/ppermute | solution.py:120
  112.3 2.1 %fusion.16 = f32[384,1024]{1,0:T(8,128)} fusion(bf16[384,1024]{1,0:T(8,128)(2,1)S(1)} %pad_maximum_fusion, bf16[1,1024,1024]{2,1,0:T(8,128)(2,1)S(1)} %copy-done), kind=kOutput, calls=%fused_computation.16 | convolution fusion | flops 805306368 | bytes 4456448 | tf_op jit(solution)/shard_map/dot_general | solution.py:98
  114.5 5.7 %fusion.28 = bf16[384,1024]{1,0:T(8,128)(2,1)} fusion(bf16[1,1024,1024]{2,1,0:T(8,128)(2,1)} %param.27, f32[384,1024]{1,0:T(8,128)} %fusion.16, bf16[384,1024]{1,0:T(8,128)(2,1)} %copy-done.6, bf16[1,1024,1024]{2,1,0:T(8,128)(2,1)} %param.26), kind=kOutput, calls=%fused_computation.30 | convolution fusion | flops 1613365248 | bytes 7340032 | tf_op jit(solution)/shard_map/dot_general | solution.py:101
  121.6 2.7 %collective-permute-start.10 = (bf16[192,1024]{1,0:T(8,128)(2,1)S(1)}, bf16[192,1024]{1,0:T(8,128)(2,1)S(1)}, u32[]{:S(2)}, u32[]{:S(2)}) collective-permute-start(bf16[192,1024]{1,0:T(8,128)(2,1)S(1)} %get-tuple-element.22), channel_id=1, source_target_pairs={{0,192},{64,0},{128,64},{192,128},{1,193},{65,1},{129,65},{193,129... | collective-permute-start | bytes 1179656 | tf_op jit(solution)/shard_map/ppermute | solution.py:123
  124.2 12.0 %collective-permute-done.8 = bf16[192,1024]{1,0:T(8,128)(2,1)S(1)} collective-permute-done((bf16[192,1024]{1,0:T(8,128)(2,1)S(1)}, bf16[192,1024]{1,0:T(8,128)(2,1)S(1)}, u32[]{:S(2)}, u32[]{:S(2)}) %collective-permute-start.8) | collective-permute-done | bytes 393248 | tf_op jit(solution)/shard_map/ppermute | solution.py:122
  136.2 2.7 %collective-permute-start.11 = (bf16[192,1024]{1,0:T(8,128)(2,1)S(1)}, bf16[192,1024]{1,0:T(8,128)(2,1)S(1)}, u32[]{:S(2)}, u32[]{:S(2)}) collective-permute-start(bf16[192,1024]{1,0:T(8,128)(2,1)S(1)} %collective-permute-done.10), channel_id=1, source_target_pairs={{0,192},{64,0},{128,64},{192,128},{1,193},{65,1},{129,65},{193,129... | collective-permute-start | bytes 1179656 | tf_op jit(solution)/shard_map/ppermute | solution.py:125
  138.9 5.9 %collective-permute-done.9 = bf16[192,1024]{1,0:T(8,128)(2,1)S(1)} collective-permute-done((bf16[192,1024]{1,0:T(8,128)(2,1)S(1)}, bf16[192,1024]{1,0:T(8,128)(2,1)S(1)}, u32[]{:S(2)}, u32[]{:S(2)}) %collective-permute-start.9) | collective-permute-done | bytes 393248 | tf_op jit(solution)/shard_map/ppermute | solution.py:125
  144.8 1.9 %add_convert_fusion = bf16[384,1024]{1,0:T(8,128)(2,1)S(1)} fusion(bf16[384,1024]{1,0:T(8,128)(2,1)} %copy-done.5, f32[384,1024]{1,0:T(8,128)S(1)} %copy-done.4, bf16[384,1024]{1,0:T(8,128)(2,1)} %collective-permute-done.6, bf16[192,1024]{1,0:T(8,128)(2,1)S(1)} %collective-permute-done.11, bf16[192,1024]{1,0:T(8,128)(2,1)S(1)} %collective-permute-done.9), kind=kLoop, calls=%fused_computation.24 | loop fusion | flops 3932160 | bytes 4718592 | tf_op jit(solution)/shard_map/convert_element_type | solution.py:128
  148.0 10.1 %all-to-all-start.1 = ((bf16[64,48,128]{2,1,0:T(8,128)(2,1)}), bf16[64,48,128]{2,1,0:T(8,128)(2,1)}, u32[]{:S(2)}, u32[]{:S(2)}) async-start(bf16[64,48,128]{2,1,0:T(8,128)(2,1)} %reshape.91), calls=%async_computation.1 | async-start | bytes 1572864 | tf_op jit(solution)/shard_map/all_to_all | solution.py:129
  158.9 22.1 %all-to-all-done.1 = bf16[64,48,128]{2,1,0:T(8,128)(2,1)} async-done(((bf16[64,48,128]{2,1,0:T(8,128)(2,1)}), bf16[64,48,128]{2,1,0:T(8,128)(2,1)}, u32[]{:S(2)}, u32[]{:S(2)}) %all-to-all-start.1) | async-done | bytes 786464 | tf_op jit(solution)/shard_map/all_to_all | solution.py:129
  (85 shorter events, 26.4 us)
Async XLA Ops:
  0.0 67.8 %copy-start = (bf16[1,1024,1024]{2,1,0:T(8,128)(2,1)S(1)}, bf16[1,1024,1024]{2,1,0:T(8,128)(2,1)}, u32[]{:S(2)}) copy-start(bf16[1,1024,1024]{2,1,0:T(8,128)(2,1)} %param.25) | copy-start | bytes 6291460
  0.0 15.6 %copy-start.8 = (f32[1024]{0:T(1024)S(1)}, f32[1024]{0:T(1024)}, u32[]{:S(2)}) copy-start(f32[1024]{0:T(1024)} %param.17) | copy-start | bytes 12292
  1.0 14.2 %collective-permute-start = (bf16[15,1024]{1,0:T(8,128)(2,1)S(1)}, bf16[15,1024]{1,0:T(8,128)(2,1)S(1)}, u32[]{:S(2)}, u32[]{:S(2)}) collective-permute-start(bf16[15,1024]{1,0:T(8,128)(2,1)S(1)} %get-tuple-element.23), channel_id=1, source_target_pairs={{0,8},{8,16},{16,24},{24,32},{32,40},{40,48},{48,56},{1,9},{9,17},... | collective-permute-start | bytes 92168 | tf_op jit(solution)/shard_map/ppermute | solution.py:38
  5.3 9.9 %collective-permute-start.1 = (bf16[15,1024]{1,0:T(8,128)(2,1)S(1)}, bf16[15,1024]{1,0:T(8,128)(2,1)S(1)}, u32[]{:S(2)}, u32[]{:S(2)}) collective-permute-start(bf16[15,1024]{1,0:T(8,128)(2,1)S(1)} %get-tuple-element.24), channel_id=1, source_target_pairs={{8,0},{16,8},{24,16},{32,24},{40,32},{48,40},{56,48},{9,1},{17,9},... | collective-permute-start | bytes 92168 | tf_op jit(solution)/shard_map/ppermute | solution.py:39
  15.7 3.4 %copy-start.11 = (bf16[1024,1024]{1,0:T(8,128)(2,1)S(1)}, bf16[1024,1024]{1,0:T(8,128)(2,1)}, u32[]{:S(2)}) copy-start(bf16[1024,1024]{1,0:T(8,128)(2,1)} %param.22) | copy-start | bytes 6291460
  19.8 2.8 %copy-start.9 = (f32[1024]{0:T(1024)S(1)}, f32[1024]{0:T(1024)}, u32[]{:S(2)}) copy-start(f32[1024]{0:T(1024)} %param.23) | copy-start | bytes 12292
  65.0 19.0 %collective-permute-start.3 = (bf16[384,1024]{1,0:T(8,128)(2,1)S(1)}, bf16[384,1024]{1,0:T(8,128)(2,1)}, u32[]{:S(2)}, u32[]{:S(2)}) collective-permute-start(bf16[384,1024]{1,0:T(8,128)(2,1)S(1)} %reshape.90), channel_id=1, source_target_pairs={{0,192},{64,0},{128,64},{192,128},{1,193},{65,1},{129,65},{193,129... | collective-permute-start | bytes 2359304 | tf_op jit(solution)/shard_map/ppermute | solution.py:110
  67.8 19.4 %collective-permute-start.2 = (bf16[384,1024]{1,0:T(8,128)(2,1)S(1)}, bf16[384,1024]{1,0:T(8,128)(2,1)}, u32[]{:S(2)}, u32[]{:S(2)}) collective-permute-start(bf16[384,1024]{1,0:T(8,128)(2,1)S(1)} %reshape.90), channel_id=1, source_target_pairs={{0,64},{64,128},{128,192},{192,0},{1,65},{65,129},{129,193},{193,1... | collective-permute-start | bytes 2359304 | tf_op jit(solution)/shard_map/ppermute | solution.py:109
  88.3 5.1 %copy-start.12 = (bf16[1,1024,1024]{2,1,0:T(8,128)(2,1)S(1)}, bf16[1,1024,1024]{2,1,0:T(8,128)(2,1)}, u32[]{:S(2)}) copy-start(bf16[1,1024,1024]{2,1,0:T(8,128)(2,1)} %param.26) | copy-start | bytes 6291460
  96.7 11.7 %collective-permute-start.5 = (bf16[192,1024]{1,0:T(8,128)(2,1)S(1)}, bf16[192,1024]{1,0:T(8,128)(2,1)}, u32[]{:S(2)}, u32[]{:S(2)}) collective-permute-start(bf16[192,1024]{1,0:T(8,128)(2,1)S(1)} %slice.303), channel_id=1, source_target_pairs={{0,192},{64,0},{128,64},{192,128},{1,193},{65,1},{129,65},{193,129... | collective-permute-start | bytes 1179656 | tf_op jit(solution)/shard_map/ppermute | solution.py:114
  97.0 11.4 %collective-permute-start.4 = (bf16[192,1024]{1,0:T(8,128)(2,1)S(1)}, bf16[192,1024]{1,0:T(8,128)(2,1)}, u32[]{:S(2)}, u32[]{:S(2)}) collective-permute-start(bf16[192,1024]{1,0:T(8,128)(2,1)S(1)} %slice.302), channel_id=1, source_target_pairs={{0,64},{64,128},{128,192},{192,0},{1,65},{65,129},{129,193},{193,1... | collective-permute-start | bytes 1179656 | tf_op jit(solution)/shard_map/ppermute | solution.py:114
  109.6 2.8 %copy-start.6 = (bf16[384,1024]{1,0:T(8,128)(2,1)}, bf16[384,1024]{1,0:T(8,128)(2,1)S(1)}, u32[]{:S(2)}) copy-start(bf16[384,1024]{1,0:T(8,128)(2,1)S(1)} %pad_maximum_fusion) | copy-start | bytes 2359300
  109.6 29.3 %collective-permute-start.6 = (bf16[384,1024]{1,0:T(8,128)(2,1)}, bf16[384,1024]{1,0:T(8,128)(2,1)}, u32[]{:S(2)}, u32[]{:S(2)}) collective-permute-start(bf16[384,1024]{1,0:T(8,128)(2,1)} %fusion.2), channel_id=1, source_target_pairs={{0,64},{64,128},{128,192},{192,0},{1,65},{65,129},{129,193},{193,1... | collective-permute-start | bytes 2359304 | tf_op jit(solution)/shard_map/ppermute | solution.py:119
  109.7 29.2 %collective-permute-start.7 = (bf16[384,1024]{1,0:T(8,128)(2,1)}, bf16[384,1024]{1,0:T(8,128)(2,1)S(1)}, u32[]{:S(2)}, u32[]{:S(2)}) collective-permute-start(bf16[384,1024]{1,0:T(8,128)(2,1)} %fusion.4), channel_id=1, source_target_pairs={{0,192},{64,0},{128,64},{192,128},{1,193},{65,1},{129,65},{193,129... | collective-permute-start | bytes 2359304 | tf_op jit(solution)/shard_map/ppermute | solution.py:120
  120.2 24.7 %copy-start.4 = (f32[384,1024]{1,0:T(8,128)S(1)}, f32[384,1024]{1,0:T(8,128)}, u32[]{:S(2)}) copy-start(f32[384,1024]{1,0:T(8,128)} %fusion.6) | copy-start | bytes 4718596
  121.5 14.7 %collective-permute-start.8 = (bf16[192,1024]{1,0:T(8,128)(2,1)S(1)}, bf16[192,1024]{1,0:T(8,128)(2,1)S(1)}, u32[]{:S(2)}, u32[]{:S(2)}) collective-permute-start(bf16[192,1024]{1,0:T(8,128)(2,1)S(1)} %get-tuple-element.21), channel_id=1, source_target_pairs={{0,64},{64,128},{128,192},{192,0},{1,65},{65,129},{129,193},{193,1... | collective-permute-start | bytes 1179656 | tf_op jit(solution)/shard_map/ppermute | solution.py:122
  121.6 14.6 %collective-permute-start.10 = (bf16[192,1024]{1,0:T(8,128)(2,1)S(1)}, bf16[192,1024]{1,0:T(8,128)(2,1)S(1)}, u32[]{:S(2)}, u32[]{:S(2)}) collective-permute-start(bf16[192,1024]{1,0:T(8,128)(2,1)S(1)} %get-tuple-element.22), channel_id=1, source_target_pairs={{0,192},{64,0},{128,64},{192,128},{1,193},{65,1},{129,65},{193,129... | collective-permute-start | bytes 1179656 | tf_op jit(solution)/shard_map/ppermute | solution.py:123
  136.2 8.6 %collective-permute-start.9 = (bf16[192,1024]{1,0:T(8,128)(2,1)S(1)}, bf16[192,1024]{1,0:T(8,128)(2,1)S(1)}, u32[]{:S(2)}, u32[]{:S(2)}) collective-permute-start(bf16[192,1024]{1,0:T(8,128)(2,1)S(1)} %collective-permute-done.8), channel_id=1, source_target_pairs={{0,64},{64,128},{128,192},{192,0},{1,65},{65,129},{129,193},{193,1... | collective-permute-start | bytes 1179656 | tf_op jit(solution)/shard_map/ppermute | solution.py:125
  136.2 8.6 %collective-permute-start.11 = (bf16[192,1024]{1,0:T(8,128)(2,1)S(1)}, bf16[192,1024]{1,0:T(8,128)(2,1)S(1)}, u32[]{:S(2)}, u32[]{:S(2)}) collective-permute-start(bf16[192,1024]{1,0:T(8,128)(2,1)S(1)} %collective-permute-done.10), channel_id=1, source_target_pairs={{0,192},{64,0},{128,64},{192,128},{1,193},{65,1},{129,65},{193,129... | collective-permute-start | bytes 1179656 | tf_op jit(solution)/shard_map/ppermute | solution.py:125
  138.9 5.9 %copy-start.5 = (bf16[384,1024]{1,0:T(8,128)(2,1)}, bf16[384,1024]{1,0:T(8,128)(2,1)S(1)}, u32[]{:S(2)}) copy-start(bf16[384,1024]{1,0:T(8,128)(2,1)S(1)} %collective-permute-done.7) | copy-start | bytes 2359300
  146.8 11.9 %copy-start.7 = (bf16[1024,64]{0,1:T(8,128)(2,1)S(1)}, bf16[1024,64]{0,1:T(8,128)(2,1)}, u32[]{:S(2)}) copy-start(bf16[1024,64]{0,1:T(8,128)(2,1)} %param.24) | copy-start | bytes 393220
  148.0 10.7 %copy-start.3 = (bf16[128,1024]{1,0:T(8,128)(2,1)S(1)}, bf16[128,1024]{1,0:T(8,128)(2,1)}, u32[]{:S(2)}) copy-start(bf16[128,1024]{1,0:T(8,128)(2,1)} %copy-done.2) | copy-start | bytes 786436
  148.0 33.0 %all-to-all-start.1 = ((bf16[64,48,128]{2,1,0:T(8,128)(2,1)}), bf16[64,48,128]{2,1,0:T(8,128)(2,1)}, u32[]{:S(2)}, u32[]{:S(2)}) async-start(bf16[64,48,128]{2,1,0:T(8,128)(2,1)} %reshape.91), calls=%async_computation.1 | async-start | bytes 1572864 | tf_op jit(solution)/shard_map/all_to_all | solution.py:129
  158.9 23.9 %copy-start.10 = (f32[128]{0:T(128)S(1)}, f32[128]{0:T(128)}, u32[]{:S(2)}) copy-start(f32[128]{0:T(128)} %compare_convert_fusion) | copy-start | bytes 1540
  (4 other events, 3.5 us)

commit v8 on v5

--- a/solution.py
+++ b/solution.py
@@ -110,8 +110,8 @@
     far_rows = jnp.concatenate(
         [lax.ppermute(from_below[:half], "dp", up), lax.ppermute(from_above[half:], "dp", down)], axis=0
     )
-    for_below = serve(from_below)
-    for_above = serve(from_above)
+    for_near = serve(jnp.concatenate([from_below, from_above], axis=0))
+    for_below, for_above = for_near[: 2 * half], for_near[2 * half :]
     far_rows, for_below, for_above = lax.optimization_barrier((far_rows, for_below, for_above))
     got_below = lax.ppermute(for_above.astype(jnp.bfloat16), "dp", up).astype(jnp.float32)
     got_above = lax.ppermute(for_below.astype(jnp.bfloat16), "dp", down).astype(jnp.float32)

time: 178 us -> 178 us (level)
  local copies, waits for them, and re-layouts: 9.91 us -> 16.2 us
  matrix products: 40 us -> 35.3 us
    dot_general x2 -> x1, matrix products: 7.35 us -> 3.45 us  [serve(): up_part = jnp.dot(rows, up_local, preferred_element_type=jnp.float32)]
    slice x0 -> x1, local copies, waits for them, and re-layouts: none -> 2.62 us  [local(): for_below, for_above = (for_near[:2 * half], for_near[2 * half:])]
    unnamed x34 -> x37, local copies, waits for them, and re-layouts: 0.78 us -> 3.1 us
    dot_general x4 -> x3, matrix products: 21.7 us -> 19.6 us  [serve(): lax.dot_general(hidden, down_local, (((1,), (1,)), ((), ())), preferred_e...]
  transfers between devices with their start and end apart: 13 -> 13, of which waited for: 6 -> 6; matrix products, arithmetic and copies ran while one was open for 17% -> 20% of each run, Pallas kernels for 0% -> 0%
where the time goes in v8:
time: 178 us; the launch traced here: 177 us
  waiting for transfers between devices  52 us (29%)
  blocking collectives  36.4 us (20%)
  matrix products  35.3 us (20%)
  starting transfers between devices  28.1 us (16%)
  local copies, waits for them, and re-layouts  16.2 us (9%)
  other arithmetic  8.25 us (5%)
    all_to_all x1, blocking collectives, local(): lax.all_to_all(outgoing, ('seq', 'expert'), split_axis=0, concat_axis=0,...  36.4 us
    all_to_all x1, waiting for transfers between devices, local(): lax.all_to_all(served, ('seq', 'expert'), split_axis=0, concat_axis=0, ti...  22.7 us
    dot_general x3, matrix products, serve(): lax.dot_general(hidden, down_local, (((1,), (1,)), ((), ())), preferred_e...  19.6 us
    ppermute x1, waiting for transfers between devices, local(): hop_up = lax.ppermute(for_far[:half], 'dp', up)  11.9 us
    all_to_all x1, starting transfers between devices, local(): lax.all_to_all(served, ('seq', 'expert'), split_axis=0, concat_axis=0, ti...  10.1 us
    ppermute x1, waiting for transfers between devices, local(): from_above = lax.ppermute(own_rows, 'dp', down)  7.19 us
    ppermute x1, waiting for transfers between devices, local(): lax.ppermute(hop_up, 'dp', up)  5.94 us
    dot_general x2, matrix products, serve(): gate_part = jnp.dot(rows, gate_local, preferred_element_type=jnp.float32)  5.5 us
  transfers between devices with their start and end apart: 13, of which 6 were waited for; matrix products, arithmetic and copies ran while one was open for 20% of the time, Pallas kernels for 0%

profile of v8, /device:TPU:1, one launch (start us, length us, event | category | flops | bytes accessed | tf_op | source)
XLA Modules:
  0.0 177.5 jit_solution(7824251501284900540)
XLA Ops:
  3.1 3.1 %fusion.53 = f32[128,2048]{1,0:T(8,128)S(1)} fusion(bf16[1024,2048]{1,0:T(8,128)(2,1)} %param.18, bf16[1,128,1024]{2,1,0:T(8,128)(2,1)} %param.14, f32[1024]{0:T(1024)} %param.17, f32[128]{0:T(128)S(1)} %add_rsqrt_fusion.1, f32[128]{0:T(128)S(1)} %broadcast_multiply_fusion.1), kind=kOutput, calls=%fused_computation.82 | convolution fusion | flops 537526272 | bytes 5510144 | tf_op jit(solution)/shard_map/dot_general | solution.py:36
  6.4 4.4 %collective-permute-start = (bf16[15,1024]{1,0:T(8,128)(2,1)S(1)}, bf16[15,1024]{1,0:T(8,128)(2,1)S(1)}, u32[]{:S(2)}, u32[]{:S(2)}) collective-permute-start(bf16[15,1024]{1,0:T(8,128)(2,1)S(1)} %get-tuple-element.27), channel_id=1, source_target_pairs={{0,8},{8,16},{16,24},{24,32},{32,40},{40,48},{48,56},{1,9},{9,17},... | collective-permute-start | bytes 92168 | tf_op jit(solution)/shard_map/ppermute | solution.py:45
  12.7 1.5 multiply_add_fusion
  20.5 36.4 %all_to_all.10 = bf16[64,48,128]{2,1,0:T(8,128)(2,1)} all-to-all(bf16[64,48,128]{2,1,0:T(8,128)(2,1)S(1)} %reshape.67), channel_id=1, replica_groups=mesh['dp'=4,'seq'=8,'expert'=8] {'seq','expert'}, dimensions={0} | all-to-all | bytes 1572864 | tf_op jit(solution)/shard_map/all_to_all | solution.py:90
  56.9 2.2 %reshape.68 = bf16[384,1024]{1,0:T(8,128)(2,1)} reshape(bf16[64,48,128]{2,1,0:T(8,128)(2,1)} %all_to_all.10) | data formatting | bytes 1572864 | tf_op jit(solution)/shard_map/reshape | solution.py:92
  59.1 2.7 %collective-permute-start.3 = (bf16[384,1024]{1,0:T(8,128)(2,1)}, bf16[384,1024]{1,0:T(8,128)(2,1)S(1)}, u32[]{:S(2)}, u32[]{:S(2)}) collective-permute-start(bf16[384,1024]{1,0:T(8,128)(2,1)} %reshape.68), channel_id=1, source_target_pairs={{0,192},{64,0},{128,64},{192,128},{1,193},{65,1},{129,65},{193,129... | collective-permute-start | bytes 2359304 | tf_op jit(solution)/shard_map/ppermute | solution.py:107
  61.8 3.3 %fusion.16 = f32[384,1024]{1,0:T(8,128)} fusion(bf16[384,1024]{1,0:T(8,128)(2,1)} %reshape.68, bf16[1,1024,1024]{2,1,0:T(8,128)(2,1)S(1)} %copy-done), kind=kOutput, calls=%fused_computation.17 | convolution fusion | flops 805306368 | bytes 4456448 | tf_op jit(solution)/shard_map/dot_general | solution.py:95
  65.2 6.0 %fusion.4 = f32[384,1024]{1,0:T(8,128)} fusion(bf16[1,1024,1024]{2,1,0:T(8,128)(2,1)} %param.27, f32[384,1024]{1,0:T(8,128)} %fusion.16, bf16[384,1024]{1,0:T(8,128)(2,1)} %reshape.68, bf16[1,1024,1024]{2,1,0:T(8,128)(2,1)} %param.26), kind=kOutput, calls=%fused_computation.5 | convolution fusion | flops 1612972032 | bytes 8126464 | tf_op jit(solution)/shard_map/dot_general | solution.py:98
  71.1 7.2 %collective-permute-done.3 = bf16[384,1024]{1,0:T(8,128)(2,1)S(1)} collective-permute-done((bf16[384,1024]{1,0:T(8,128)(2,1)}, bf16[384,1024]{1,0:T(8,128)(2,1)S(1)}, u32[]{:S(2)}, u32[]{:S(2)}) %collective-permute-start.3) | collective-permute-done | bytes 786464 | tf_op jit(solution)/shard_map/ppermute | solution.py:107
  78.3 3.1 %collective-permute-done.2 = bf16[384,1024]{1,0:T(8,128)(2,1)} collective-permute-done((bf16[384,1024]{1,0:T(8,128)(2,1)}, bf16[384,1024]{1,0:T(8,128)(2,1)}, u32[]{:S(2)}, u32[]{:S(2)}) %collective-permute-start.2) | collective-permute-done | bytes 786464 | tf_op jit(solution)/shard_map/ppermute | solution.py:106
  81.5 1.8 %slice.628 = bf16[192,1024]{1,0:T(8,128)(2,1)} slice(bf16[384,1024]{1,0:T(8,128)(2,1)} %collective-permute-done.2), slice={[0:192], [0:1024]} | slice | bytes 786432 | tf_op jit(solution)/shard_map/slice | solution.py:111
  87.9 3.5 %fusion.8 = f32[768,1024]{1,0:T(8,128)} fusion(bf16[768,1024]{1,0:T(8,128)(2,1)S(1)} %constant_dynamic-update-slice_fusion, bf16[1,1024,1024]{2,1,0:T(8,128)(2,1)S(1)} %copy-done.15), kind=kOutput, calls=%fused_computation.9 | convolution fusion | flops 1610612736 | bytes 6815744 | tf_op jit(solution)/shard_map/dot_general | solution.py:96
  91.4 7.9 %fusion.2 = bf16[768,1024]{1,0:T(8,128)(2,1)} fusion(bf16[1,1024,1024]{2,1,0:T(8,128)(2,1)} %param.27, f32[768,1024]{1,0:T(8,128)} %fusion.8, bf16[768,1024]{1,0:T(8,128)(2,1)} %copy-done.7, bf16[1,1024,1024]{2,1,0:T(8,128)(2,1)S(1)} %copy-done), kind=kOutput, calls=%fused_computation.3 | convolution fusion | flops 3225944064 | bytes 10485760 | tf_op jit(solution)/shard_map/dot_general | solution.py:98
  99.3 2.6 %fusion.107 = (bf16[384,1024]{1,0:T(8,128)(2,1)}, bf16[384,1024]{1,0:T(8,128)(2,1)}) fusion(bf16[768,1024]{1,0:T(8,128)(2,1)} %fusion.2), kind=kLoop, calls=%fused_computation.185 | loop fusion | bytes 3145728 | tf_op jit(solution)/shard_map/slice | solution.py:114
  103.2 2.7 %collective-permute-start.7 = (bf16[384,1024]{1,0:T(8,128)(2,1)}, bf16[384,1024]{1,0:T(8,128)(2,1)}, u32[]{:S(2)}, u32[]{:S(2)}) collective-permute-start(bf16[384,1024]{1,0:T(8,128)(2,1)} %get-tuple-element.15), channel_id=1, source_target_pairs={{0,192},{64,0},{128,64},{192,128},{1,193},{65,1},{129,65},{193,129... | collective-permute-start | bytes 2359304 | tf_op jit(solution)/shard_map/ppermute | solution.py:117
  105.9 2.2 %fusion.12 = f32[384,1024]{1,0:T(8,128)} fusion(bf16[384,1024]{1,0:T(8,128)(2,1)S(1)} %pad_maximum_fusion, bf16[1,1024,1024]{2,1,0:T(8,128)(2,1)S(1)} %copy-done), kind=kOutput, calls=%fused_computation.13 | convolution fusion | flops 805306368 | bytes 4456448 | tf_op jit(solution)/shard_map/dot_general | solution.py:95
  108.0 5.7 %fusion.26 = bf16[384,1024]{1,0:T(8,128)(2,1)} fusion(bf16[1,1024,1024]{2,1,0:T(8,128)(2,1)} %param.27, f32[384,1024]{1,0:T(8,128)} %fusion.12, bf16[384,1024]{1,0:T(8,128)(2,1)} %copy-done.6, bf16[1,1024,1024]{2,1,0:T(8,128)(2,1)} %param.26), kind=kOutput, calls=%fused_computation.23 | convolution fusion | flops 1613365248 | bytes 7340032 | tf_op jit(solution)/shard_map/dot_general | solution.py:98
  115.2 2.7 %collective-permute-start.10 = (bf16[192,1024]{1,0:T(8,128)(2,1)S(1)}, bf16[192,1024]{1,0:T(8,128)(2,1)S(1)}, u32[]{:S(2)}, u32[]{:S(2)}) collective-permute-start(bf16[192,1024]{1,0:T(8,128)(2,1)S(1)} %get-tuple-element.24), channel_id=1, source_target_pairs={{0,192},{64,0},{128,64},{192,128},{1,193},{65,1},{129,65},{193,129... | collective-permute-start | bytes 1179656 | tf_op jit(solution)/shard_map/ppermute | solution.py:120
  117.8 11.9 %collective-permute-done.8 = bf16[192,1024]{1,0:T(8,128)(2,1)S(1)} collective-permute-done((bf16[192,1024]{1,0:T(8,128)(2,1)S(1)}, bf16[192,1024]{1,0:T(8,128)(2,1)S(1)}, u32[]{:S(2)}, u32[]{:S(2)}) %collective-permute-start.8) | collective-permute-done | bytes 393248 | tf_op jit(solution)/shard_map/ppermute | solution.py:119
  129.8 2.7 %collective-permute-start.11 = (bf16[192,1024]{1,0:T(8,128)(2,1)S(1)}, bf16[192,1024]{1,0:T(8,128)(2,1)S(1)}, u32[]{:S(2)}, u32[]{:S(2)}) collective-permute-start(bf16[192,1024]{1,0:T(8,128)(2,1)S(1)} %collective-permute-done.10), channel_id=1, source_target_pairs={{0,192},{64,0},{128,64},{192,128},{1,193},{65,1},{129,65},{193,129... | collective-permute-start | bytes 1179656 | tf_op jit(solution)/shard_map/ppermute | solution.py:122
  132.4 5.9 %collective-permute-done.9 = bf16[192,1024]{1,0:T(8,128)(2,1)S(1)} collective-permute-done((bf16[192,1024]{1,0:T(8,128)(2,1)S(1)}, bf16[192,1024]{1,0:T(8,128)(2,1)S(1)}, u32[]{:S(2)}, u32[]{:S(2)}) %collective-permute-start.9) | collective-permute-done | bytes 393248 | tf_op jit(solution)/shard_map/ppermute | solution.py:122
  138.4 1.9 %add_convert_fusion = bf16[384,1024]{1,0:T(8,128)(2,1)S(1)} fusion(bf16[384,1024]{1,0:T(8,128)(2,1)} %collective-permute-done.7, f32[384,1024]{1,0:T(8,128)S(1)} %copy-done.4, bf16[384,1024]{1,0:T(8,128)(2,1)} %copy-done.5, bf16[192,1024]{1,0:T(8,128)(2,1)S(1)} %collective-permute-done.11, bf16[192,1024]{1,0:T(8,128)(2,1)S(1)} %collective-permute-done.9), kind=kLoop, calls=%fused_computation.19 | loop fusion | flops 3932160 | bytes 4718592 | tf_op jit(solution)/shard_map/convert_element_type | solution.py:125
  141.6 10.1 %all-to-all-start.1 = ((bf16[64,48,128]{2,1,0:T(8,128)(2,1)}), bf16[64,48,128]{2,1,0:T(8,128)(2,1)}, u32[]{:S(2)}, u32[]{:S(2)}) async-start(bf16[64,48,128]{2,1,0:T(8,128)(2,1)} %reshape.69), calls=%async_computation.1 | async-start | bytes 1572864 | tf_op jit(solution)/shard_map/all_to_all | solution.py:126
  151.9 22.7 %all-to-all-done.1 = bf16[64,48,128]{2,1,0:T(8,128)(2,1)} async-done(((bf16[64,48,128]{2,1,0:T(8,128)(2,1)}), bf16[64,48,128]{2,1,0:T(8,128)(2,1)}, u32[]{:S(2)}, u32[]{:S(2)}) %all-to-all-start.1) | async-done | bytes 786464 | tf_op jit(solution)/shard_map/all_to_all | solution.py:126
  (88 shorter events, 22.1 us)
Async XLA Ops:
  0.0 61.8 %copy-start = (bf16[1,1024,1024]{2,1,0:T(8,128)(2,1)S(1)}, bf16[1,1024,1024]{2,1,0:T(8,128)(2,1)}, u32[]{:S(2)}) copy-start(bf16[1,1024,1024]{2,1,0:T(8,128)(2,1)} %param.25) | copy-start | bytes 6291460
  3.1 3.1 %copy-start.12 = (f32[128]{0:T(128)}, f32[128]{0:T(128)S(1)}, u32[]{:S(2)}) copy-start(f32[128]{0:T(128)S(1)} %compare_convert_fusion) | copy-start | bytes 1540
  3.1 9.0 %copy-start.9 = (f32[31,1024]{1,0:T(8,128)S(1)}, f32[31,1024]{1,0:T(8,128)}, u32[]{:S(2)}) copy-start(f32[31,1024]{1,0:T(8,128)} %param.19) | copy-start | bytes 380932
  6.2 6.0 %copy-start.11 = (s32[1,128,2]{1,2,0:T(2,128)S(1)}, s32[1,128,2]{1,2,0:T(2,128)}, u32[]{:S(2)}) copy-start(s32[1,128,2]{1,2,0:T(2,128)} %param.16) | copy-start | bytes 3076
  6.4 7.8 %collective-permute-start = (bf16[15,1024]{1,0:T(8,128)(2,1)S(1)}, bf16[15,1024]{1,0:T(8,128)(2,1)S(1)}, u32[]{:S(2)}, u32[]{:S(2)}) collective-permute-start(bf16[15,1024]{1,0:T(8,128)(2,1)S(1)} %get-tuple-element.27), channel_id=1, source_target_pairs={{0,8},{8,16},{16,24},{24,32},{32,40},{40,48},{48,56},{1,9},{9,17},... | collective-permute-start | bytes 92168 | tf_op jit(solution)/shard_map/ppermute | solution.py:45
  10.8 4.8 %collective-permute-start.1 = (bf16[15,1024]{1,0:T(8,128)(2,1)S(1)}, bf16[15,1024]{1,0:T(8,128)(2,1)S(1)}, u32[]{:S(2)}, u32[]{:S(2)}) collective-permute-start(bf16[15,1024]{1,0:T(8,128)(2,1)S(1)} %get-tuple-element.28), channel_id=1, source_target_pairs={{8,0},{16,8},{24,16},{32,24},{40,32},{48,40},{56,48},{9,1},{17,9},... | collective-permute-start | bytes 92168 | tf_op jit(solution)/shard_map/ppermute | solution.py:46
  12.7 3.3 %copy-start.14 = (bf16[1024,1024]{1,0:T(8,128)(2,1)S(1)}, bf16[1024,1024]{1,0:T(8,128)(2,1)}, u32[]{:S(2)}) copy-start(bf16[1024,1024]{1,0:T(8,128)(2,1)} %param.22) | copy-start | bytes 6291460
  59.1 19.3 %collective-permute-start.3 = (bf16[384,1024]{1,0:T(8,128)(2,1)}, bf16[384,1024]{1,0:T(8,128)(2,1)S(1)}, u32[]{:S(2)}, u32[]{:S(2)}) collective-permute-start(bf16[384,1024]{1,0:T(8,128)(2,1)} %reshape.68), channel_id=1, source_target_pairs={{0,192},{64,0},{128,64},{192,128},{1,193},{65,1},{129,65},{193,129... | collective-permute-start | bytes 2359304 | tf_op jit(solution)/shard_map/ppermute | solution.py:107
  61.8 19.6 %collective-permute-start.2 = (bf16[384,1024]{1,0:T(8,128)(2,1)}, bf16[384,1024]{1,0:T(8,128)(2,1)}, u32[]{:S(2)}, u32[]{:S(2)}) collective-permute-start(bf16[384,1024]{1,0:T(8,128)(2,1)} %reshape.68), channel_id=1, source_target_pairs={{0,64},{64,128},{128,192},{192,0},{1,65},{65,129},{129,193},{193,1... | collective-permute-start | bytes 2359304 | tf_op jit(solution)/shard_map/ppermute | solution.py:106
  84.5 3.5 %copy-start.15 = (bf16[1,1024,1024]{2,1,0:T(8,128)(2,1)S(1)}, bf16[1,1024,1024]{2,1,0:T(8,128)(2,1)}, u32[]{:S(2)}) copy-start(bf16[1,1024,1024]{2,1,0:T(8,128)(2,1)} %param.26) | copy-start | bytes 6291460
  85.3 16.7 %collective-permute-start.5 = (bf16[192,1024]{1,0:T(8,128)(2,1)}, bf16[192,1024]{1,0:T(8,128)(2,1)}, u32[]{:S(2)}, u32[]{:S(2)}) collective-permute-start(bf16[192,1024]{1,0:T(8,128)(2,1)} %slice.629), channel_id=1, source_target_pairs={{0,192},{64,0},{128,64},{192,128},{1,193},{65,1},{129,65},{193,129... | collective-permute-start | bytes 1179656 | tf_op jit(solution)/shard_map/ppermute | solution.py:111
  85.4 16.5 %collective-permute-start.4 = (bf16[192,1024]{1,0:T(8,128)(2,1)}, bf16[192,1024]{1,0:T(8,128)(2,1)}, u32[]{:S(2)}, u32[]{:S(2)}) collective-permute-start(bf16[192,1024]{1,0:T(8,128)(2,1)} %slice.628), channel_id=1, source_target_pairs={{0,64},{64,128},{128,192},{192,0},{1,65},{65,129},{129,193},{193,1... | collective-permute-start | bytes 1179656 | tf_op jit(solution)/shard_map/ppermute | solution.py:111
  103.1 29.3 %collective-permute-start.6 = (bf16[384,1024]{1,0:T(8,128)(2,1)}, bf16[384,1024]{1,0:T(8,128)(2,1)S(1)}, u32[]{:S(2)}, u32[]{:S(2)}) collective-permute-start(bf16[384,1024]{1,0:T(8,128)(2,1)} %get-tuple-element.14), channel_id=1, source_target_pairs={{0,64},{64,128},{128,192},{192,0},{1,65},{65,129},{129,193},{193,1... | collective-permute-start | bytes 2359304 | tf_op jit(solution)/shard_map/ppermute | solution.py:116
  103.2 29.2 %collective-permute-start.7 = (bf16[384,1024]{1,0:T(8,128)(2,1)}, bf16[384,1024]{1,0:T(8,128)(2,1)}, u32[]{:S(2)}, u32[]{:S(2)}) collective-permute-start(bf16[384,1024]{1,0:T(8,128)(2,1)} %get-tuple-element.15), channel_id=1, source_target_pairs={{0,192},{64,0},{128,64},{192,128},{1,193},{65,1},{129,65},{193,129... | collective-permute-start | bytes 2359304 | tf_op jit(solution)/shard_map/ppermute | solution.py:117
  113.8 24.6 %copy-start.4 = (f32[384,1024]{1,0:T(8,128)S(1)}, f32[384,1024]{1,0:T(8,128)}, u32[]{:S(2)}) copy-start(f32[384,1024]{1,0:T(8,128)} %fusion.4) | copy-start | bytes 4718596
  115.1 14.7 %collective-permute-start.8 = (bf16[192,1024]{1,0:T(8,128)(2,1)S(1)}, bf16[192,1024]{1,0:T(8,128)(2,1)S(1)}, u32[]{:S(2)}, u32[]{:S(2)}) collective-permute-start(bf16[192,1024]{1,0:T(8,128)(2,1)S(1)} %get-tuple-element.23), channel_id=1, source_target_pairs={{0,64},{64,128},{128,192},{192,0},{1,65},{65,129},{129,193},{193,1... | collective-permute-start | bytes 1179656 | tf_op jit(solution)/shard_map/ppermute | solution.py:119
  115.2 14.6 %collective-permute-start.10 = (bf16[192,1024]{1,0:T(8,128)(2,1)S(1)}, bf16[192,1024]{1,0:T(8,128)(2,1)S(1)}, u32[]{:S(2)}, u32[]{:S(2)}) collective-permute-start(bf16[192,1024]{1,0:T(8,128)(2,1)S(1)} %get-tuple-element.24), channel_id=1, source_target_pairs={{0,192},{64,0},{128,64},{192,128},{1,193},{65,1},{129,65},{193,129... | collective-permute-start | bytes 1179656 | tf_op jit(solution)/shard_map/ppermute | solution.py:120
  129.8 8.6 %collective-permute-start.9 = (bf16[192,1024]{1,0:T(8,128)(2,1)S(1)}, bf16[192,1024]{1,0:T(8,128)(2,1)S(1)}, u32[]{:S(2)}, u32[]{:S(2)}) collective-permute-start(bf16[192,1024]{1,0:T(8,128)(2,1)S(1)} %collective-permute-done.8), channel_id=1, source_target_pairs={{0,64},{64,128},{128,192},{192,0},{1,65},{65,129},{129,193},{193,1... | collective-permute-start | bytes 1179656 | tf_op jit(solution)/shard_map/ppermute | solution.py:122
  129.8 8.6 %collective-permute-start.11 = (bf16[192,1024]{1,0:T(8,128)(2,1)S(1)}, bf16[192,1024]{1,0:T(8,128)(2,1)S(1)}, u32[]{:S(2)}, u32[]{:S(2)}) collective-permute-start(bf16[192,1024]{1,0:T(8,128)(2,1)S(1)} %collective-permute-done.10), channel_id=1, source_target_pairs={{0,192},{64,0},{128,64},{192,128},{1,193},{65,1},{129,65},{193,129... | collective-permute-start | bytes 1179656 | tf_op jit(solution)/shard_map/ppermute | solution.py:122
  132.4 6.0 %copy-start.5 = (bf16[384,1024]{1,0:T(8,128)(2,1)}, bf16[384,1024]{1,0:T(8,128)(2,1)S(1)}, u32[]{:S(2)}) copy-start(bf16[384,1024]{1,0:T(8,128)(2,1)S(1)} %collective-permute-done.6) | copy-start | bytes 2359300
  140.3 11.3 %copy-start.8 = (bf16[1024,64]{0,1:T(8,128)(2,1)S(1)}, bf16[1024,64]{0,1:T(8,128)(2,1)}, u32[]{:S(2)}) copy-start(bf16[1024,64]{0,1:T(8,128)(2,1)} %param.24) | copy-start | bytes 393220
  141.6 10.1 %copy-start.2 = (bf16[128,1024]{1,0:T(8,128)(2,1)S(1)}, bf16[128,1024]{1,0:T(8,128)(2,1)}, u32[]{:S(2)}) copy-start(bf16[128,1024]{1,0:T(8,128)(2,1)} %copy-done.1) | copy-start | bytes 786436
  141.6 33.0 %all-to-all-start.1 = ((bf16[64,48,128]{2,1,0:T(8,128)(2,1)}), bf16[64,48,128]{2,1,0:T(8,128)(2,1)}, u32[]{:S(2)}, u32[]{:S(2)}) async-start(bf16[64,48,128]{2,1,0:T(8,128)(2,1)} %reshape.69), calls=%async_computation.1 | async-start | bytes 1572864 | tf_op jit(solution)/shard_map/all_to_all | solution.py:126
  151.9 24.5 %copy-start.13 = (f32[128]{0:T(128)S(1)}, f32[128]{0:T(128)}, u32[]{:S(2)}) copy-start(f32[128]{0:T(128)} %copy-done.12) | copy-start | bytes 1540
  (7 other events, 10.9 us)

commit v9 on v8

--- a/solution.py
+++ b/solution.py
@@ -113,15 +113,16 @@
     for_near = serve(jnp.concatenate([from_below, from_above], axis=0))
     for_below, for_above = for_near[: 2 * half], for_near[2 * half :]
     far_rows, for_below, for_above = lax.optimization_barrier((far_rows, for_below, for_above))
-    got_below = lax.ppermute(for_above.astype(jnp.bfloat16), "dp", up).astype(jnp.float32)
-    got_above = lax.ppermute(for_below.astype(jnp.bfloat16), "dp", down).astype(jnp.float32)
+    early_up = lax.ppermute(for_above[half:].astype(jnp.bfloat16), "dp", up).astype(jnp.float32)
+    early_down = lax.ppermute(for_below[:half].astype(jnp.bfloat16), "dp", down).astype(jnp.float32)
     for_far = serve(far_rows).astype(jnp.bfloat16)
-    hop_up = lax.ppermute(for_far[:half], "dp", up)
-    hop_down = lax.ppermute(for_far[half:], "dp", down)
-    far_got = jnp.concatenate(
-        [lax.ppermute(hop_up, "dp", up), lax.ppermute(hop_down, "dp", down)], axis=0
-    ).astype(jnp.float32)
-    summed = for_own + got_below + got_above + far_got
+    far_up = lax.ppermute(for_far[:half], "dp", up).astype(jnp.float32)
+    far_down = lax.ppermute(for_far[half:], "dp", down).astype(jnp.float32)
+    late_up = lax.ppermute((for_above[:half] + far_up).astype(jnp.bfloat16), "dp", up)
+    late_down = lax.ppermute((for_below[half:] + far_down).astype(jnp.bfloat16), "dp", down)
+    summed = for_own + jnp.concatenate(
+        [late_up.astype(jnp.float32) + early_down, early_up + late_down.astype(jnp.float32)], axis=0
+    )
     served = summed.astype(jnp.bfloat16).reshape(arrived_shape)
     returned_rows = lax.all_to_all(
         served, ("seq", "expert"), split_axis=0, concat_axis=0, tiled=True

time: 178 us -> 177 us (level)
  local copies, waits for them, and re-layouts: 16.2 us -> 18.8 us
  starting transfers between devices: 28.1 us -> 26 us
  transfers between devices with their start and end apart: 13 -> 13, of which waited for: 6 -> 7; matrix products, arithmetic and copies ran while one was open for 20% -> 17% of each run, Pallas kernels for 0% -> 0%
where the time goes in v9:
time: 177 us
  waiting for transfers between devices  51.7 us (29%)
  blocking collectives  36.4 us (21%)
  matrix products  35.5 us (20%)
  starting transfers between devices  26 us (15%)
  local copies, waits for them, and re-layouts  18.8 us (11%)
  other arithmetic  7.03 us (4%)
    all_to_all x1, blocking collectives, local(): lax.all_to_all(outgoing, ('seq', 'expert'), split_axis=0, concat_axis=0,...  36.4 us
    all_to_all x1, waiting for transfers between devices, local(): lax.all_to_all(served, ('seq', 'expert'), split_axis=0, concat_axis=0, ti...  22.7 us
    dot_general x3, matrix products, serve(): lax.dot_general(hidden, down_local, (((1,), (1,)), ((), ())), preferred_e...  19.8 us
    ppermute x1, waiting for transfers between devices, local(): lax.ppermute((for_above[:half] + far_up).astype(jnp.bfloat16), 'dp', up)  9.44 us
    all_to_all x1, starting transfers between devices, local(): lax.all_to_all(served, ('seq', 'expert'), split_axis=0, concat_axis=0, ti...  8.8 us
    ppermute x1, waiting for transfers between devices, local(): from_above = lax.ppermute(own_rows, 'dp', down)  7.2 us
    dot_general x2, matrix products, serve(): gate_part = jnp.dot(rows, gate_local, preferred_element_type=jnp.float32)  5.5 us
    ppermute x1, starting transfers between devices, local(): before = lax.ppermute(gated[token_count - reach:], 'seq', seq_up)  4.36 us
  transfers between devices with their start and end apart: 13, of which 7 were waited for; matrix products, arithmetic and copies ran while one was open for 17% of the time, Pallas kernels for 0%

profile of v9, /device:TPU:1, one launch (start us, length us, event | category | flops | bytes accessed | tf_op | source)
XLA Modules:
  0.0 176.8 jit_solution(12040365482126492898)
XLA Ops:
  3.1 3.1 %fusion.54 = f32[128,2048]{1,0:T(8,128)S(1)} fusion(bf16[1024,2048]{1,0:T(8,128)(2,1)} %param.18, bf16[1,128,1024]{2,1,0:T(8,128)(2,1)} %param.14, f32[1024]{0:T(1024)} %param.17, f32[128]{0:T(128)S(1)} %add_rsqrt_fusion.1, f32[128]{0:T(128)S(1)} %broadcast_multiply_fusion.1), kind=kOutput, calls=%fused_computation.89 | convolution fusion | flops 537526272 | bytes 5510144 | tf_op jit(solution)/shard_map/dot_general | solution.py:36
  6.4 4.4 %collective-permute-start = (bf16[15,1024]{1,0:T(8,128)(2,1)S(1)}, bf16[15,1024]{1,0:T(8,128)(2,1)S(1)}, u32[]{:S(2)}, u32[]{:S(2)}) collective-permute-start(bf16[15,1024]{1,0:T(8,128)(2,1)S(1)} %get-tuple-element.27), channel_id=1, source_target_pairs={{0,8},{8,16},{16,24},{24,32},{32,40},{40,48},{48,56},{1,9},{9,17},... | collective-permute-start | bytes 92168 | tf_op jit(solution)/shard_map/ppermute | solution.py:45
  12.7 1.5 multiply_add_fusion
  20.5 36.4 %all_to_all.10 = bf16[64,48,128]{2,1,0:T(8,128)(2,1)} all-to-all(bf16[64,48,128]{2,1,0:T(8,128)(2,1)S(1)} %reshape.67), channel_id=1, replica_groups=mesh['dp'=4,'seq'=8,'expert'=8] {'seq','expert'}, dimensions={0} | all-to-all | bytes 1572864 | tf_op jit(solution)/shard_map/all_to_all | solution.py:90
  56.9 2.2 %reshape.68 = bf16[384,1024]{1,0:T(8,128)(2,1)} reshape(bf16[64,48,128]{2,1,0:T(8,128)(2,1)} %all_to_all.10) | data formatting | bytes 1572864 | tf_op jit(solution)/shard_map/reshape | solution.py:92
  59.1 2.7 %collective-permute-start.3 = (bf16[384,1024]{1,0:T(8,128)(2,1)}, bf16[384,1024]{1,0:T(8,128)(2,1)S(1)}, u32[]{:S(2)}, u32[]{:S(2)}) collective-permute-start(bf16[384,1024]{1,0:T(8,128)(2,1)} %reshape.68), channel_id=1, source_target_pairs={{0,192},{64,0},{128,64},{192,128},{1,193},{65,1},{129,65},{193,129... | collective-permute-start | bytes 2359304 | tf_op jit(solution)/shard_map/ppermute | solution.py:107
  61.8 3.3 %fusion.16 = f32[384,1024]{1,0:T(8,128)} fusion(bf16[384,1024]{1,0:T(8,128)(2,1)} %reshape.68, bf16[1,1024,1024]{2,1,0:T(8,128)(2,1)S(1)} %copy-done), kind=kOutput, calls=%fused_computation.17 | convolution fusion | flops 805306368 | bytes 4456448 | tf_op jit(solution)/shard_map/dot_general | solution.py:95
  65.2 6.0 %fusion.4 = f32[384,1024]{1,0:T(8,128)} fusion(bf16[1,1024,1024]{2,1,0:T(8,128)(2,1)} %param.27, f32[384,1024]{1,0:T(8,128)} %fusion.16, bf16[384,1024]{1,0:T(8,128)(2,1)} %reshape.68, bf16[1,1024,1024]{2,1,0:T(8,128)(2,1)} %param.26), kind=kOutput, calls=%fused_computation.5 | convolution fusion | flops 1612972032 | bytes 8126464 | tf_op jit(solution)/shard_map/dot_general | solution.py:98
  71.1 7.2 %collective-permute-done.3 = bf16[384,1024]{1,0:T(8,128)(2,1)S(1)} collective-permute-done((bf16[384,1024]{1,0:T(8,128)(2,1)}, bf16[384,1024]{1,0:T(8,128)(2,1)S(1)}, u32[]{:S(2)}, u32[]{:S(2)}) %collective-permute-start.3) | collective-permute-done | bytes 786464 | tf_op jit(solution)/shard_map/ppermute | solution.py:107
  78.3 3.1 %collective-permute-done.2 = bf16[384,1024]{1,0:T(8,128)(2,1)} collective-permute-done((bf16[384,1024]{1,0:T(8,128)(2,1)}, bf16[384,1024]{1,0:T(8,128)(2,1)}, u32[]{:S(2)}, u32[]{:S(2)}) %collective-permute-start.2) | collective-permute-done | bytes 786464 | tf_op jit(solution)/shard_map/ppermute | solution.py:106
  81.5 1.8 %slice.642 = bf16[192,1024]{1,0:T(8,128)(2,1)} slice(bf16[384,1024]{1,0:T(8,128)(2,1)} %collective-permute-done.2), slice={[0:192], [0:1024]} | slice | bytes 786432 | tf_op jit(solution)/shard_map/slice | solution.py:111
  88.0 3.5 %fusion.8 = f32[768,1024]{1,0:T(8,128)} fusion(bf16[768,1024]{1,0:T(8,128)(2,1)S(1)} %constant_dynamic-update-slice_fusion, bf16[1,1024,1024]{2,1,0:T(8,128)(2,1)S(1)} %copy-done.15), kind=kOutput, calls=%fused_computation.9 | convolution fusion | flops 1610612736 | bytes 6815744 | tf_op jit(solution)/shard_map/dot_general | solution.py:96
  91.5 8.4 %fusion.2 = f32[768,1024]{1,0:T(8,128)} fusion(bf16[1,1024,1024]{2,1,0:T(8,128)(2,1)} %param.27, f32[768,1024]{1,0:T(8,128)} %fusion.8, bf16[768,1024]{1,0:T(8,128)(2,1)} %copy-done.7, bf16[1,1024,1024]{2,1,0:T(8,128)(2,1)S(1)} %copy-done), kind=kOutput, calls=%fused_computation.3 | convolution fusion | flops 3225944064 | bytes 12058624 | tf_op jit(solution)/shard_map/dot_general | solution.py:98
  99.9 4.0 %fusion.108 = (f32[384,1024]{1,0:T(8,128)}, f32[384,1024]{1,0:T(8,128)}) fusion(f32[768,1024]{1,0:T(8,128)} %fusion.2), kind=kLoop, calls=%fused_computation.192 | loop fusion | bytes 6291456 | tf_op jit(solution)/shard_map/slice | solution.py:114
  105.0 2.2 %fusion.12 = f32[384,1024]{1,0:T(8,128)} fusion(bf16[384,1024]{1,0:T(8,128)(2,1)S(1)} %pad_maximum_fusion, bf16[1,1024,1024]{2,1,0:T(8,128)(2,1)S(1)} %copy-done), kind=kOutput, calls=%fused_computation.13 | convolution fusion | flops 805306368 | bytes 4456448 | tf_op jit(solution)/shard_map/dot_general | solution.py:95
  107.2 5.5 %fusion.27 = bf16[384,1024]{1,0:T(8,128)(2,1)} fusion(bf16[1,1024,1024]{2,1,0:T(8,128)(2,1)} %param.27, f32[384,1024]{1,0:T(8,128)} %fusion.12, bf16[384,1024]{1,0:T(8,128)(2,1)S(1)} %pad_maximum_fusion, bf16[1,1024,1024]{2,1,0:T(8,128)(2,1)} %param.26), kind=kOutput, calls=%fused_computation.24 | convolution fusion | flops 1613365248 | bytes 7340032 | tf_op jit(solution)/shard_map/dot_general | solution.py:98
  114.0 2.7 %collective-permute-start.10 = (bf16[192,1024]{1,0:T(8,128)(2,1)S(1)}, bf16[192,1024]{1,0:T(8,128)(2,1)S(1)}, u32[]{:S(2)}, u32[]{:S(2)}) collective-permute-start(bf16[192,1024]{1,0:T(8,128)(2,1)S(1)} %get-tuple-element.24), channel_id=1, source_target_pairs={{0,192},{64,0},{128,64},{192,128},{1,193},{65,1},{129,65},{193,129... | collective-permute-start | bytes 1179656 | tf_op jit(solution)/shard_map/ppermute | solution.py:120
  119.5 4.0 %collective-permute-done.6 = bf16[192,1024]{1,0:T(8,128)(2,1)S(1)} collective-permute-done((bf16[192,1024]{1,0:T(8,128)(2,1)S(1)}, bf16[192,1024]{1,0:T(8,128)(2,1)S(1)}, u32[]{:S(2)}, u32[]{:S(2)}) %collective-permute-start.6) | collective-permute-done | bytes 393248 | tf_op jit(solution)/shard_map/ppermute | solution.py:119
  123.8 2.9 %collective-permute-start.11 = (bf16[192,1024]{1,0:T(8,128)(2,1)S(1)}, bf16[192,1024]{1,0:T(8,128)(2,1)S(1)}, u32[]{:S(2)}, u32[]{:S(2)}) collective-permute-start(bf16[192,1024]{1,0:T(8,128)(2,1)S(1)} %add_convert_fusion), channel_id=1, source_target_pairs={{0,192},{64,0},{128,64},{192,128},{1,193},{65,1},{129,65},{193,129... | collective-permute-start | bytes 1179656 | tf_op jit(solution)/shard_map/ppermute | solution.py:122
  126.8 4.2 %collective-permute-done.8 = bf16[192,1024]{1,0:T(8,128)(2,1)S(1)} collective-permute-done((bf16[192,1024]{1,0:T(8,128)(2,1)S(1)}, bf16[192,1024]{1,0:T(8,128)(2,1)S(1)}, u32[]{:S(2)}, u32[]{:S(2)}) %collective-permute-start.8) | collective-permute-done | bytes 393248 | tf_op jit(solution)/shard_map/ppermute | solution.py:117
  130.9 9.4 %collective-permute-done.7 = bf16[192,1024]{1,0:T(8,128)(2,1)S(1)} collective-permute-done((bf16[192,1024]{1,0:T(8,128)(2,1)S(1)}, bf16[192,1024]{1,0:T(8,128)(2,1)S(1)}, u32[]{:S(2)}, u32[]{:S(2)}) %collective-permute-start.7) | collective-permute-done | bytes 393248 | tf_op jit(solution)/shard_map/ppermute | solution.py:121
  142.2 8.8 %all-to-all-start.1 = ((bf16[64,48,128]{2,1,0:T(8,128)(2,1)}), bf16[64,48,128]{2,1,0:T(8,128)(2,1)}, u32[]{:S(2)}, u32[]{:S(2)}) async-start(bf16[64,48,128]{2,1,0:T(8,128)(2,1)} %reshape.69), calls=%async_computation.1 | async-start | bytes 1572864 | tf_op jit(solution)/shard_map/all_to_all | solution.py:127
  151.3 22.7 %all-to-all-done.1 = bf16[64,48,128]{2,1,0:T(8,128)(2,1)} async-done(((bf16[64,48,128]{2,1,0:T(8,128)(2,1)}), bf16[64,48,128]{2,1,0:T(8,128)(2,1)}, u32[]{:S(2)}, u32[]{:S(2)}) %all-to-all-start.1) | async-done | bytes 786464 | tf_op jit(solution)/shard_map/all_to_all | solution.py:127
  174.0 1.4 reshape.70
  (94 shorter events, 24.3 us)
Async XLA Ops:
  0.0 61.8 %copy-start = (bf16[1,1024,1024]{2,1,0:T(8,128)(2,1)S(1)}, bf16[1,1024,1024]{2,1,0:T(8,128)(2,1)}, u32[]{:S(2)}) copy-start(bf16[1,1024,1024]{2,1,0:T(8,128)(2,1)} %param.25) | copy-start | bytes 6291460
  3.1 9.0 %copy-start.9 = (f32[31,1024]{1,0:T(8,128)S(1)}, f32[31,1024]{1,0:T(8,128)}, u32[]{:S(2)}) copy-start(f32[31,1024]{1,0:T(8,128)} %param.19) | copy-start | bytes 380932
  6.2 6.0 %copy-start.11 = (s32[1,128,2]{1,2,0:T(2,128)S(1)}, s32[1,128,2]{1,2,0:T(2,128)}, u32[]{:S(2)}) copy-start(s32[1,128,2]{1,2,0:T(2,128)} %param.16) | copy-start | bytes 3076
  6.4 7.8 %collective-permute-start = (bf16[15,1024]{1,0:T(8,128)(2,1)S(1)}, bf16[15,1024]{1,0:T(8,128)(2,1)S(1)}, u32[]{:S(2)}, u32[]{:S(2)}) collective-permute-start(bf16[15,1024]{1,0:T(8,128)(2,1)S(1)} %get-tuple-element.27), channel_id=1, source_target_pairs={{0,8},{8,16},{16,24},{24,32},{32,40},{40,48},{48,56},{1,9},{9,17},... | collective-permute-start | bytes 92168 | tf_op jit(solution)/shard_map/ppermute | solution.py:45
  10.8 4.8 %collective-permute-start.1 = (bf16[15,1024]{1,0:T(8,128)(2,1)S(1)}, bf16[15,1024]{1,0:T(8,128)(2,1)S(1)}, u32[]{:S(2)}, u32[]{:S(2)}) collective-permute-start(bf16[15,1024]{1,0:T(8,128)(2,1)S(1)} %get-tuple-element.28), channel_id=1, source_target_pairs={{8,0},{16,8},{24,16},{32,24},{40,32},{48,40},{56,48},{9,1},{17,9},... | collective-permute-start | bytes 92168 | tf_op jit(solution)/shard_map/ppermute | solution.py:46
  12.7 3.3 %copy-start.14 = (bf16[1024,1024]{1,0:T(8,128)(2,1)S(1)}, bf16[1024,1024]{1,0:T(8,128)(2,1)}, u32[]{:S(2)}) copy-start(bf16[1024,1024]{1,0:T(8,128)(2,1)} %param.22) | copy-start | bytes 6291460
  59.1 19.3 %collective-permute-start.3 = (bf16[384,1024]{1,0:T(8,128)(2,1)}, bf16[384,1024]{1,0:T(8,128)(2,1)S(1)}, u32[]{:S(2)}, u32[]{:S(2)}) collective-permute-start(bf16[384,1024]{1,0:T(8,128)(2,1)} %reshape.68), channel_id=1, source_target_pairs={{0,192},{64,0},{128,64},{192,128},{1,193},{65,1},{129,65},{193,129... | collective-permute-start | bytes 2359304 | tf_op jit(solution)/shard_map/ppermute | solution.py:107
  61.8 19.6 %collective-permute-start.2 = (bf16[384,1024]{1,0:T(8,128)(2,1)}, bf16[384,1024]{1,0:T(8,128)(2,1)}, u32[]{:S(2)}, u32[]{:S(2)}) collective-permute-start(bf16[384,1024]{1,0:T(8,128)(2,1)} %reshape.68), channel_id=1, source_target_pairs={{0,64},{64,128},{128,192},{192,0},{1,65},{65,129},{129,193},{193,1... | collective-permute-start | bytes 2359304 | tf_op jit(solution)/shard_map/ppermute | solution.py:106
  84.4 3.6 %copy-start.15 = (bf16[1,1024,1024]{2,1,0:T(8,128)(2,1)S(1)}, bf16[1,1024,1024]{2,1,0:T(8,128)(2,1)}, u32[]{:S(2)}) copy-start(bf16[1,1024,1024]{2,1,0:T(8,128)(2,1)} %param.26) | copy-start | bytes 6291460
  85.2 18.6 %collective-permute-start.5 = (bf16[192,1024]{1,0:T(8,128)(2,1)}, bf16[192,1024]{1,0:T(8,128)(2,1)}, u32[]{:S(2)}, u32[]{:S(2)}) collective-permute-start(bf16[192,1024]{1,0:T(8,128)(2,1)} %slice.643), channel_id=1, source_target_pairs={{0,192},{64,0},{128,64},{192,128},{1,193},{65,1},{129,65},{193,129... | collective-permute-start | bytes 1179656 | tf_op jit(solution)/shard_map/ppermute | solution.py:111
  85.4 18.4 %collective-permute-start.4 = (bf16[192,1024]{1,0:T(8,128)(2,1)}, bf16[192,1024]{1,0:T(8,128)(2,1)}, u32[]{:S(2)}, u32[]{:S(2)}) collective-permute-start(bf16[192,1024]{1,0:T(8,128)(2,1)} %slice.642), channel_id=1, source_target_pairs={{0,64},{64,128},{128,192},{192,0},{1,65},{65,129},{129,193},{193,1... | collective-permute-start | bytes 1179656 | tf_op jit(solution)/shard_map/ppermute | solution.py:111
  112.7 4.0 %copy-start.1 = (f32[384,1024]{1,0:T(8,128)S(1)}, f32[384,1024]{1,0:T(8,128)}, u32[]{:S(2)}) copy-start(f32[384,1024]{1,0:T(8,128)} %get-tuple-element.14) | copy-start | bytes 4718596
  113.9 9.6 %collective-permute-start.6 = (bf16[192,1024]{1,0:T(8,128)(2,1)S(1)}, bf16[192,1024]{1,0:T(8,128)(2,1)S(1)}, u32[]{:S(2)}, u32[]{:S(2)}) collective-permute-start(bf16[192,1024]{1,0:T(8,128)(2,1)S(1)} %get-tuple-element.23), channel_id=1, source_target_pairs={{0,64},{64,128},{128,192},{192,0},{1,65},{65,129},{129,193},{193,1... | collective-permute-start | bytes 1179656 | tf_op jit(solution)/shard_map/ppermute | solution.py:119
  114.0 9.7 %copy-start.2 = (f32[384,1024]{1,0:T(8,128)S(1)}, f32[384,1024]{1,0:T(8,128)}, u32[]{:S(2)}) copy-start(f32[384,1024]{1,0:T(8,128)} %get-tuple-element.16) | copy-start | bytes 4718596
  114.0 9.6 %collective-permute-start.10 = (bf16[192,1024]{1,0:T(8,128)(2,1)S(1)}, bf16[192,1024]{1,0:T(8,128)(2,1)S(1)}, u32[]{:S(2)}, u32[]{:S(2)}) collective-permute-start(bf16[192,1024]{1,0:T(8,128)(2,1)S(1)} %get-tuple-element.24), channel_id=1, source_target_pairs={{0,192},{64,0},{128,64},{192,128},{1,193},{65,1},{129,65},{193,129... | collective-permute-start | bytes 1179656 | tf_op jit(solution)/shard_map/ppermute | solution.py:120
  117.9 13.0 %collective-permute-start.8 = (bf16[192,1024]{1,0:T(8,128)(2,1)S(1)}, bf16[192,1024]{1,0:T(8,128)(2,1)S(1)}, u32[]{:S(2)}, u32[]{:S(2)}) collective-permute-start(bf16[192,1024]{1,0:T(8,128)(2,1)S(1)} %slice.1073), channel_id=1, source_target_pairs={{0,192},{64,0},{128,64},{192,128},{1,193},{65,1},{129,65},{193,129... | collective-permute-start | bytes 1179656 | tf_op jit(solution)/shard_map/ppermute | solution.py:117
  118.3 22.2 %collective-permute-start.9 = (bf16[192,1024]{1,0:T(8,128)(2,1)S(1)}, bf16[192,1024]{1,0:T(8,128)(2,1)S(1)}, u32[]{:S(2)}, u32[]{:S(2)}) collective-permute-start(bf16[192,1024]{1,0:T(8,128)(2,1)S(1)} %slice.1072), channel_id=1, source_target_pairs={{0,64},{64,128},{128,192},{192,0},{1,65},{65,129},{129,193},{193,1... | collective-permute-start | bytes 1179656 | tf_op jit(solution)/shard_map/ppermute | solution.py:116
  123.6 16.8 %collective-permute-start.7 = (bf16[192,1024]{1,0:T(8,128)(2,1)S(1)}, bf16[192,1024]{1,0:T(8,128)(2,1)S(1)}, u32[]{:S(2)}, u32[]{:S(2)}) collective-permute-start(bf16[192,1024]{1,0:T(8,128)(2,1)S(1)} %add_convert_fusion.1), channel_id=1, source_target_pairs={{0,64},{64,128},{128,192},{192,0},{1,65},{65,129},{129,193},{193,1... | collective-permute-start | bytes 1179656 | tf_op jit(solution)/shard_map/ppermute | solution.py:121
  123.8 16.8 %copy-start.6 = (f32[384,1024]{1,0:T(8,128)S(1)}, f32[384,1024]{1,0:T(8,128)}, u32[]{:S(2)}) copy-start(f32[384,1024]{1,0:T(8,128)} %fusion.4) | copy-start | bytes 4718596
  123.8 16.7 %collective-permute-start.11 = (bf16[192,1024]{1,0:T(8,128)(2,1)S(1)}, bf16[192,1024]{1,0:T(8,128)(2,1)S(1)}, u32[]{:S(2)}, u32[]{:S(2)}) collective-permute-start(bf16[192,1024]{1,0:T(8,128)(2,1)S(1)} %add_convert_fusion), channel_id=1, source_target_pairs={{0,192},{64,0},{128,64},{192,128},{1,193},{65,1},{129,65},{193,129... | collective-permute-start | bytes 1179656 | tf_op jit(solution)/shard_map/ppermute | solution.py:122
  141.0 10.1 %copy-start.8 = (bf16[1024,64]{0,1:T(8,128)(2,1)S(1)}, bf16[1024,64]{0,1:T(8,128)(2,1)}, u32[]{:S(2)}) copy-start(bf16[1024,64]{0,1:T(8,128)(2,1)} %param.24) | copy-start | bytes 393220
  142.2 8.8 %copy-start.4 = (bf16[128,1024]{1,0:T(8,128)(2,1)S(1)}, bf16[128,1024]{1,0:T(8,128)(2,1)}, u32[]{:S(2)}) copy-start(bf16[128,1024]{1,0:T(8,128)(2,1)} %copy-done.3) | copy-start | bytes 786436
  142.2 31.7 %all-to-all-start.1 = ((bf16[64,48,128]{2,1,0:T(8,128)(2,1)}), bf16[64,48,128]{2,1,0:T(8,128)(2,1)}, u32[]{:S(2)}, u32[]{:S(2)}) async-start(bf16[64,48,128]{2,1,0:T(8,128)(2,1)} %reshape.69), calls=%async_computation.1 | async-start | bytes 1572864 | tf_op jit(solution)/shard_map/all_to_all | solution.py:127
  151.3 24.5 %copy-start.13 = (f32[128]{0:T(128)S(1)}, f32[128]{0:T(128)}, u32[]{:S(2)}) copy-start(f32[128]{0:T(128)} %copy-done.12) | copy-start | bytes 1540
  (7 other events, 11.4 us)

commit v10 on v9

--- a/solution.py
+++ b/solution.py
@@ -120,10 +120,12 @@
     far_down = lax.ppermute(for_far[half:], "dp", down).astype(jnp.float32)
     late_up = lax.ppermute((for_above[:half] + far_up).astype(jnp.bfloat16), "dp", up)
     late_down = lax.ppermute((for_below[half:] + far_down).astype(jnp.bfloat16), "dp", down)
-    summed = for_own + jnp.concatenate(
-        [late_up.astype(jnp.float32) + early_down, early_up + late_down.astype(jnp.float32)], axis=0
+    parts = (
+        for_own,
+        jnp.concatenate([late_up.astype(jnp.float32), early_up], axis=0),
+        jnp.concatenate([early_down, late_down.astype(jnp.float32)], axis=0),
     )
-    served = summed.astype(jnp.bfloat16).reshape(arrived_shape)
+    served = sum(part.reshape(arrived_shape) for part in parts).astype(jnp.bfloat16)
     returned_rows = lax.all_to_all(
         served, ("seq", "expert"), split_axis=0, concat_axis=0, tiled=True
     )

time: 177 us -> 179 us (1.011)
    ppermute x1, waiting for transfers between devices: 9.44 us -> 2.61 us  [local(): lax.ppermute((for_above[:half] + far_up).astype(jnp.bfloat16), 'dp', up)]
    ppermute x1, waiting for transfers between devices: 0.01 us -> 5.82 us  [local(): lax.ppermute((for_below[half:] + far_down).astype(jnp.bfloat16), 'dp', down)]
    ppermute x1, waiting for transfers between devices: 4.02 us -> 0.01 us  [local(): far_up = lax.ppermute(for_far[:half], 'dp', up).astype(jnp.float32)]
    ppermute x1, waiting for transfers between devices: 0.01 us -> 2.87 us  [local(): far_down = lax.ppermute(for_far[half:], 'dp', down).astype(jnp.float32)]
    ppermute x1, waiting for transfers between devices: 0.01 us -> 2.6 us  [local(): lax.ppermute(for_above[half:].astype(jnp.bfloat16), 'dp', up)]
    ppermute x1, starting transfers between devices: 0.37 us -> 2.68 us  [local(): lax.ppermute(for_below[:half].astype(jnp.bfloat16), 'dp', down)]
  transfers between devices with their start and end apart: 13 -> 13, of which waited for: 7 -> 9; matrix products, arithmetic and copies ran while one was open for 17% -> 16% of each run, Pallas kernels for 0% -> 0%
where the time goes in v10:
time: 179 us; the launch traced here: 178 us
  waiting for transfers between devices  53 us (30%)
  blocking collectives  36.4 us (20%)
  matrix products  35.5 us (20%)
  starting transfers between devices  26.1 us (15%)
  local copies, waits for them, and re-layouts  18.9 us (11%)
  other arithmetic  6.87 us (4%)
    all_to_all x1, blocking collectives, local(): lax.all_to_all(outgoing, ('seq', 'expert'), split_axis=0, concat_axis=0,...  36.4 us
    all_to_all x1, waiting for transfers between devices, local(): lax.all_to_all(served, ('seq', 'expert'), split_axis=0, concat_axis=0, ti...  22.7 us
    dot_general x3, matrix products, serve(): lax.dot_general(hidden, down_local, (((1,), (1,)), ((), ())), preferred_e...  19.8 us
    all_to_all x1, starting transfers between devices, local(): lax.all_to_all(served, ('seq', 'expert'), split_axis=0, concat_axis=0, ti...  8.79 us
    ppermute x1, waiting for transfers between devices, local(): from_above = lax.ppermute(own_rows, 'dp', down)  7.2 us
    ppermute x1, waiting for transfers between devices, local(): lax.ppermute((for_below[half:] + far_down).astype(jnp.bfloat16), 'dp', down)  5.82 us
    dot_general x2, matrix products, serve(): gate_part = jnp.dot(rows, gate_local, preferred_element_type=jnp.float32)  5.5 us
    ppermute x1, waiting for transfers between devices, local(): lax.ppermute(for_below[:half].astype(jnp.bfloat16), 'dp', down)  4.96 us
  transfers between devices with their start and end apart: 13, of which 9 were waited for; matrix products, arithmetic and copies ran while one was open for 16% of the time, Pallas kernels for 0%

profile of v10, /device:TPU:1, one launch (start us, length us, event | category | flops | bytes accessed | tf_op | source)
XLA Modules:
  0.0 178.1 jit_solution(15247854844893311828)
XLA Ops:
  3.1 3.1 %fusion.53 = f32[128,2048]{1,0:T(8,128)S(1)} fusion(bf16[1024,2048]{1,0:T(8,128)(2,1)} %param.18, bf16[1,128,1024]{2,1,0:T(8,128)(2,1)} %param.14, f32[1024]{0:T(1024)} %param.17, f32[128]{0:T(128)S(1)} %add_rsqrt_fusion.1, f32[128]{0:T(128)S(1)} %broadcast_multiply_fusion.1), kind=kOutput, calls=%fused_computation.86 | convolution fusion | flops 537526272 | bytes 5510144 | tf_op jit(solution)/shard_map/dot_general | solution.py:36
  6.4 4.4 %collective-permute-start = (bf16[15,1024]{1,0:T(8,128)(2,1)S(1)}, bf16[15,1024]{1,0:T(8,128)(2,1)S(1)}, u32[]{:S(2)}, u32[]{:S(2)}) collective-permute-start(bf16[15,1024]{1,0:T(8,128)(2,1)S(1)} %get-tuple-element.27), channel_id=1, source_target_pairs={{0,8},{8,16},{16,24},{24,32},{32,40},{40,48},{48,56},{1,9},{9,17},... | collective-permute-start | bytes 92168 | tf_op jit(solution)/shard_map/ppermute | solution.py:45
  20.5 36.4 %all_to_all.10 = bf16[64,48,128]{2,1,0:T(8,128)(2,1)} all-to-all(bf16[64,48,128]{2,1,0:T(8,128)(2,1)S(1)} %reshape.70), channel_id=1, replica_groups=mesh['dp'=4,'seq'=8,'expert'=8] {'seq','expert'}, dimensions={0} | all-to-all | bytes 1572864 | tf_op jit(solution)/shard_map/all_to_all | solution.py:90
  56.9 2.2 %reshape.71 = bf16[384,1024]{1,0:T(8,128)(2,1)} reshape(bf16[64,48,128]{2,1,0:T(8,128)(2,1)} %all_to_all.10) | data formatting | bytes 1572864 | tf_op jit(solution)/shard_map/reshape | solution.py:92
  59.1 2.7 %collective-permute-start.3 = (bf16[384,1024]{1,0:T(8,128)(2,1)}, bf16[384,1024]{1,0:T(8,128)(2,1)S(1)}, u32[]{:S(2)}, u32[]{:S(2)}) collective-permute-start(bf16[384,1024]{1,0:T(8,128)(2,1)} %reshape.71), channel_id=1, source_target_pairs={{0,192},{64,0},{128,64},{192,128},{1,193},{65,1},{129,65},{193,129... | collective-permute-start | bytes 2359304 | tf_op jit(solution)/shard_map/ppermute | solution.py:107
  61.8 3.3 %fusion.16 = f32[384,1024]{1,0:T(8,128)} fusion(bf16[384,1024]{1,0:T(8,128)(2,1)} %reshape.71, bf16[1,1024,1024]{2,1,0:T(8,128)(2,1)S(1)} %copy-done), kind=kOutput, calls=%fused_computation.17 | convolution fusion | flops 805306368 | bytes 4456448 | tf_op jit(solution)/shard_map/dot_general | solution.py:95
  65.2 6.0 %fusion.4 = f32[384,1024]{1,0:T(8,128)} fusion(bf16[1,1024,1024]{2,1,0:T(8,128)(2,1)} %param.27, f32[384,1024]{1,0:T(8,128)} %fusion.16, bf16[384,1024]{1,0:T(8,128)(2,1)} %reshape.71, bf16[1,1024,1024]{2,1,0:T(8,128)(2,1)} %param.26), kind=kOutput, calls=%fused_computation.5 | convolution fusion | flops 1612972032 | bytes 8126464 | tf_op jit(solution)/shard_map/dot_general | solution.py:98
  71.1 7.2 %collective-permute-done.3 = bf16[384,1024]{1,0:T(8,128)(2,1)S(1)} collective-permute-done((bf16[384,1024]{1,0:T(8,128)(2,1)}, bf16[384,1024]{1,0:T(8,128)(2,1)S(1)}, u32[]{:S(2)}, u32[]{:S(2)}) %collective-permute-start.3) | collective-permute-done | bytes 786464 | tf_op jit(solution)/shard_map/ppermute | solution.py:107
  78.3 3.1 %collective-permute-done.2 = bf16[384,1024]{1,0:T(8,128)(2,1)} collective-permute-done((bf16[384,1024]{1,0:T(8,128)(2,1)}, bf16[384,1024]{1,0:T(8,128)(2,1)}, u32[]{:S(2)}, u32[]{:S(2)}) %collective-permute-start.2) | collective-permute-done | bytes 786464 | tf_op jit(solution)/shard_map/ppermute | solution.py:106
  81.5 1.8 %slice.642 = bf16[192,1024]{1,0:T(8,128)(2,1)} slice(bf16[384,1024]{1,0:T(8,128)(2,1)} %collective-permute-done.2), slice={[0:192], [0:1024]} | slice | bytes 786432 | tf_op jit(solution)/shard_map/slice | solution.py:111
  88.0 3.5 %fusion.8 = f32[768,1024]{1,0:T(8,128)} fusion(bf16[768,1024]{1,0:T(8,128)(2,1)S(1)} %constant_dynamic-update-slice_fusion, bf16[1,1024,1024]{2,1,0:T(8,128)(2,1)S(1)} %copy-done.15), kind=kOutput, calls=%fused_computation.9 | convolution fusion | flops 1610612736 | bytes 6815744 | tf_op jit(solution)/shard_map/dot_general | solution.py:96
  91.5 8.4 %fusion.2 = f32[768,1024]{1,0:T(8,128)} fusion(bf16[1,1024,1024]{2,1,0:T(8,128)(2,1)} %param.27, f32[768,1024]{1,0:T(8,128)} %fusion.8, bf16[768,1024]{1,0:T(8,128)(2,1)} %copy-done.7, bf16[1,1024,1024]{2,1,0:T(8,128)(2,1)S(1)} %copy-done), kind=kOutput, calls=%fused_computation.3 | convolution fusion | flops 3225944064 | bytes 12058624 | tf_op jit(solution)/shard_map/dot_general | solution.py:98
  99.9 4.0 %fusion.107 = (f32[384,1024]{1,0:T(8,128)}, f32[384,1024]{1,0:T(8,128)}) fusion(f32[768,1024]{1,0:T(8,128)} %fusion.2), kind=kLoop, calls=%fused_computation.189 | loop fusion | bytes 6291456 | tf_op jit(solution)/shard_map/slice | solution.py:114
  105.0 2.2 %fusion.12 = f32[384,1024]{1,0:T(8,128)} fusion(bf16[384,1024]{1,0:T(8,128)(2,1)S(1)} %pad_maximum_fusion, bf16[1,1024,1024]{2,1,0:T(8,128)(2,1)S(1)} %copy-done), kind=kOutput, calls=%fused_computation.13 | convolution fusion | flops 805306368 | bytes 4456448 | tf_op jit(solution)/shard_map/dot_general | solution.py:95
  107.2 5.5 %fusion.26 = bf16[384,1024]{1,0:T(8,128)(2,1)} fusion(bf16[1,1024,1024]{2,1,0:T(8,128)(2,1)} %param.27, f32[384,1024]{1,0:T(8,128)} %fusion.12, bf16[384,1024]{1,0:T(8,128)(2,1)S(1)} %pad_maximum_fusion, bf16[1,1024,1024]{2,1,0:T(8,128)(2,1)} %param.26), kind=kOutput, calls=%fused_computation.23 | convolution fusion | flops 1613365248 | bytes 7340032 | tf_op jit(solution)/shard_map/dot_general | solution.py:98
  116.8 2.7 %collective-permute-start.9 = (bf16[192,1024]{1,0:T(8,128)(2,1)S(1)}, bf16[192,1024]{1,0:T(8,128)(2,1)S(1)}, u32[]{:S(2)}, u32[]{:S(2)}) collective-permute-start(bf16[192,1024]{1,0:T(8,128)(2,1)S(1)} %slice.1072), channel_id=1, source_target_pairs={{0,192},{64,0},{128,64},{192,128},{1,193},{65,1},{129,65},{193,129... | collective-permute-start | bytes 1179656 | tf_op jit(solution)/shard_map/ppermute | solution.py:117
  119.5 2.9 %collective-permute-done.10 = bf16[192,1024]{1,0:T(8,128)(2,1)S(1)} collective-permute-done((bf16[192,1024]{1,0:T(8,128)(2,1)S(1)}, bf16[192,1024]{1,0:T(8,128)(2,1)S(1)}, u32[]{:S(2)}, u32[]{:S(2)}) %collective-permute-start.10) | collective-permute-done | bytes 393248 | tf_op jit(solution)/shard_map/ppermute | solution.py:120
  122.4 3.0 %collective-permute-start.11 = (bf16[192,1024]{1,0:T(8,128)(2,1)S(1)}, bf16[192,1024]{1,0:T(8,128)(2,1)S(1)}, u32[]{:S(2)}, u32[]{:S(2)}) collective-permute-start(bf16[192,1024]{1,0:T(8,128)(2,1)S(1)} %add_convert_fusion.1), channel_id=1, source_target_pairs={{0,192},{64,0},{128,64},{192,128},{1,193},{65,1},{129,65},{193,129... | collective-permute-start | bytes 1179656 | tf_op jit(solution)/shard_map/ppermute | solution.py:122
  125.8 5.0 %collective-permute-done.9 = bf16[192,1024]{1,0:T(8,128)(2,1)S(1)} collective-permute-done((bf16[192,1024]{1,0:T(8,128)(2,1)S(1)}, bf16[192,1024]{1,0:T(8,128)(2,1)S(1)}, u32[]{:S(2)}, u32[]{:S(2)}) %collective-permute-start.9) | collective-permute-done | bytes 393248 | tf_op jit(solution)/shard_map/ppermute | solution.py:117
  130.8 2.6 %collective-permute-done.8 = bf16[192,1024]{1,0:T(8,128)(2,1)S(1)} collective-permute-done((bf16[192,1024]{1,0:T(8,128)(2,1)S(1)}, bf16[192,1024]{1,0:T(8,128)(2,1)S(1)}, u32[]{:S(2)}, u32[]{:S(2)}) %collective-permute-start.8) | collective-permute-done | bytes 393248 | tf_op jit(solution)/shard_map/ppermute | solution.py:116
  133.4 5.8 %collective-permute-done.11 = bf16[192,1024]{1,0:T(8,128)(2,1)S(1)} collective-permute-done((bf16[192,1024]{1,0:T(8,128)(2,1)S(1)}, bf16[192,1024]{1,0:T(8,128)(2,1)S(1)}, u32[]{:S(2)}, u32[]{:S(2)}) %collective-permute-start.11) | collective-permute-done | bytes 393248 | tf_op jit(solution)/shard_map/ppermute | solution.py:122
  139.2 2.6 %collective-permute-done.7 = bf16[192,1024]{1,0:T(8,128)(2,1)S(1)} collective-permute-done((bf16[192,1024]{1,0:T(8,128)(2,1)S(1)}, bf16[192,1024]{1,0:T(8,128)(2,1)S(1)}, u32[]{:S(2)}, u32[]{:S(2)}) %collective-permute-start.7) | collective-permute-done | bytes 393248 | tf_op jit(solution)/shard_map/ppermute | solution.py:121
  143.5 8.8 %all-to-all-start.1 = ((bf16[64,48,128]{2,1,0:T(8,128)(2,1)}), bf16[64,48,128]{2,1,0:T(8,128)(2,1)}, u32[]{:S(2)}, u32[]{:S(2)}) async-start(bf16[64,48,128]{2,1,0:T(8,128)(2,1)} %convert_element_type.481), calls=%async_computation.1 | async-start | bytes 1572864 | tf_op jit(solution)/shard_map/all_to_all | solution.py:129
  152.5 22.7 %all-to-all-done.1 = bf16[64,48,128]{2,1,0:T(8,128)(2,1)} async-done(((bf16[64,48,128]{2,1,0:T(8,128)(2,1)}), bf16[64,48,128]{2,1,0:T(8,128)(2,1)}, u32[]{:S(2)}, u32[]{:S(2)}) %all-to-all-start.1) | async-done | bytes 786464 | tf_op jit(solution)/shard_map/all_to_all | solution.py:129
  (92 shorter events, 27.2 us)
Async XLA Ops:
  0.0 61.8 %copy-start = (bf16[1,1024,1024]{2,1,0:T(8,128)(2,1)S(1)}, bf16[1,1024,1024]{2,1,0:T(8,128)(2,1)}, u32[]{:S(2)}) copy-start(bf16[1,1024,1024]{2,1,0:T(8,128)(2,1)} %param.25) | copy-start | bytes 6291460
  3.1 3.1 %copy-start.12 = (f32[128]{0:T(128)}, f32[128]{0:T(128)S(1)}, u32[]{:S(2)}) copy-start(f32[128]{0:T(128)S(1)} %compare_convert_fusion) | copy-start | bytes 1540
  3.1 9.0 %copy-start.9 = (f32[31,1024]{1,0:T(8,128)S(1)}, f32[31,1024]{1,0:T(8,128)}, u32[]{:S(2)}) copy-start(f32[31,1024]{1,0:T(8,128)} %param.19) | copy-start | bytes 380932
  6.2 6.0 %copy-start.11 = (s32[1,128,2]{1,2,0:T(2,128)S(1)}, s32[1,128,2]{1,2,0:T(2,128)}, u32[]{:S(2)}) copy-start(s32[1,128,2]{1,2,0:T(2,128)} %param.16) | copy-start | bytes 3076
  6.4 7.8 %collective-permute-start = (bf16[15,1024]{1,0:T(8,128)(2,1)S(1)}, bf16[15,1024]{1,0:T(8,128)(2,1)S(1)}, u32[]{:S(2)}, u32[]{:S(2)}) collective-permute-start(bf16[15,1024]{1,0:T(8,128)(2,1)S(1)} %get-tuple-element.27), channel_id=1, source_target_pairs={{0,8},{8,16},{16,24},{24,32},{32,40},{40,48},{48,56},{1,9},{9,17},... | collective-permute-start | bytes 92168 | tf_op jit(solution)/shard_map/ppermute | solution.py:45
  10.8 4.8 %collective-permute-start.1 = (bf16[15,1024]{1,0:T(8,128)(2,1)S(1)}, bf16[15,1024]{1,0:T(8,128)(2,1)S(1)}, u32[]{:S(2)}, u32[]{:S(2)}) collective-permute-start(bf16[15,1024]{1,0:T(8,128)(2,1)S(1)} %get-tuple-element.28), channel_id=1, source_target_pairs={{8,0},{16,8},{24,16},{32,24},{40,32},{48,40},{56,48},{9,1},{17,9},... | collective-permute-start | bytes 92168 | tf_op jit(solution)/shard_map/ppermute | solution.py:46
  12.7 3.3 %copy-start.14 = (bf16[1024,1024]{1,0:T(8,128)(2,1)S(1)}, bf16[1024,1024]{1,0:T(8,128)(2,1)}, u32[]{:S(2)}) copy-start(bf16[1024,1024]{1,0:T(8,128)(2,1)} %param.22) | copy-start | bytes 6291460
  59.1 19.3 %collective-permute-start.3 = (bf16[384,1024]{1,0:T(8,128)(2,1)}, bf16[384,1024]{1,0:T(8,128)(2,1)S(1)}, u32[]{:S(2)}, u32[]{:S(2)}) collective-permute-start(bf16[384,1024]{1,0:T(8,128)(2,1)} %reshape.71), channel_id=1, source_target_pairs={{0,192},{64,0},{128,64},{192,128},{1,193},{65,1},{129,65},{193,129... | collective-permute-start | bytes 2359304 | tf_op jit(solution)/shard_map/ppermute | solution.py:107
  61.8 19.6 %collective-permute-start.2 = (bf16[384,1024]{1,0:T(8,128)(2,1)}, bf16[384,1024]{1,0:T(8,128)(2,1)}, u32[]{:S(2)}, u32[]{:S(2)}) collective-permute-start(bf16[384,1024]{1,0:T(8,128)(2,1)} %reshape.71), channel_id=1, source_target_pairs={{0,64},{64,128},{128,192},{192,0},{1,65},{65,129},{129,193},{193,1... | collective-permute-start | bytes 2359304 | tf_op jit(solution)/shard_map/ppermute | solution.py:106
  84.4 3.6 %copy-start.15 = (bf16[1,1024,1024]{2,1,0:T(8,128)(2,1)S(1)}, bf16[1,1024,1024]{2,1,0:T(8,128)(2,1)}, u32[]{:S(2)}) copy-start(bf16[1,1024,1024]{2,1,0:T(8,128)(2,1)} %param.26) | copy-start | bytes 6291460
  85.2 18.6 %collective-permute-start.5 = (bf16[192,1024]{1,0:T(8,128)(2,1)}, bf16[192,1024]{1,0:T(8,128)(2,1)}, u32[]{:S(2)}, u32[]{:S(2)}) collective-permute-start(bf16[192,1024]{1,0:T(8,128)(2,1)} %slice.643), channel_id=1, source_target_pairs={{0,192},{64,0},{128,64},{192,128},{1,193},{65,1},{129,65},{193,129... | collective-permute-start | bytes 1179656 | tf_op jit(solution)/shard_map/ppermute | solution.py:111
  85.4 18.4 %collective-permute-start.4 = (bf16[192,1024]{1,0:T(8,128)(2,1)}, bf16[192,1024]{1,0:T(8,128)(2,1)}, u32[]{:S(2)}, u32[]{:S(2)}) collective-permute-start(bf16[192,1024]{1,0:T(8,128)(2,1)} %slice.642), channel_id=1, source_target_pairs={{0,64},{64,128},{128,192},{192,0},{1,65},{65,129},{129,193},{193,1... | collective-permute-start | bytes 1179656 | tf_op jit(solution)/shard_map/ppermute | solution.py:111
  112.7 9.7 %copy-start.2 = (f32[384,1024]{1,0:T(8,128)S(1)}, f32[384,1024]{1,0:T(8,128)}, u32[]{:S(2)}) copy-start(f32[384,1024]{1,0:T(8,128)} %get-tuple-element.16) | copy-start | bytes 4718596
  114.0 8.4 %collective-permute-start.10 = (bf16[192,1024]{1,0:T(8,128)(2,1)S(1)}, bf16[192,1024]{1,0:T(8,128)(2,1)S(1)}, u32[]{:S(2)}, u32[]{:S(2)}) collective-permute-start(bf16[192,1024]{1,0:T(8,128)(2,1)S(1)} %get-tuple-element.23), channel_id=1, source_target_pairs={{0,192},{64,0},{128,64},{192,128},{1,193},{65,1},{129,65},{193,129... | collective-permute-start | bytes 1179656 | tf_op jit(solution)/shard_map/ppermute | solution.py:120
  115.4 9.9 %collective-permute-start.6 = (bf16[192,1024]{1,0:T(8,128)(2,1)S(1)}, bf16[192,1024]{1,0:T(8,128)(2,1)S(1)}, u32[]{:S(2)}, u32[]{:S(2)}) collective-permute-start(bf16[192,1024]{1,0:T(8,128)(2,1)S(1)} %get-tuple-element.24), channel_id=1, source_target_pairs={{0,64},{64,128},{128,192},{192,0},{1,65},{65,129},{129,193},{193,1... | collective-permute-start | bytes 1179656 | tf_op jit(solution)/shard_map/ppermute | solution.py:119
  116.8 25.0 %copy-start.6 = (f32[384,1024]{1,0:T(8,128)S(1)}, f32[384,1024]{1,0:T(8,128)}, u32[]{:S(2)}) copy-start(f32[384,1024]{1,0:T(8,128)} %fusion.4) | copy-start | bytes 4718596
  116.8 14.0 %collective-permute-start.9 = (bf16[192,1024]{1,0:T(8,128)(2,1)S(1)}, bf16[192,1024]{1,0:T(8,128)(2,1)S(1)}, u32[]{:S(2)}, u32[]{:S(2)}) collective-permute-start(bf16[192,1024]{1,0:T(8,128)(2,1)S(1)} %slice.1072), channel_id=1, source_target_pairs={{0,192},{64,0},{128,64},{192,128},{1,193},{65,1},{129,65},{193,129... | collective-permute-start | bytes 1179656 | tf_op jit(solution)/shard_map/ppermute | solution.py:117
  119.5 13.9 %collective-permute-start.8 = (bf16[192,1024]{1,0:T(8,128)(2,1)S(1)}, bf16[192,1024]{1,0:T(8,128)(2,1)S(1)}, u32[]{:S(2)}, u32[]{:S(2)}) collective-permute-start(bf16[192,1024]{1,0:T(8,128)(2,1)S(1)} %slice.1073), channel_id=1, source_target_pairs={{0,64},{64,128},{128,192},{192,0},{1,65},{65,129},{129,193},{193,1... | collective-permute-start | bytes 1179656 | tf_op jit(solution)/shard_map/ppermute | solution.py:116
  122.4 16.8 %collective-permute-start.11 = (bf16[192,1024]{1,0:T(8,128)(2,1)S(1)}, bf16[192,1024]{1,0:T(8,128)(2,1)S(1)}, u32[]{:S(2)}, u32[]{:S(2)}) collective-permute-start(bf16[192,1024]{1,0:T(8,128)(2,1)S(1)} %add_convert_fusion.1), channel_id=1, source_target_pairs={{0,192},{64,0},{128,64},{192,128},{1,193},{65,1},{129,65},{193,129... | collective-permute-start | bytes 1179656 | tf_op jit(solution)/shard_map/ppermute | solution.py:122
  125.5 16.3 %collective-permute-start.7 = (bf16[192,1024]{1,0:T(8,128)(2,1)S(1)}, bf16[192,1024]{1,0:T(8,128)(2,1)S(1)}, u32[]{:S(2)}, u32[]{:S(2)}) collective-permute-start(bf16[192,1024]{1,0:T(8,128)(2,1)S(1)} %add_convert_fusion.2), channel_id=1, source_target_pairs={{0,64},{64,128},{128,192},{192,0},{1,65},{65,129},{129,193},{193,1... | collective-permute-start | bytes 1179656 | tf_op jit(solution)/shard_map/ppermute | solution.py:121
  142.2 10.1 %copy-start.8 = (bf16[1024,64]{0,1:T(8,128)(2,1)S(1)}, bf16[1024,64]{0,1:T(8,128)(2,1)}, u32[]{:S(2)}) copy-start(bf16[1024,64]{0,1:T(8,128)(2,1)} %param.24) | copy-start | bytes 393220
  143.4 8.8 %copy-start.4 = (bf16[128,1024]{1,0:T(8,128)(2,1)S(1)}, bf16[128,1024]{1,0:T(8,128)(2,1)}, u32[]{:S(2)}) copy-start(bf16[128,1024]{1,0:T(8,128)(2,1)} %copy-done.3) | copy-start | bytes 786436
  143.5 31.7 %all-to-all-start.1 = ((bf16[64,48,128]{2,1,0:T(8,128)(2,1)}), bf16[64,48,128]{2,1,0:T(8,128)(2,1)}, u32[]{:S(2)}, u32[]{:S(2)}) async-start(bf16[64,48,128]{2,1,0:T(8,128)(2,1)} %convert_element_type.481), calls=%async_computation.1 | async-start | bytes 1572864 | tf_op jit(solution)/shard_map/all_to_all | solution.py:129
  152.5 24.5 %copy-start.13 = (f32[128]{0:T(128)S(1)}, f32[128]{0:T(128)}, u32[]{:S(2)}) copy-start(f32[128]{0:T(128)} %copy-done.12) | copy-start | bytes 1540
  (7 other events, 11.1 us)

commit v11 on v9

--- a/solution.py
+++ b/solution.py
@@ -42,8 +42,17 @@
     seq_size = lax.axis_size("seq")
     seq_up = [(i, i + 1) for i in range(seq_size - 1)]
     seq_down = [(j, i) for i, j in seq_up]
-    before = lax.ppermute(gated[token_count - reach :], "seq", seq_up)
-    after = lax.ppermute(gated[:reach], "seq", seq_down)
+    edge_lifted = jnp.dot(
+        jnp.concatenate([conv_in[:reach], conv_in[token_count - reach :]], axis=0),
+        point_in,
+        preferred_element_type=jnp.float32,
+    )
+    edge_mask = jnp.concatenate([frame_mask[:reach], frame_mask[token_count - reach :]], axis=0)
+    edge_gated = (
+        edge_lifted[:, :model_width] * jax.nn.sigmoid(edge_lifted[:, model_width:]) * edge_mask
+    ).astype(jnp.bfloat16)
+    before = lax.ppermute(edge_gated[reach:], "seq", seq_up)
+    after = lax.ppermute(edge_gated[:reach], "seq", seq_down)
 
     def depthwise(rows, count):
         total = jnp.zeros((count, model_width), jnp.float32)

time: 177 us -> 184 us (1.040)
  other arithmetic: 7.03 us -> 11.5 us
  waiting for transfers between devices: 51.7 us -> 49.5 us
  matrix products: 35.5 us -> 37.4 us
    add x3, other arithmetic: 2.11 us -> 5.3 us  [depthwise(): total + rows[offset:offset + count].astype(jnp.float32) * depth_kernel[of...]
    dot_general x0 -> x1, matrix products: none -> 3.15 us  [local(): jnp.dot(jnp.concatenate([conv_in[:reach], conv_in[token_count - reach:]],...]
    dot_general x1, matrix products: 3.11 us -> 0.73 us  [local(): lifted = jnp.dot(conv_in, point_in, preferred_element_type=jnp.float32)]
  transfers between devices with their start and end apart: 13 -> 13, of which waited for: 7 -> 6; matrix products, arithmetic and copies ran while one was open for 17% -> 18% of each run, Pallas kernels for 0% -> 0%
where the time goes in v11:
time: 184 us; the launch traced here: 183 us
  waiting for transfers between devices  49.5 us (27%)
  matrix products  37.4 us (20%)
  blocking collectives  36.7 us (20%)
  starting transfers between devices  26.6 us (14%)
  local copies, waits for them, and re-layouts  20 us (11%)
  other arithmetic  11.5 us (6%)
    all_to_all x1, blocking collectives, local(): lax.all_to_all(outgoing, ('seq', 'expert'), split_axis=0, concat_axis=0,...  36.7 us
    all_to_all x1, waiting for transfers between devices, local(): lax.all_to_all(served, ('seq', 'expert'), split_axis=0, concat_axis=0, ti...  22.7 us
    dot_general x3, matrix products, serve(): lax.dot_general(hidden, down_local, (((1,), (1,)), ((), ())), preferred_e...  19.8 us
    ppermute x1, waiting for transfers between devices, local(): lax.ppermute((for_above[:half] + far_up).astype(jnp.bfloat16), 'dp', up)  9.44 us
    all_to_all x1, starting transfers between devices, local(): lax.all_to_all(served, ('seq', 'expert'), split_axis=0, concat_axis=0, ti...  8.85 us
    ppermute x1, waiting for transfers between devices, local(): from_above = lax.ppermute(own_rows, 'dp', down)  7.19 us
    dot_general x2, matrix products, serve(): gate_part = jnp.dot(rows, gate_local, preferred_element_type=jnp.float32)  5.5 us
    add x3, other arithmetic, depthwise(): total + rows[offset:offset + count].astype(jnp.float32) * depth_kernel[of...  5.3 us
  transfers between devices with their start and end apart: 13, of which 6 were waited for; matrix products, arithmetic and copies ran while one was open for 18% of the time, Pallas kernels for 0%

profile of v11, /device:TPU:1, one launch (start us, length us, event | category | flops | bytes accessed | tf_op | source)
XLA Modules:
  0.0 183.0 jit_solution(13321112192344497095)
XLA Ops:
  4.4 3.2 %fusion.72 = f32[30,2048]{1,0:T(8,128)S(1)} fusion(bf16[1024,2048]{1,0:T(8,128)(2,1)} %param.18, bf16[15,1024]{1,0:T(8,128)(2,1)S(1)} %get-tuple-element.28, bf16[15,1024]{1,0:T(8,128)(2,1)S(1)} %get-tuple-element.27), kind=kOutput, calls=%fused_computation.134 | convolution fusion | flops 125952000 | bytes 4501504 | tf_op jit(solution)/shard_map/dot_general | solution.py:45
  8.3 5.0 %collective-permute-start = (bf16[15,1024]{1,0:T(8,128)(2,1)}, bf16[15,1024]{1,0:T(8,128)(2,1)}, u32[]{:S(2)}, u32[]{:S(2)}) collective-permute-start(bf16[15,1024]{1,0:T(8,128)(2,1)} %get-tuple-element.60), channel_id=1, source_target_pairs={{0,8},{8,16},{16,24},{24,32},{32,40},{40,48},{48,56},{1,9},{9,17},... | collective-permute-start | bytes 92168 | tf_op jit(solution)/shard_map/ppermute | solution.py:54
  16.1 1.5 multiply_add_fusion
  17.6 1.8 multiply_add_fusion.2
  19.5 2.0 %multiply_add_fusion.1 = f32[15,1024]{1,0:T(8,128)S(1)} fusion(bf16[15,1024]{1,0:T(8,128)(2,1)} %collective-permute-done.1, bf16[30,1024]{1,0:T(8,128)(2,1)S(1)} %get-tuple-element.26, bf16[128,1024]{1,0:T(8,128)(2,1)S(1)} %fusion.53, f32[1024]{0:T(1024)S(1)} %bitcast.156, f32[1024]{0:T(1024)S(1)} %bitcast.159, f32[1024]{0:T(1024)S(1)} %bitcast.165, ...), kind=kLoop, calls=%fused_computation.138 | loop fusion | flops 2058240 | bytes 772096 | tf_op jit(solution)/shard_map/add | solution.py:60
  25.9 36.7 %all_to_all.10 = bf16[64,48,128]{2,1,0:T(8,128)(2,1)} all-to-all(bf16[64,48,128]{2,1,0:T(8,128)(2,1)S(1)} %reshape.69), channel_id=1, replica_groups=mesh['dp'=4,'seq'=8,'expert'=8] {'seq','expert'}, dimensions={0} | all-to-all | bytes 1572864 | tf_op jit(solution)/shard_map/all_to_all | solution.py:99
  62.6 2.1 %reshape.70 = bf16[384,1024]{1,0:T(8,128)(2,1)} reshape(bf16[64,48,128]{2,1,0:T(8,128)(2,1)} %all_to_all.10) | data formatting | bytes 1572864 | tf_op jit(solution)/shard_map/reshape | solution.py:101
  64.8 2.7 %collective-permute-start.3 = (bf16[384,1024]{1,0:T(8,128)(2,1)}, bf16[384,1024]{1,0:T(8,128)(2,1)S(1)}, u32[]{:S(2)}, u32[]{:S(2)}) collective-permute-start(bf16[384,1024]{1,0:T(8,128)(2,1)} %reshape.70), channel_id=1, source_target_pairs={{0,192},{64,0},{128,64},{192,128},{1,193},{65,1},{129,65},{193,129... | collective-permute-start | bytes 2359304 | tf_op jit(solution)/shard_map/ppermute | solution.py:116
  67.5 3.3 %fusion.16 = f32[384,1024]{1,0:T(8,128)} fusion(bf16[384,1024]{1,0:T(8,128)(2,1)} %reshape.70, bf16[1,1024,1024]{2,1,0:T(8,128)(2,1)S(1)} %copy-done), kind=kOutput, calls=%fused_computation.17 | convolution fusion | flops 805306368 | bytes 4456448 | tf_op jit(solution)/shard_map/dot_general | solution.py:104
  70.8 6.0 %fusion.4 = f32[384,1024]{1,0:T(8,128)} fusion(bf16[1,1024,1024]{2,1,0:T(8,128)(2,1)} %param.27, f32[384,1024]{1,0:T(8,128)} %fusion.16, bf16[384,1024]{1,0:T(8,128)(2,1)} %reshape.70, bf16[1,1024,1024]{2,1,0:T(8,128)(2,1)} %param.26), kind=kOutput, calls=%fused_computation.5 | convolution fusion | flops 1612972032 | bytes 8126464 | tf_op jit(solution)/shard_map/dot_general | solution.py:107
  76.8 7.2 %collective-permute-done.3 = bf16[384,1024]{1,0:T(8,128)(2,1)S(1)} collective-permute-done((bf16[384,1024]{1,0:T(8,128)(2,1)}, bf16[384,1024]{1,0:T(8,128)(2,1)S(1)}, u32[]{:S(2)}, u32[]{:S(2)}) %collective-permute-start.3) | collective-permute-done | bytes 786464 | tf_op jit(solution)/shard_map/ppermute | solution.py:116
  84.0 3.1 %collective-permute-done.2 = bf16[384,1024]{1,0:T(8,128)(2,1)} collective-permute-done((bf16[384,1024]{1,0:T(8,128)(2,1)}, bf16[384,1024]{1,0:T(8,128)(2,1)}, u32[]{:S(2)}, u32[]{:S(2)}) %collective-permute-start.2) | collective-permute-done | bytes 786464 | tf_op jit(solution)/shard_map/ppermute | solution.py:115
  93.1 3.5 %fusion.8 = f32[768,1024]{1,0:T(8,128)} fusion(bf16[768,1024]{1,0:T(8,128)(2,1)S(1)} %constant_dynamic-update-slice_fusion, bf16[1,1024,1024]{2,1,0:T(8,128)(2,1)S(1)} %copy-done.16), kind=kOutput, calls=%fused_computation.9 | convolution fusion | flops 1610612736 | bytes 6815744 | tf_op jit(solution)/shard_map/dot_general | solution.py:105
  96.6 8.4 %fusion.2 = f32[768,1024]{1,0:T(8,128)} fusion(bf16[1,1024,1024]{2,1,0:T(8,128)(2,1)} %param.27, f32[768,1024]{1,0:T(8,128)} %fusion.8, bf16[768,1024]{1,0:T(8,128)(2,1)} %copy-done.7, bf16[1,1024,1024]{2,1,0:T(8,128)(2,1)S(1)} %copy-done), kind=kOutput, calls=%fused_computation.3 | convolution fusion | flops 3225944064 | bytes 12058624 | tf_op jit(solution)/shard_map/dot_general | solution.py:107
  105.0 4.0 %fusion.114 = (f32[384,1024]{1,0:T(8,128)}, f32[384,1024]{1,0:T(8,128)}) fusion(f32[768,1024]{1,0:T(8,128)} %fusion.2), kind=kLoop, calls=%fused_computation.203 | loop fusion | bytes 6291456 | tf_op jit(solution)/shard_map/slice | solution.py:123
  110.1 2.2 %fusion.12 = f32[384,1024]{1,0:T(8,128)} fusion(bf16[384,1024]{1,0:T(8,128)(2,1)S(1)} %pad_maximum_fusion, bf16[1,1024,1024]{2,1,0:T(8,128)(2,1)S(1)} %copy-done), kind=kOutput, calls=%fused_computation.13 | convolution fusion | flops 805306368 | bytes 4456448 | tf_op jit(solution)/shard_map/dot_general | solution.py:104
  112.3 5.5 %fusion.27 = bf16[384,1024]{1,0:T(8,128)(2,1)} fusion(bf16[1,1024,1024]{2,1,0:T(8,128)(2,1)} %param.27, f32[384,1024]{1,0:T(8,128)} %fusion.12, bf16[384,1024]{1,0:T(8,128)(2,1)S(1)} %pad_maximum_fusion, bf16[1,1024,1024]{2,1,0:T(8,128)(2,1)} %param.26), kind=kOutput, calls=%fused_computation.24 | convolution fusion | flops 1613365248 | bytes 7340032 | tf_op jit(solution)/shard_map/dot_general | solution.py:107
  119.2 2.7 %collective-permute-start.10 = (bf16[192,1024]{1,0:T(8,128)(2,1)S(1)}, bf16[192,1024]{1,0:T(8,128)(2,1)S(1)}, u32[]{:S(2)}, u32[]{:S(2)}) collective-permute-start(bf16[192,1024]{1,0:T(8,128)(2,1)S(1)} %get-tuple-element.24), channel_id=1, source_target_pairs={{0,192},{64,0},{128,64},{192,128},{1,193},{65,1},{129,65},{193,129... | collective-permute-start | bytes 1179656 | tf_op jit(solution)/shard_map/ppermute | solution.py:129
  125.7 2.9 %collective-permute-done.6 = bf16[192,1024]{1,0:T(8,128)(2,1)S(1)} collective-permute-done((bf16[192,1024]{1,0:T(8,128)(2,1)S(1)}, bf16[192,1024]{1,0:T(8,128)(2,1)S(1)}, u32[]{:S(2)}, u32[]{:S(2)}) %collective-permute-start.6) | collective-permute-done | bytes 393248 | tf_op jit(solution)/shard_map/ppermute | solution.py:128
  128.9 2.9 %collective-permute-start.11 = (bf16[192,1024]{1,0:T(8,128)(2,1)S(1)}, bf16[192,1024]{1,0:T(8,128)(2,1)S(1)}, u32[]{:S(2)}, u32[]{:S(2)}) collective-permute-start(bf16[192,1024]{1,0:T(8,128)(2,1)S(1)} %add_convert_fusion), channel_id=1, source_target_pairs={{0,192},{64,0},{128,64},{192,128},{1,193},{65,1},{129,65},{193,129... | collective-permute-start | bytes 1179656 | tf_op jit(solution)/shard_map/ppermute | solution.py:131
  131.9 4.2 %collective-permute-done.8 = bf16[192,1024]{1,0:T(8,128)(2,1)S(1)} collective-permute-done((bf16[192,1024]{1,0:T(8,128)(2,1)S(1)}, bf16[192,1024]{1,0:T(8,128)(2,1)S(1)}, u32[]{:S(2)}, u32[]{:S(2)}) %collective-permute-start.8) | collective-permute-done | bytes 393248 | tf_op jit(solution)/shard_map/ppermute | solution.py:126
  136.0 9.4 %collective-permute-done.7 = bf16[192,1024]{1,0:T(8,128)(2,1)S(1)} collective-permute-done((bf16[192,1024]{1,0:T(8,128)(2,1)S(1)}, bf16[192,1024]{1,0:T(8,128)(2,1)S(1)}, u32[]{:S(2)}, u32[]{:S(2)}) %collective-permute-start.7) | collective-permute-done | bytes 393248 | tf_op jit(solution)/shard_map/ppermute | solution.py:130
  147.3 8.8 %all-to-all-start.1 = ((bf16[64,48,128]{2,1,0:T(8,128)(2,1)}), bf16[64,48,128]{2,1,0:T(8,128)(2,1)}, u32[]{:S(2)}, u32[]{:S(2)}) async-start(bf16[64,48,128]{2,1,0:T(8,128)(2,1)} %reshape.71), calls=%async_computation.1 | async-start | bytes 1572864 | tf_op jit(solution)/shard_map/all_to_all | solution.py:136
  156.4 22.7 %all-to-all-done.1 = bf16[64,48,128]{2,1,0:T(8,128)(2,1)} async-done(((bf16[64,48,128]{2,1,0:T(8,128)(2,1)}), bf16[64,48,128]{2,1,0:T(8,128)(2,1)}, u32[]{:S(2)}, u32[]{:S(2)}) %all-to-all-start.1) | async-done | bytes 786464 | tf_op jit(solution)/shard_map/all_to_all | solution.py:136
  (102 shorter events, 30.0 us)
Async XLA Ops:
  0.0 67.5 %copy-start = (bf16[1,1024,1024]{2,1,0:T(8,128)(2,1)S(1)}, bf16[1,1024,1024]{2,1,0:T(8,128)(2,1)}, u32[]{:S(2)}) copy-start(bf16[1,1024,1024]{2,1,0:T(8,128)(2,1)} %param.25) | copy-start | bytes 6291460
  4.4 10.1 %copy-start.9 = (f32[31,1024]{1,0:T(8,128)S(1)}, f32[31,1024]{1,0:T(8,128)}, u32[]{:S(2)}) copy-start(f32[31,1024]{1,0:T(8,128)} %param.19) | copy-start | bytes 380932
  4.4 10.3 %copy-start.1 = (bf16[1024,2048]{1,0:T(8,128)(2,1)S(1)}, bf16[1024,2048]{1,0:T(8,128)(2,1)}, u32[]{:S(2)}) copy-start(bf16[1024,2048]{1,0:T(8,128)(2,1)} %param.18) | copy-start | bytes 12582916
  8.3 9.3 %collective-permute-start = (bf16[15,1024]{1,0:T(8,128)(2,1)}, bf16[15,1024]{1,0:T(8,128)(2,1)}, u32[]{:S(2)}, u32[]{:S(2)}) collective-permute-start(bf16[15,1024]{1,0:T(8,128)(2,1)} %get-tuple-element.60), channel_id=1, source_target_pairs={{0,8},{8,16},{16,24},{24,32},{32,40},{40,48},{48,56},{1,9},{9,17},... | collective-permute-start | bytes 92168 | tf_op jit(solution)/shard_map/ppermute | solution.py:54
  13.3 6.2 %collective-permute-start.1 = (bf16[15,1024]{1,0:T(8,128)(2,1)}, bf16[15,1024]{1,0:T(8,128)(2,1)}, u32[]{:S(2)}, u32[]{:S(2)}) collective-permute-start(bf16[15,1024]{1,0:T(8,128)(2,1)} %get-tuple-element.61), channel_id=1, source_target_pairs={{8,0},{16,8},{24,16},{32,24},{40,32},{48,40},{56,48},{9,1},{17,9},... | collective-permute-start | bytes 92168 | tf_op jit(solution)/shard_map/ppermute | solution.py:55
  16.1 5.4 %copy-start.5 = (bf16[1,128,1024]{2,1,0:T(8,128)(2,1)S(1)}, bf16[1,128,1024]{2,1,0:T(8,128)(2,1)}, u32[]{:S(2)}) copy-start(bf16[1,128,1024]{2,1,0:T(8,128)(2,1)} %param.14) | copy-start | bytes 786436
  16.1 5.4 %copy-start.15 = (bf16[1024,1024]{1,0:T(8,128)(2,1)S(1)}, bf16[1024,1024]{1,0:T(8,128)(2,1)}, u32[]{:S(2)}) copy-start(bf16[1024,1024]{1,0:T(8,128)(2,1)} %param.22) | copy-start | bytes 6291460
  17.6 5.5 %copy-start.10 = (s32[128]{0:T(128)}, s32[128]{0:T(128)S(1)}, u32[]{:S(2)}) copy-start(s32[128]{0:T(128)S(1)} %get-tuple-element.64) | copy-start | bytes 1540
  64.8 19.3 %collective-permute-start.3 = (bf16[384,1024]{1,0:T(8,128)(2,1)}, bf16[384,1024]{1,0:T(8,128)(2,1)S(1)}, u32[]{:S(2)}, u32[]{:S(2)}) collective-permute-start(bf16[384,1024]{1,0:T(8,128)(2,1)} %reshape.70), channel_id=1, source_target_pairs={{0,192},{64,0},{128,64},{192,128},{1,193},{65,1},{129,65},{193,129... | collective-permute-start | bytes 2359304 | tf_op jit(solution)/shard_map/ppermute | solution.py:116
  67.5 19.6 %collective-permute-start.2 = (bf16[384,1024]{1,0:T(8,128)(2,1)}, bf16[384,1024]{1,0:T(8,128)(2,1)}, u32[]{:S(2)}, u32[]{:S(2)}) collective-permute-start(bf16[384,1024]{1,0:T(8,128)(2,1)} %reshape.70), channel_id=1, source_target_pairs={{0,64},{64,128},{128,192},{192,0},{1,65},{65,129},{129,193},{193,1... | collective-permute-start | bytes 2359304 | tf_op jit(solution)/shard_map/ppermute | solution.py:115
  90.3 18.6 %collective-permute-start.5 = (bf16[192,1024]{1,0:T(8,128)(2,1)}, bf16[192,1024]{1,0:T(8,128)(2,1)}, u32[]{:S(2)}, u32[]{:S(2)}) collective-permute-start(bf16[192,1024]{1,0:T(8,128)(2,1)} %slice.681), channel_id=1, source_target_pairs={{0,192},{64,0},{128,64},{192,128},{1,193},{65,1},{129,65},{193,129... | collective-permute-start | bytes 1179656 | tf_op jit(solution)/shard_map/ppermute | solution.py:120
  90.5 18.5 %collective-permute-start.4 = (bf16[192,1024]{1,0:T(8,128)(2,1)S(1)}, bf16[192,1024]{1,0:T(8,128)(2,1)}, u32[]{:S(2)}, u32[]{:S(2)}) collective-permute-start(bf16[192,1024]{1,0:T(8,128)(2,1)S(1)} %slice.680), channel_id=1, source_target_pairs={{0,64},{64,128},{128,192},{192,0},{1,65},{65,129},{129,193},{193,1... | collective-permute-start | bytes 1179656 | tf_op jit(solution)/shard_map/ppermute | solution.py:120
  117.7 10.9 %copy-start.2 = (f32[384,1024]{1,0:T(8,128)S(1)}, f32[384,1024]{1,0:T(8,128)}, u32[]{:S(2)}) copy-start(f32[384,1024]{1,0:T(8,128)} %get-tuple-element.14) | copy-start | bytes 4718596
  117.7 11.1 %copy-start.3 = (f32[384,1024]{1,0:T(8,128)S(1)}, f32[384,1024]{1,0:T(8,128)}, u32[]{:S(2)}) copy-start(f32[384,1024]{1,0:T(8,128)} %get-tuple-element.16) | copy-start | bytes 4718596
  119.1 9.5 %collective-permute-start.6 = (bf16[192,1024]{1,0:T(8,128)(2,1)S(1)}, bf16[192,1024]{1,0:T(8,128)(2,1)S(1)}, u32[]{:S(2)}, u32[]{:S(2)}) collective-permute-start(bf16[192,1024]{1,0:T(8,128)(2,1)S(1)} %get-tuple-element.23), channel_id=1, source_target_pairs={{0,64},{64,128},{128,192},{192,0},{1,65},{65,129},{129,193},{193,1... | collective-permute-start | bytes 1179656 | tf_op jit(solution)/shard_map/ppermute | solution.py:128
  119.2 9.6 %collective-permute-start.10 = (bf16[192,1024]{1,0:T(8,128)(2,1)S(1)}, bf16[192,1024]{1,0:T(8,128)(2,1)S(1)}, u32[]{:S(2)}, u32[]{:S(2)}) collective-permute-start(bf16[192,1024]{1,0:T(8,128)(2,1)S(1)} %get-tuple-element.24), channel_id=1, source_target_pairs={{0,192},{64,0},{128,64},{192,128},{1,193},{65,1},{129,65},{193,129... | collective-permute-start | bytes 1179656 | tf_op jit(solution)/shard_map/ppermute | solution.py:129
  124.2 11.8 %collective-permute-start.8 = (bf16[192,1024]{1,0:T(8,128)(2,1)S(1)}, bf16[192,1024]{1,0:T(8,128)(2,1)S(1)}, u32[]{:S(2)}, u32[]{:S(2)}) collective-permute-start(bf16[192,1024]{1,0:T(8,128)(2,1)S(1)} %slice.1135), channel_id=1, source_target_pairs={{0,192},{64,0},{128,64},{192,128},{1,193},{65,1},{129,65},{193,129... | collective-permute-start | bytes 1179656 | tf_op jit(solution)/shard_map/ppermute | solution.py:126
  124.4 21.1 %collective-permute-start.9 = (bf16[192,1024]{1,0:T(8,128)(2,1)S(1)}, bf16[192,1024]{1,0:T(8,128)(2,1)S(1)}, u32[]{:S(2)}, u32[]{:S(2)}) collective-permute-start(bf16[192,1024]{1,0:T(8,128)(2,1)S(1)} %slice.1134), channel_id=1, source_target_pairs={{0,64},{64,128},{128,192},{192,0},{1,65},{65,129},{129,193},{193,1... | collective-permute-start | bytes 1179656 | tf_op jit(solution)/shard_map/ppermute | solution.py:125
  128.7 17.0 %copy-start.6 = (f32[384,1024]{1,0:T(8,128)S(1)}, f32[384,1024]{1,0:T(8,128)}, u32[]{:S(2)}) copy-start(f32[384,1024]{1,0:T(8,128)} %fusion.4) | copy-start | bytes 4718596
  128.7 16.7 %collective-permute-start.7 = (bf16[192,1024]{1,0:T(8,128)(2,1)S(1)}, bf16[192,1024]{1,0:T(8,128)(2,1)S(1)}, u32[]{:S(2)}, u32[]{:S(2)}) collective-permute-start(bf16[192,1024]{1,0:T(8,128)(2,1)S(1)} %add_convert_fusion.1), channel_id=1, source_target_pairs={{0,64},{64,128},{128,192},{192,0},{1,65},{65,129},{129,193},{193,1... | collective-permute-start | bytes 1179656 | tf_op jit(solution)/shard_map/ppermute | solution.py:130
  128.9 16.7 %collective-permute-start.11 = (bf16[192,1024]{1,0:T(8,128)(2,1)S(1)}, bf16[192,1024]{1,0:T(8,128)(2,1)S(1)}, u32[]{:S(2)}, u32[]{:S(2)}) collective-permute-start(bf16[192,1024]{1,0:T(8,128)(2,1)S(1)} %add_convert_fusion), channel_id=1, source_target_pairs={{0,192},{64,0},{128,64},{192,128},{1,193},{65,1},{129,65},{193,129... | collective-permute-start | bytes 1179656 | tf_op jit(solution)/shard_map/ppermute | solution.py:131
  146.1 10.1 %copy-start.8 = (bf16[1024,64]{0,1:T(8,128)(2,1)S(1)}, bf16[1024,64]{0,1:T(8,128)(2,1)}, u32[]{:S(2)}) copy-start(bf16[1024,64]{0,1:T(8,128)(2,1)} %param.24) | copy-start | bytes 393220
  147.3 33.2 %copy-start.11 = (s32[128]{0:T(128)S(1)}, s32[128]{0:T(128)}, u32[]{:S(2)}) copy-start(s32[128]{0:T(128)} %copy-done.10) | copy-start | bytes 1540
  147.3 31.8 %all-to-all-start.1 = ((bf16[64,48,128]{2,1,0:T(8,128)(2,1)}), bf16[64,48,128]{2,1,0:T(8,128)(2,1)}, u32[]{:S(2)}, u32[]{:S(2)}) async-start(bf16[64,48,128]{2,1,0:T(8,128)(2,1)} %reshape.71), calls=%async_computation.1 | async-start | bytes 1572864 | tf_op jit(solution)/shard_map/all_to_all | solution.py:136
  (8 other events, 21.5 us)

commit v12 on v9

--- a/solution.py
+++ b/solution.py
@@ -107,9 +107,7 @@
     from_above = lax.ppermute(own_rows, "dp", down)
     for_own = serve(own_rows)
     for_own, from_below, from_above = lax.optimization_barrier((for_own, from_below, from_above))
-    far_rows = jnp.concatenate(
-        [lax.ppermute(from_below[:half], "dp", up), lax.ppermute(from_above[half:], "dp", down)], axis=0
-    )
+    far_rows = lax.ppermute(from_below, "dp", up)
     for_near = serve(jnp.concatenate([from_below, from_above], axis=0))
     for_below, for_above = for_near[: 2 * half], for_near[2 * half :]
     far_rows, for_below, for_above = lax.optimization_barrier((far_rows, for_below, for_above))

time: 177 us -> 172 us (0.972)
  local copies, waits for them, and re-layouts: 18.8 us -> 16.2 us
  starting transfers between devices: 26 us -> 23.6 us
  matrix products: 35.5 us -> 37.6 us
    dot_general x1 -> x2, matrix products: 3.49 us -> 6.77 us  [serve(): up_part = jnp.dot(rows, up_local, preferred_element_type=jnp.float32)]
    slice x2 -> x0, local copies, waits for them, and re-layouts: 2.57 us -> none  [the longest x1 1.78 us: local(): from_below[:half]]
    dot_general x2 -> x1, matrix products: 5.5 us -> 3.98 us  [serve(): gate_part = jnp.dot(rows, gate_local, preferred_element_type=jnp.float32)]
  transfers between devices with their start and end apart: 13 -> 12, of which waited for: 7 -> 7; matrix products, arithmetic and copies ran while one was open for 17% -> 19% of each run, Pallas kernels for 0% -> 0%
where the time goes in v12:
time: 172 us; the launch traced here: 171 us
  waiting for transfers between devices  50.5 us (29%)
  matrix products  37.6 us (22%)
  blocking collectives  36.2 us (21%)
  starting transfers between devices  23.6 us (14%)
  local copies, waits for them, and re-layouts  16.2 us (9%)
  other arithmetic  5.86 us (3%)
    all_to_all x1, blocking collectives, local(): lax.all_to_all(outgoing, ('seq', 'expert'), split_axis=0, concat_axis=0,...  36.2 us
    all_to_all x1, waiting for transfers between devices, local(): lax.all_to_all(served, ('seq', 'expert'), split_axis=0, concat_axis=0, ti...  21.7 us
    dot_general x3, matrix products, serve(): lax.dot_general(hidden, down_local, (((1,), (1,)), ((), ())), preferred_e...  19.1 us
    ppermute x1, waiting for transfers between devices, local(): lax.ppermute((for_above[:half] + far_up).astype(jnp.bfloat16), 'dp', up)  10.3 us
    all_to_all x1, starting transfers between devices, local(): lax.all_to_all(served, ('seq', 'expert'), split_axis=0, concat_axis=0, ti...  7.76 us
    ppermute x1, waiting for transfers between devices, local(): from_above = lax.ppermute(own_rows, 'dp', down)  7.19 us
    dot_general x2, matrix products, serve(): up_part = jnp.dot(rows, up_local, preferred_element_type=jnp.float32)  6.77 us
    ppermute x1, starting transfers between devices, local(): before = lax.ppermute(gated[token_count - reach:], 'seq', seq_up)  4.36 us
  transfers between devices with their start and end apart: 12, of which 7 were waited for; matrix products, arithmetic and copies ran while one was open for 19% of the time, Pallas kernels for 0%

profile of v12, /device:TPU:1, one launch (start us, length us, event | category | flops | bytes accessed | tf_op | source)
XLA Modules:
  0.0 171.2 jit_solution(3777738658120101726)
XLA Ops:
  3.1 3.1 %fusion.54 = f32[128,2048]{1,0:T(8,128)S(1)} fusion(bf16[1024,2048]{1,0:T(8,128)(2,1)} %param.18, bf16[1,128,1024]{2,1,0:T(8,128)(2,1)} %param.14, f32[1024]{0:T(1024)} %param.17, f32[128]{0:T(128)S(1)} %add_rsqrt_fusion.1, f32[128]{0:T(128)S(1)} %broadcast_multiply_fusion.1), kind=kOutput, calls=%fused_computation.88 | convolution fusion | flops 537526272 | bytes 5510144 | tf_op jit(solution)/shard_map/dot_general | solution.py:36
  6.4 4.4 %collective-permute-start = (bf16[15,1024]{1,0:T(8,128)(2,1)S(1)}, bf16[15,1024]{1,0:T(8,128)(2,1)S(1)}, u32[]{:S(2)}, u32[]{:S(2)}) collective-permute-start(bf16[15,1024]{1,0:T(8,128)(2,1)S(1)} %get-tuple-element.27), channel_id=1, source_target_pairs={{0,8},{8,16},{16,24},{24,32},{32,40},{40,48},{48,56},{1,9},{9,17},... | collective-permute-start | bytes 92168 | tf_op jit(solution)/shard_map/ppermute | solution.py:45
  12.7 1.5 multiply_add_fusion
  20.5 36.2 %all_to_all.10 = bf16[64,48,128]{2,1,0:T(8,128)(2,1)} all-to-all(bf16[64,48,128]{2,1,0:T(8,128)(2,1)S(1)} %reshape.67), channel_id=1, replica_groups=mesh['dp'=4,'seq'=8,'expert'=8] {'seq','expert'}, dimensions={0} | all-to-all | bytes 1572864 | tf_op jit(solution)/shard_map/all_to_all | solution.py:90
  56.7 2.2 %reshape.68 = bf16[384,1024]{1,0:T(8,128)(2,1)} reshape(bf16[64,48,128]{2,1,0:T(8,128)(2,1)} %all_to_all.10) | data formatting | bytes 1572864 | tf_op jit(solution)/shard_map/reshape | solution.py:92
  58.9 2.7 %collective-permute-start.3 = (bf16[384,1024]{1,0:T(8,128)(2,1)}, bf16[384,1024]{1,0:T(8,128)(2,1)}, u32[]{:S(2)}, u32[]{:S(2)}) collective-permute-start(bf16[384,1024]{1,0:T(8,128)(2,1)} %reshape.68), channel_id=1, source_target_pairs={{0,192},{64,0},{128,64},{192,128},{1,193},{65,1},{129,65},{193,129... | collective-permute-start | bytes 2359304 | tf_op jit(solution)/shard_map/ppermute | solution.py:107
  61.6 4.0 %fusion.16 = f32[384,1024]{1,0:T(8,128)} fusion(bf16[384,1024]{1,0:T(8,128)(2,1)} %reshape.68, bf16[1,1024,1024]{2,1,0:T(8,128)(2,1)} %param.25), kind=kOutput, calls=%fused_computation.17 | convolution fusion | flops 805306368 | bytes 4456448 | tf_op jit(solution)/shard_map/dot_general | solution.py:95
  65.6 5.3 %fusion.4 = f32[384,1024]{1,0:T(8,128)} fusion(bf16[1,1024,1024]{2,1,0:T(8,128)(2,1)} %param.27, f32[384,1024]{1,0:T(8,128)} %fusion.16, bf16[384,1024]{1,0:T(8,128)(2,1)} %reshape.68, bf16[1,1024,1024]{2,1,0:T(8,128)(2,1)S(1)} %copy-done), kind=kOutput, calls=%fused_computation.5 | convolution fusion | flops 1612972032 | bytes 8126464 | tf_op jit(solution)/shard_map/dot_general | solution.py:98
  70.9 7.2 %collective-permute-done.3 = bf16[384,1024]{1,0:T(8,128)(2,1)} collective-permute-done((bf16[384,1024]{1,0:T(8,128)(2,1)}, bf16[384,1024]{1,0:T(8,128)(2,1)}, u32[]{:S(2)}, u32[]{:S(2)}) %collective-permute-start.3) | collective-permute-done | bytes 786464 | tf_op jit(solution)/shard_map/ppermute | solution.py:107
  78.1 3.0 %collective-permute-done.2 = bf16[384,1024]{1,0:T(8,128)(2,1)S(1)} collective-permute-done((bf16[384,1024]{1,0:T(8,128)(2,1)}, bf16[384,1024]{1,0:T(8,128)(2,1)S(1)}, u32[]{:S(2)}, u32[]{:S(2)}) %collective-permute-start.2) | collective-permute-done | bytes 786464 | tf_op jit(solution)/shard_map/ppermute | solution.py:106
  83.6 3.5 %fusion.8 = f32[768,1024]{1,0:T(8,128)} fusion(bf16[768,1024]{1,0:T(8,128)(2,1)S(1)} %constant_dynamic-update-slice_fusion, bf16[1,1024,1024]{2,1,0:T(8,128)(2,1)S(1)} %copy-done), kind=kOutput, calls=%fused_computation.9 | convolution fusion | flops 1610612736 | bytes 6815744 | tf_op jit(solution)/shard_map/dot_general | solution.py:96
  87.1 9.0 %fusion.2 = f32[768,1024]{1,0:T(8,128)} fusion(bf16[1,1024,1024]{2,1,0:T(8,128)(2,1)} %param.27, f32[768,1024]{1,0:T(8,128)} %fusion.8, bf16[768,1024]{1,0:T(8,128)(2,1)} %copy-done.6, bf16[1,1024,1024]{2,1,0:T(8,128)(2,1)} %param.25), kind=kOutput, calls=%fused_computation.3 | convolution fusion | flops 3225944064 | bytes 12058624 | tf_op jit(solution)/shard_map/dot_general | solution.py:98
  96.1 4.0 %fusion.108 = (f32[384,1024]{1,0:T(8,128)}, f32[384,1024]{1,0:T(8,128)}) fusion(f32[768,1024]{1,0:T(8,128)} %fusion.2), kind=kLoop, calls=%fused_computation.191 | loop fusion | bytes 6291456 | tf_op jit(solution)/shard_map/slice | solution.py:112
  100.0 3.3 %fusion.6 = f32[384,1024]{1,0:T(8,128)} fusion(bf16[384,1024]{1,0:T(8,128)(2,1)} %collective-permute-done.4, bf16[1,1024,1024]{2,1,0:T(8,128)(2,1)S(1)} %copy-done), kind=kOutput, calls=%fused_computation.7 | convolution fusion | flops 805306368 | bytes 4456448 | tf_op jit(solution)/shard_map/dot_general | solution.py:96
  103.3 4.8 %fusion.25 = bf16[384,1024]{1,0:T(8,128)(2,1)S(1)} fusion(bf16[1,1024,1024]{2,1,0:T(8,128)(2,1)} %param.27, f32[384,1024]{1,0:T(8,128)} %fusion.6, bf16[384,1024]{1,0:T(8,128)(2,1)} %collective-permute-done.4, bf16[1,1024,1024]{2,1,0:T(8,128)(2,1)} %param.25), kind=kOutput, calls=%fused_computation.24 | convolution fusion | flops 1613365248 | bytes 7340032 | tf_op jit(solution)/shard_map/dot_general | solution.py:98
  108.4 2.7 %collective-permute-start.9 = (bf16[192,1024]{1,0:T(8,128)(2,1)S(1)}, bf16[192,1024]{1,0:T(8,128)(2,1)S(1)}, u32[]{:S(2)}, u32[]{:S(2)}) collective-permute-start(bf16[192,1024]{1,0:T(8,128)(2,1)S(1)} %get-tuple-element.24), channel_id=1, source_target_pairs={{0,192},{64,0},{128,64},{192,128},{1,193},{65,1},{129,65},{193,129... | collective-permute-start | bytes 1179656 | tf_op jit(solution)/shard_map/ppermute | solution.py:118
  113.5 1.5 collective-permute-start.7
  115.0 2.8 %collective-permute-done.5 = bf16[192,1024]{1,0:T(8,128)(2,1)S(1)} collective-permute-done((bf16[192,1024]{1,0:T(8,128)(2,1)S(1)}, bf16[192,1024]{1,0:T(8,128)(2,1)S(1)}, u32[]{:S(2)}, u32[]{:S(2)}) %collective-permute-start.5) | collective-permute-done | bytes 393248 | tf_op jit(solution)/shard_map/ppermute | solution.py:117
  118.2 2.9 %collective-permute-start.10 = (bf16[192,1024]{1,0:T(8,128)(2,1)S(1)}, bf16[192,1024]{1,0:T(8,128)(2,1)S(1)}, u32[]{:S(2)}, u32[]{:S(2)}) collective-permute-start(bf16[192,1024]{1,0:T(8,128)(2,1)S(1)} %add_convert_fusion), channel_id=1, source_target_pairs={{0,192},{64,0},{128,64},{192,128},{1,193},{65,1},{129,65},{193,129... | collective-permute-start | bytes 1179656 | tf_op jit(solution)/shard_map/ppermute | solution.py:120
  121.1 4.3 %collective-permute-done.7 = bf16[192,1024]{1,0:T(8,128)(2,1)S(1)} collective-permute-done((bf16[192,1024]{1,0:T(8,128)(2,1)S(1)}, bf16[192,1024]{1,0:T(8,128)(2,1)S(1)}, u32[]{:S(2)}, u32[]{:S(2)}) %collective-permute-start.7) | collective-permute-done | bytes 393248 | tf_op jit(solution)/shard_map/ppermute | solution.py:115
  125.4 10.3 %collective-permute-done.6 = bf16[192,1024]{1,0:T(8,128)(2,1)S(1)} collective-permute-done((bf16[192,1024]{1,0:T(8,128)(2,1)S(1)}, bf16[192,1024]{1,0:T(8,128)(2,1)S(1)}, u32[]{:S(2)}, u32[]{:S(2)}) %collective-permute-start.6) | collective-permute-done | bytes 393248 | tf_op jit(solution)/shard_map/ppermute | solution.py:119
  137.6 7.8 %all-to-all-start.1 = ((bf16[64,48,128]{2,1,0:T(8,128)(2,1)}), bf16[64,48,128]{2,1,0:T(8,128)(2,1)}, u32[]{:S(2)}, u32[]{:S(2)}) async-start(bf16[64,48,128]{2,1,0:T(8,128)(2,1)} %reshape.69), calls=%async_computation.1 | async-start | bytes 1572864 | tf_op jit(solution)/shard_map/all_to_all | solution.py:125
  146.6 21.7 %all-to-all-done.1 = bf16[64,48,128]{2,1,0:T(8,128)(2,1)} async-done(((bf16[64,48,128]{2,1,0:T(8,128)(2,1)}), bf16[64,48,128]{2,1,0:T(8,128)(2,1)}, u32[]{:S(2)}, u32[]{:S(2)}) %all-to-all-start.1) | async-done | bytes 786464 | tf_op jit(solution)/shard_map/all_to_all | solution.py:125
  168.3 1.4 reshape.70
  (85 shorter events, 20.3 us)
Async XLA Ops:
  0.0 65.6 %copy-start = (bf16[1,1024,1024]{2,1,0:T(8,128)(2,1)S(1)}, bf16[1,1024,1024]{2,1,0:T(8,128)(2,1)}, u32[]{:S(2)}) copy-start(bf16[1,1024,1024]{2,1,0:T(8,128)(2,1)} %param.26) | copy-start | bytes 6291460
  3.1 9.0 %copy-start.8 = (f32[31,1024]{1,0:T(8,128)S(1)}, f32[31,1024]{1,0:T(8,128)}, u32[]{:S(2)}) copy-start(f32[31,1024]{1,0:T(8,128)} %param.19) | copy-start | bytes 380932
  3.1 9.1 %copy-start.10 = (s32[1,128,2]{1,2,0:T(2,128)S(1)}, s32[1,128,2]{1,2,0:T(2,128)}, u32[]{:S(2)}) copy-start(s32[1,128,2]{1,2,0:T(2,128)} %param.16) | copy-start | bytes 3076
  6.4 7.8 %collective-permute-start = (bf16[15,1024]{1,0:T(8,128)(2,1)S(1)}, bf16[15,1024]{1,0:T(8,128)(2,1)S(1)}, u32[]{:S(2)}, u32[]{:S(2)}) collective-permute-start(bf16[15,1024]{1,0:T(8,128)(2,1)S(1)} %get-tuple-element.27), channel_id=1, source_target_pairs={{0,8},{8,16},{16,24},{24,32},{32,40},{40,48},{48,56},{1,9},{9,17},... | collective-permute-start | bytes 92168 | tf_op jit(solution)/shard_map/ppermute | solution.py:45
  10.8 4.8 %collective-permute-start.1 = (bf16[15,1024]{1,0:T(8,128)(2,1)S(1)}, bf16[15,1024]{1,0:T(8,128)(2,1)S(1)}, u32[]{:S(2)}, u32[]{:S(2)}) collective-permute-start(bf16[15,1024]{1,0:T(8,128)(2,1)S(1)} %get-tuple-element.28), channel_id=1, source_target_pairs={{8,0},{16,8},{24,16},{32,24},{40,32},{48,40},{56,48},{9,1},{17,9},... | collective-permute-start | bytes 92168 | tf_op jit(solution)/shard_map/ppermute | solution.py:46
  12.7 3.3 %copy-start.4 = (bf16[1,128,1024]{2,1,0:T(8,128)(2,1)S(1)}, bf16[1,128,1024]{2,1,0:T(8,128)(2,1)}, u32[]{:S(2)}) copy-start(bf16[1,128,1024]{2,1,0:T(8,128)(2,1)} %param.14) | copy-start | bytes 786436
  12.7 3.3 %copy-start.13 = (bf16[1024,1024]{1,0:T(8,128)(2,1)S(1)}, bf16[1024,1024]{1,0:T(8,128)(2,1)}, u32[]{:S(2)}) copy-start(bf16[1024,1024]{1,0:T(8,128)(2,1)} %param.22) | copy-start | bytes 6291460
  12.7 3.3 %copy-start.14 = (f32[1024]{0:T(1024)S(1)}, f32[1024]{0:T(1024)}, u32[]{:S(2)}) copy-start(f32[1024]{0:T(1024)} %param.21) | copy-start | bytes 12292
  12.7 3.3 %copy-start.15 = (f32[1024]{0:T(1024)S(1)}, f32[1024]{0:T(1024)}, u32[]{:S(2)}) copy-start(f32[1024]{0:T(1024)} %param.20) | copy-start | bytes 12292
  58.9 19.3 %collective-permute-start.3 = (bf16[384,1024]{1,0:T(8,128)(2,1)}, bf16[384,1024]{1,0:T(8,128)(2,1)}, u32[]{:S(2)}, u32[]{:S(2)}) collective-permute-start(bf16[384,1024]{1,0:T(8,128)(2,1)} %reshape.68), channel_id=1, source_target_pairs={{0,192},{64,0},{128,64},{192,128},{1,193},{65,1},{129,65},{193,129... | collective-permute-start | bytes 2359304 | tf_op jit(solution)/shard_map/ppermute | solution.py:107
  61.6 19.5 %collective-permute-start.2 = (bf16[384,1024]{1,0:T(8,128)(2,1)}, bf16[384,1024]{1,0:T(8,128)(2,1)S(1)}, u32[]{:S(2)}, u32[]{:S(2)}) collective-permute-start(bf16[384,1024]{1,0:T(8,128)(2,1)} %reshape.68), channel_id=1, source_target_pairs={{0,64},{64,128},{128,192},{192,0},{1,65},{65,129},{129,193},{193,1... | collective-permute-start | bytes 2359304 | tf_op jit(solution)/shard_map/ppermute | solution.py:106
  81.1 18.9 %collective-permute-start.4 = (bf16[384,1024]{1,0:T(8,128)(2,1)S(1)}, bf16[384,1024]{1,0:T(8,128)(2,1)}, u32[]{:S(2)}, u32[]{:S(2)}) collective-permute-start(bf16[384,1024]{1,0:T(8,128)(2,1)S(1)} %collective-permute-done.2), channel_id=1, source_target_pairs={{0,64},{64,128},{128,192},{192,0},{1,65},{65,129},{129,193},{193,1... | collective-permute-start | bytes 2359304 | tf_op jit(solution)/shard_map/ppermute | solution.py:110
  108.2 9.7 %copy-start.1 = (f32[384,1024]{1,0:T(8,128)S(1)}, f32[384,1024]{1,0:T(8,128)}, u32[]{:S(2)}) copy-start(f32[384,1024]{1,0:T(8,128)} %get-tuple-element.14) | copy-start | bytes 4718596
  108.2 9.9 %copy-start.2 = (f32[384,1024]{1,0:T(8,128)S(1)}, f32[384,1024]{1,0:T(8,128)}, u32[]{:S(2)}) copy-start(f32[384,1024]{1,0:T(8,128)} %get-tuple-element.16) | copy-start | bytes 4718596
  108.3 9.6 %collective-permute-start.5 = (bf16[192,1024]{1,0:T(8,128)(2,1)S(1)}, bf16[192,1024]{1,0:T(8,128)(2,1)S(1)}, u32[]{:S(2)}, u32[]{:S(2)}) collective-permute-start(bf16[192,1024]{1,0:T(8,128)(2,1)S(1)} %get-tuple-element.23), channel_id=1, source_target_pairs={{0,64},{64,128},{128,192},{192,0},{1,65},{65,129},{129,193},{193,1... | collective-permute-start | bytes 1179656 | tf_op jit(solution)/shard_map/ppermute | solution.py:117
  108.4 9.7 %collective-permute-start.9 = (bf16[192,1024]{1,0:T(8,128)(2,1)S(1)}, bf16[192,1024]{1,0:T(8,128)(2,1)S(1)}, u32[]{:S(2)}, u32[]{:S(2)}) collective-permute-start(bf16[192,1024]{1,0:T(8,128)(2,1)S(1)} %get-tuple-element.24), channel_id=1, source_target_pairs={{0,192},{64,0},{128,64},{192,128},{1,193},{65,1},{129,65},{193,129... | collective-permute-start | bytes 1179656 | tf_op jit(solution)/shard_map/ppermute | solution.py:118
  113.5 12.0 %collective-permute-start.7 = (bf16[192,1024]{1,0:T(8,128)(2,1)S(1)}, bf16[192,1024]{1,0:T(8,128)(2,1)S(1)}, u32[]{:S(2)}, u32[]{:S(2)}) collective-permute-start(bf16[192,1024]{1,0:T(8,128)(2,1)S(1)} %slice.1065), channel_id=1, source_target_pairs={{0,192},{64,0},{128,64},{192,128},{1,193},{65,1},{129,65},{193,129... | collective-permute-start | bytes 1179656 | tf_op jit(solution)/shard_map/ppermute | solution.py:115
  114.9 20.9 %collective-permute-start.8 = (bf16[192,1024]{1,0:T(8,128)(2,1)S(1)}, bf16[192,1024]{1,0:T(8,128)(2,1)S(1)}, u32[]{:S(2)}, u32[]{:S(2)}) collective-permute-start(bf16[192,1024]{1,0:T(8,128)(2,1)S(1)} %slice.1064), channel_id=1, source_target_pairs={{0,64},{64,128},{128,192},{192,0},{1,65},{65,129},{129,193},{193,1... | collective-permute-start | bytes 1179656 | tf_op jit(solution)/shard_map/ppermute | solution.py:114
  118.0 18.0 %copy-start.5 = (f32[384,1024]{1,0:T(8,128)S(1)}, f32[384,1024]{1,0:T(8,128)}, u32[]{:S(2)}) copy-start(f32[384,1024]{1,0:T(8,128)} %fusion.4) | copy-start | bytes 4718596
  118.0 17.7 %collective-permute-start.6 = (bf16[192,1024]{1,0:T(8,128)(2,1)S(1)}, bf16[192,1024]{1,0:T(8,128)(2,1)S(1)}, u32[]{:S(2)}, u32[]{:S(2)}) collective-permute-start(bf16[192,1024]{1,0:T(8,128)(2,1)S(1)} %add_convert_fusion.1), channel_id=1, source_target_pairs={{0,64},{64,128},{128,192},{192,0},{1,65},{65,129},{129,193},{193,1... | collective-permute-start | bytes 1179656 | tf_op jit(solution)/shard_map/ppermute | solution.py:119
  118.2 17.7 %collective-permute-start.10 = (bf16[192,1024]{1,0:T(8,128)(2,1)S(1)}, bf16[192,1024]{1,0:T(8,128)(2,1)S(1)}, u32[]{:S(2)}, u32[]{:S(2)}) collective-permute-start(bf16[192,1024]{1,0:T(8,128)(2,1)S(1)} %add_convert_fusion), channel_id=1, source_target_pairs={{0,192},{64,0},{128,64},{192,128},{1,193},{65,1},{129,65},{193,129... | collective-permute-start | bytes 1179656 | tf_op jit(solution)/shard_map/ppermute | solution.py:120
  136.3 9.0 %copy-start.7 = (bf16[1024,64]{0,1:T(8,128)(2,1)S(1)}, bf16[1024,64]{0,1:T(8,128)(2,1)}, u32[]{:S(2)}) copy-start(bf16[1024,64]{0,1:T(8,128)(2,1)} %param.24) | copy-start | bytes 393220
  137.6 30.7 %all-to-all-start.1 = ((bf16[64,48,128]{2,1,0:T(8,128)(2,1)}), bf16[64,48,128]{2,1,0:T(8,128)(2,1)}, u32[]{:S(2)}, u32[]{:S(2)}) async-start(bf16[64,48,128]{2,1,0:T(8,128)(2,1)} %reshape.69), calls=%async_computation.1 | async-start | bytes 1572864 | tf_op jit(solution)/shard_map/all_to_all | solution.py:125
  146.5 23.6 %copy-start.12 = (f32[128]{0:T(128)S(1)}, f32[128]{0:T(128)}, u32[]{:S(2)}) copy-start(f32[128]{0:T(128)} %copy-done.11) | copy-start | bytes 1540
  (4 other events, 6.0 us)

commit v13 on v12

--- a/solution.py
+++ b/solution.py
@@ -110,9 +110,9 @@
     far_rows = lax.ppermute(from_below, "dp", up)
     for_near = serve(jnp.concatenate([from_below, from_above], axis=0))
     for_below, for_above = for_near[: 2 * half], for_near[2 * half :]
-    far_rows, for_below, for_above = lax.optimization_barrier((far_rows, for_below, for_above))
     early_up = lax.ppermute(for_above[half:].astype(jnp.bfloat16), "dp", up).astype(jnp.float32)
     early_down = lax.ppermute(for_below[:half].astype(jnp.bfloat16), "dp", down).astype(jnp.float32)
+    far_rows, for_below, for_above = lax.optimization_barrier((far_rows, for_below, for_above))
     for_far = serve(far_rows).astype(jnp.bfloat16)
     far_up = lax.ppermute(for_far[:half], "dp", up).astype(jnp.float32)
     far_down = lax.ppermute(for_far[half:], "dp", down).astype(jnp.float32)

time: 172 us -> 171 us (level)
  transfers between devices with their start and end apart: 12 -> 12, of which waited for: 7 -> 7; matrix products, arithmetic and copies ran while one was open for 19% -> 18% of each run, Pallas kernels for 0% -> 0%
where the time goes in v13:
time: 171 us
  waiting for transfers between devices  51.6 us (30%)
  blocking collectives  36.4 us (21%)
  matrix products  35.9 us (21%)
  starting transfers between devices  24.6 us (14%)
  local copies, waits for them, and re-layouts  15.1 us (9%)
  other arithmetic  5.86 us (3%)
    all_to_all x1, blocking collectives, local(): lax.all_to_all(outgoing, ('seq', 'expert'), split_axis=0, concat_axis=0,...  36.4 us
    all_to_all x1, waiting for transfers between devices, local(): lax.all_to_all(served, ('seq', 'expert'), split_axis=0, concat_axis=0, ti...  22.7 us
    dot_general x3, matrix products, serve(): lax.dot_general(hidden, down_local, (((1,), (1,)), ((), ())), preferred_e...  18.4 us
    ppermute x1, waiting for transfers between devices, local(): lax.ppermute((for_above[:half] + far_up).astype(jnp.bfloat16), 'dp', up)  9.27 us
    all_to_all x1, starting transfers between devices, local(): lax.all_to_all(served, ('seq', 'expert'), split_axis=0, concat_axis=0, ti...  8.81 us
    ppermute x1, waiting for transfers between devices, local(): from_above = lax.ppermute(own_rows, 'dp', down)  7.22 us
    dot_general x2, matrix products, serve(): up_part = jnp.dot(rows, up_local, preferred_element_type=jnp.float32)  6.8 us
    ppermute x1, starting transfers between devices, local(): before = lax.ppermute(gated[token_count - reach:], 'seq', seq_up)  4.36 us
  transfers between devices with their start and end apart: 12, of which 7 were waited for; matrix products, arithmetic and copies ran while one was open for 18% of the time, Pallas kernels for 0%

profile of v13, /device:TPU:1, one launch (start us, length us, event | category | flops | bytes accessed | tf_op | source)
XLA Modules:
  0.0 170.8 jit_solution(1868183125321553260)
XLA Ops:
  3.1 3.1 %fusion.54 = f32[128,2048]{1,0:T(8,128)S(1)} fusion(bf16[1024,2048]{1,0:T(8,128)(2,1)} %param.18, bf16[1,128,1024]{2,1,0:T(8,128)(2,1)} %param.14, f32[1024]{0:T(1024)} %param.17, f32[128]{0:T(128)S(1)} %add_rsqrt_fusion.1, f32[128]{0:T(128)S(1)} %broadcast_multiply_fusion.1), kind=kOutput, calls=%fused_computation.86 | convolution fusion | flops 537526272 | bytes 5510144 | tf_op jit(solution)/shard_map/dot_general | solution.py:36
  6.4 4.4 %collective-permute-start = (bf16[15,1024]{1,0:T(8,128)(2,1)S(1)}, bf16[15,1024]{1,0:T(8,128)(2,1)S(1)}, u32[]{:S(2)}, u32[]{:S(2)}) collective-permute-start(bf16[15,1024]{1,0:T(8,128)(2,1)S(1)} %get-tuple-element.29), channel_id=1, source_target_pairs={{0,8},{8,16},{16,24},{24,32},{32,40},{40,48},{48,56},{1,9},{9,17},... | collective-permute-start | bytes 92168 | tf_op jit(solution)/shard_map/ppermute | solution.py:45
  12.7 1.5 multiply_add_fusion
  20.5 36.4 %all_to_all.10 = bf16[64,48,128]{2,1,0:T(8,128)(2,1)} all-to-all(bf16[64,48,128]{2,1,0:T(8,128)(2,1)S(1)} %reshape.67), channel_id=1, replica_groups=mesh['dp'=4,'seq'=8,'expert'=8] {'seq','expert'}, dimensions={0} | all-to-all | bytes 1572864 | tf_op jit(solution)/shard_map/all_to_all | solution.py:90
  56.9 2.2 %reshape.68 = bf16[384,1024]{1,0:T(8,128)(2,1)} reshape(bf16[64,48,128]{2,1,0:T(8,128)(2,1)} %all_to_all.10) | data formatting | bytes 1572864 | tf_op jit(solution)/shard_map/reshape | solution.py:92
  59.1 2.7 %collective-permute-start.3 = (bf16[384,1024]{1,0:T(8,128)(2,1)}, bf16[384,1024]{1,0:T(8,128)(2,1)}, u32[]{:S(2)}, u32[]{:S(2)}) collective-permute-start(bf16[384,1024]{1,0:T(8,128)(2,1)} %reshape.68), channel_id=1, source_target_pairs={{0,192},{64,0},{128,64},{192,128},{1,193},{65,1},{129,65},{193,129... | collective-permute-start | bytes 2359304 | tf_op jit(solution)/shard_map/ppermute | solution.py:107
  61.8 4.0 %fusion.16 = f32[384,1024]{1,0:T(8,128)} fusion(bf16[384,1024]{1,0:T(8,128)(2,1)} %reshape.68, bf16[1,1024,1024]{2,1,0:T(8,128)(2,1)} %param.25), kind=kOutput, calls=%fused_computation.17 | convolution fusion | flops 805306368 | bytes 4456448 | tf_op jit(solution)/shard_map/dot_general | solution.py:95
  65.8 5.3 %fusion.4 = f32[384,1024]{1,0:T(8,128)} fusion(bf16[1,1024,1024]{2,1,0:T(8,128)(2,1)S(1)} %copy-done, f32[384,1024]{1,0:T(8,128)} %fusion.16, bf16[384,1024]{1,0:T(8,128)(2,1)} %reshape.68, bf16[1,1024,1024]{2,1,0:T(8,128)(2,1)} %param.26), kind=kOutput, calls=%fused_computation.5 | convolution fusion | flops 1612972032 | bytes 8126464 | tf_op jit(solution)/shard_map/dot_general | solution.py:98
  71.1 7.2 %collective-permute-done.3 = bf16[384,1024]{1,0:T(8,128)(2,1)} collective-permute-done((bf16[384,1024]{1,0:T(8,128)(2,1)}, bf16[384,1024]{1,0:T(8,128)(2,1)}, u32[]{:S(2)}, u32[]{:S(2)}) %collective-permute-start.3) | collective-permute-done | bytes 786464 | tf_op jit(solution)/shard_map/ppermute | solution.py:107
  78.3 3.0 %collective-permute-done.2 = bf16[384,1024]{1,0:T(8,128)(2,1)S(1)} collective-permute-done((bf16[384,1024]{1,0:T(8,128)(2,1)}, bf16[384,1024]{1,0:T(8,128)(2,1)S(1)}, u32[]{:S(2)}, u32[]{:S(2)}) %collective-permute-start.2) | collective-permute-done | bytes 786464 | tf_op jit(solution)/shard_map/ppermute | solution.py:106
  83.7 3.5 %fusion.8 = f32[768,1024]{1,0:T(8,128)} fusion(bf16[768,1024]{1,0:T(8,128)(2,1)S(1)} %constant_dynamic-update-slice_fusion, bf16[1,1024,1024]{2,1,0:T(8,128)(2,1)S(1)} %copy-done.15), kind=kOutput, calls=%fused_computation.9 | convolution fusion | flops 1610612736 | bytes 6815744 | tf_op jit(solution)/shard_map/dot_general | solution.py:96
  87.2 8.9 %fusion.116 = (bf16[768,1024]{1,0:T(8,128)(2,1)}, f32[768,1024]{1,0:T(8,128)}) fusion(bf16[1,1024,1024]{2,1,0:T(8,128)(2,1)S(1)} %copy-done, f32[768,1024]{1,0:T(8,128)} %fusion.8, bf16[768,1024]{1,0:T(8,128)(2,1)} %copy-done.7, bf16[1,1024,1024]{2,1,0:T(8,128)(2,1)} %param.25), kind=kOutput, calls=%fused_computation.197 | convolution fusion | flops 3226730496 | bytes 13631488 | tf_op jit(solution)/shard_map/dot_general | solution.py:98
  96.1 4.1 %fusion.108 = (f32[384,1024]{1,0:T(8,128)}, f32[384,1024]{1,0:T(8,128)}) fusion(f32[768,1024]{1,0:T(8,128)} %get-tuple-element.71), kind=kLoop, calls=%fused_computation.189 | loop fusion | bytes 6291456 | tf_op jit(solution)/shard_map/slice | solution.py:112
  100.3 3.3 %fusion.6 = f32[384,1024]{1,0:T(8,128)} fusion(bf16[384,1024]{1,0:T(8,128)(2,1)} %collective-permute-done.4, bf16[1,1024,1024]{2,1,0:T(8,128)(2,1)S(1)} %copy-done.16), kind=kOutput, calls=%fused_computation.7 | convolution fusion | flops 805306368 | bytes 4456448 | tf_op jit(solution)/shard_map/dot_general | solution.py:96
  103.6 4.2 %fusion.25 = bf16[384,1024]{1,0:T(8,128)(2,1)S(1)} fusion(bf16[1,1024,1024]{2,1,0:T(8,128)(2,1)S(1)} %copy-done, f32[384,1024]{1,0:T(8,128)} %fusion.6, bf16[384,1024]{1,0:T(8,128)(2,1)} %collective-permute-done.4, bf16[1,1024,1024]{2,1,0:T(8,128)(2,1)} %param.25), kind=kOutput, calls=%fused_computation.24 | convolution fusion | flops 1613365248 | bytes 7340032 | tf_op jit(solution)/shard_map/dot_general | solution.py:98
  107.9 2.8 %collective-permute-start.9 = (bf16[192,1024]{1,0:T(8,128)(2,1)S(1)}, bf16[192,1024]{1,0:T(8,128)(2,1)S(1)}, u32[]{:S(2)}, u32[]{:S(2)}) collective-permute-start(bf16[192,1024]{1,0:T(8,128)(2,1)S(1)} %get-tuple-element.26), channel_id=1, source_target_pairs={{0,192},{64,0},{128,64},{192,128},{1,193},{65,1},{129,65},{193,129... | collective-permute-start | bytes 1179656 | tf_op jit(solution)/shard_map/ppermute | solution.py:118
  112.0 1.5 collective-permute-start.7
  113.5 4.0 %collective-permute-done.5 = bf16[192,1024]{1,0:T(8,128)(2,1)S(1)} collective-permute-done((bf16[192,1024]{1,0:T(8,128)(2,1)S(1)}, bf16[192,1024]{1,0:T(8,128)(2,1)S(1)}, u32[]{:S(2)}, u32[]{:S(2)}) %collective-permute-start.5) | collective-permute-done | bytes 393248 | tf_op jit(solution)/shard_map/ppermute | solution.py:117
  117.8 2.9 %collective-permute-start.10 = (bf16[192,1024]{1,0:T(8,128)(2,1)S(1)}, bf16[192,1024]{1,0:T(8,128)(2,1)S(1)}, u32[]{:S(2)}, u32[]{:S(2)}) collective-permute-start(bf16[192,1024]{1,0:T(8,128)(2,1)S(1)} %add_convert_fusion), channel_id=1, source_target_pairs={{0,192},{64,0},{128,64},{192,128},{1,193},{65,1},{129,65},{193,129... | collective-permute-start | bytes 1179656 | tf_op jit(solution)/shard_map/ppermute | solution.py:120
  120.7 4.3 %collective-permute-done.7 = bf16[192,1024]{1,0:T(8,128)(2,1)S(1)} collective-permute-done((bf16[192,1024]{1,0:T(8,128)(2,1)S(1)}, bf16[192,1024]{1,0:T(8,128)(2,1)S(1)}, u32[]{:S(2)}, u32[]{:S(2)}) %collective-permute-start.7) | collective-permute-done | bytes 393248 | tf_op jit(solution)/shard_map/ppermute | solution.py:114
  125.1 9.3 %collective-permute-done.6 = bf16[192,1024]{1,0:T(8,128)(2,1)S(1)} collective-permute-done((bf16[192,1024]{1,0:T(8,128)(2,1)S(1)}, bf16[192,1024]{1,0:T(8,128)(2,1)S(1)}, u32[]{:S(2)}, u32[]{:S(2)}) %collective-permute-start.6) | collective-permute-done | bytes 393248 | tf_op jit(solution)/shard_map/ppermute | solution.py:119
  136.2 8.8 %all-to-all-start.1 = ((bf16[64,48,128]{2,1,0:T(8,128)(2,1)}), bf16[64,48,128]{2,1,0:T(8,128)(2,1)}, u32[]{:S(2)}, u32[]{:S(2)}) async-start(bf16[64,48,128]{2,1,0:T(8,128)(2,1)} %reshape.69), calls=%async_computation.1 | async-start | bytes 1572864 | tf_op jit(solution)/shard_map/all_to_all | solution.py:125
  145.3 22.7 %all-to-all-done.1 = bf16[64,48,128]{2,1,0:T(8,128)(2,1)} async-done(((bf16[64,48,128]{2,1,0:T(8,128)(2,1)}), bf16[64,48,128]{2,1,0:T(8,128)(2,1)}, u32[]{:S(2)}, u32[]{:S(2)}) %all-to-all-start.1) | async-done | bytes 786464 | tf_op jit(solution)/shard_map/all_to_all | solution.py:125
  168.0 1.4 reshape.70
  (90 shorter events, 18.1 us)
Async XLA Ops:
  0.0 65.8 %copy-start = (bf16[1,1024,1024]{2,1,0:T(8,128)(2,1)S(1)}, bf16[1,1024,1024]{2,1,0:T(8,128)(2,1)}, u32[]{:S(2)}) copy-start(bf16[1,1024,1024]{2,1,0:T(8,128)(2,1)} %param.27) | copy-start | bytes 6291460
  3.1 9.0 %copy-start.9 = (f32[31,1024]{1,0:T(8,128)S(1)}, f32[31,1024]{1,0:T(8,128)}, u32[]{:S(2)}) copy-start(f32[31,1024]{1,0:T(8,128)} %param.19) | copy-start | bytes 380932
  6.2 6.0 %copy-start.11 = (s32[1,128,2]{1,2,0:T(2,128)S(1)}, s32[1,128,2]{1,2,0:T(2,128)}, u32[]{:S(2)}) copy-start(s32[1,128,2]{1,2,0:T(2,128)} %param.16) | copy-start | bytes 3076
  6.4 7.8 %collective-permute-start = (bf16[15,1024]{1,0:T(8,128)(2,1)S(1)}, bf16[15,1024]{1,0:T(8,128)(2,1)S(1)}, u32[]{:S(2)}, u32[]{:S(2)}) collective-permute-start(bf16[15,1024]{1,0:T(8,128)(2,1)S(1)} %get-tuple-element.29), channel_id=1, source_target_pairs={{0,8},{8,16},{16,24},{24,32},{32,40},{40,48},{48,56},{1,9},{9,17},... | collective-permute-start | bytes 92168 | tf_op jit(solution)/shard_map/ppermute | solution.py:45
  10.8 4.8 %collective-permute-start.1 = (bf16[15,1024]{1,0:T(8,128)(2,1)S(1)}, bf16[15,1024]{1,0:T(8,128)(2,1)S(1)}, u32[]{:S(2)}, u32[]{:S(2)}) collective-permute-start(bf16[15,1024]{1,0:T(8,128)(2,1)S(1)} %get-tuple-element.30), channel_id=1, source_target_pairs={{8,0},{16,8},{24,16},{32,24},{40,32},{48,40},{56,48},{9,1},{17,9},... | collective-permute-start | bytes 92168 | tf_op jit(solution)/shard_map/ppermute | solution.py:46
  12.7 3.3 %copy-start.14 = (bf16[1024,1024]{1,0:T(8,128)(2,1)S(1)}, bf16[1024,1024]{1,0:T(8,128)(2,1)}, u32[]{:S(2)}) copy-start(bf16[1024,1024]{1,0:T(8,128)(2,1)} %param.22) | copy-start | bytes 6291460
  59.1 19.3 %collective-permute-start.3 = (bf16[384,1024]{1,0:T(8,128)(2,1)}, bf16[384,1024]{1,0:T(8,128)(2,1)}, u32[]{:S(2)}, u32[]{:S(2)}) collective-permute-start(bf16[384,1024]{1,0:T(8,128)(2,1)} %reshape.68), channel_id=1, source_target_pairs={{0,192},{64,0},{128,64},{192,128},{1,193},{65,1},{129,65},{193,129... | collective-permute-start | bytes 2359304 | tf_op jit(solution)/shard_map/ppermute | solution.py:107
  61.8 19.5 %collective-permute-start.2 = (bf16[384,1024]{1,0:T(8,128)(2,1)}, bf16[384,1024]{1,0:T(8,128)(2,1)S(1)}, u32[]{:S(2)}, u32[]{:S(2)}) collective-permute-start(bf16[384,1024]{1,0:T(8,128)(2,1)} %reshape.68), channel_id=1, source_target_pairs={{0,64},{64,128},{128,192},{192,0},{1,65},{65,129},{129,193},{193,1... | collective-permute-start | bytes 2359304 | tf_op jit(solution)/shard_map/ppermute | solution.py:106
  71.1 12.6 %copy-start.15 = (bf16[1,1024,1024]{2,1,0:T(8,128)(2,1)S(1)}, bf16[1,1024,1024]{2,1,0:T(8,128)(2,1)}, u32[]{:S(2)}) copy-start(bf16[1,1024,1024]{2,1,0:T(8,128)(2,1)} %param.26) | copy-start | bytes 6291460
  81.3 18.9 %collective-permute-start.4 = (bf16[384,1024]{1,0:T(8,128)(2,1)S(1)}, bf16[384,1024]{1,0:T(8,128)(2,1)}, u32[]{:S(2)}, u32[]{:S(2)}) collective-permute-start(bf16[384,1024]{1,0:T(8,128)(2,1)S(1)} %collective-permute-done.2), channel_id=1, source_target_pairs={{0,64},{64,128},{128,192},{192,0},{1,65},{65,129},{129,193},{193,1... | collective-permute-start | bytes 2359304 | tf_op jit(solution)/shard_map/ppermute | solution.py:110
  96.1 4.1 %copy-start.16 = (bf16[1,1024,1024]{2,1,0:T(8,128)(2,1)S(1)}, bf16[1,1024,1024]{2,1,0:T(8,128)(2,1)}, u32[]{:S(2)}) copy-start(bf16[1,1024,1024]{2,1,0:T(8,128)(2,1)} %param.26) | copy-start | bytes 6291460
  107.8 9.7 %copy-start.2 = (f32[384,1024]{1,0:T(8,128)S(1)}, f32[384,1024]{1,0:T(8,128)}, u32[]{:S(2)}) copy-start(f32[384,1024]{1,0:T(8,128)} %get-tuple-element.14) | copy-start | bytes 4718596
  107.8 9.6 %collective-permute-start.5 = (bf16[192,1024]{1,0:T(8,128)(2,1)S(1)}, bf16[192,1024]{1,0:T(8,128)(2,1)S(1)}, u32[]{:S(2)}, u32[]{:S(2)}) collective-permute-start(bf16[192,1024]{1,0:T(8,128)(2,1)S(1)} %get-tuple-element.25), channel_id=1, source_target_pairs={{0,64},{64,128},{128,192},{192,0},{1,65},{65,129},{129,193},{193,1... | collective-permute-start | bytes 1179656 | tf_op jit(solution)/shard_map/ppermute | solution.py:117
  107.9 9.7 %collective-permute-start.9 = (bf16[192,1024]{1,0:T(8,128)(2,1)S(1)}, bf16[192,1024]{1,0:T(8,128)(2,1)S(1)}, u32[]{:S(2)}, u32[]{:S(2)}) collective-permute-start(bf16[192,1024]{1,0:T(8,128)(2,1)S(1)} %get-tuple-element.26), channel_id=1, source_target_pairs={{0,192},{64,0},{128,64},{192,128},{1,193},{65,1},{129,65},{193,129... | collective-permute-start | bytes 1179656 | tf_op jit(solution)/shard_map/ppermute | solution.py:118
  110.7 7.0 %copy-start.1 = (f32[384,1024]{1,0:T(8,128)S(1)}, f32[384,1024]{1,0:T(8,128)}, u32[]{:S(2)}) copy-start(f32[384,1024]{1,0:T(8,128)} %get-tuple-element.16) | copy-start | bytes 4718596
  112.0 13.1 %collective-permute-start.7 = (bf16[192,1024]{1,0:T(8,128)(2,1)S(1)}, bf16[192,1024]{1,0:T(8,128)(2,1)S(1)}, u32[]{:S(2)}, u32[]{:S(2)}) collective-permute-start(bf16[192,1024]{1,0:T(8,128)(2,1)S(1)} %get-tuple-element.23), channel_id=1, source_target_pairs={{0,192},{64,0},{128,64},{192,128},{1,193},{65,1},{129,65},{193,129... | collective-permute-start | bytes 1179656 | tf_op jit(solution)/shard_map/ppermute | solution.py:114
  113.4 21.0 %collective-permute-start.8 = (bf16[192,1024]{1,0:T(8,128)(2,1)S(1)}, bf16[192,1024]{1,0:T(8,128)(2,1)S(1)}, u32[]{:S(2)}, u32[]{:S(2)}) collective-permute-start(bf16[192,1024]{1,0:T(8,128)(2,1)S(1)} %get-tuple-element.24), channel_id=1, source_target_pairs={{0,64},{64,128},{128,192},{192,0},{1,65},{65,129},{129,193},{193,1... | collective-permute-start | bytes 1179656 | tf_op jit(solution)/shard_map/ppermute | solution.py:113
  117.6 16.8 %collective-permute-start.6 = (bf16[192,1024]{1,0:T(8,128)(2,1)S(1)}, bf16[192,1024]{1,0:T(8,128)(2,1)S(1)}, u32[]{:S(2)}, u32[]{:S(2)}) collective-permute-start(bf16[192,1024]{1,0:T(8,128)(2,1)S(1)} %add_convert_fusion.1), channel_id=1, source_target_pairs={{0,64},{64,128},{128,192},{192,0},{1,65},{65,129},{129,193},{193,1... | collective-permute-start | bytes 1179656 | tf_op jit(solution)/shard_map/ppermute | solution.py:119
  117.8 16.8 %copy-start.6 = (f32[384,1024]{1,0:T(8,128)S(1)}, f32[384,1024]{1,0:T(8,128)}, u32[]{:S(2)}) copy-start(f32[384,1024]{1,0:T(8,128)} %fusion.4) | copy-start | bytes 4718596
  117.8 16.7 %collective-permute-start.10 = (bf16[192,1024]{1,0:T(8,128)(2,1)S(1)}, bf16[192,1024]{1,0:T(8,128)(2,1)S(1)}, u32[]{:S(2)}, u32[]{:S(2)}) collective-permute-start(bf16[192,1024]{1,0:T(8,128)(2,1)S(1)} %add_convert_fusion), channel_id=1, source_target_pairs={{0,192},{64,0},{128,64},{192,128},{1,193},{65,1},{129,65},{193,129... | collective-permute-start | bytes 1179656 | tf_op jit(solution)/shard_map/ppermute | solution.py:120
  134.9 10.1 %copy-start.8 = (bf16[1024,64]{0,1:T(8,128)(2,1)S(1)}, bf16[1024,64]{0,1:T(8,128)(2,1)}, u32[]{:S(2)}) copy-start(bf16[1024,64]{0,1:T(8,128)(2,1)} %param.24) | copy-start | bytes 393220
  136.2 8.8 %copy-start.4 = (bf16[128,1024]{1,0:T(8,128)(2,1)S(1)}, bf16[128,1024]{1,0:T(8,128)(2,1)}, u32[]{:S(2)}) copy-start(bf16[128,1024]{1,0:T(8,128)(2,1)} %copy-done.3) | copy-start | bytes 786436
  136.2 31.8 %all-to-all-start.1 = ((bf16[64,48,128]{2,1,0:T(8,128)(2,1)}), bf16[64,48,128]{2,1,0:T(8,128)(2,1)}, u32[]{:S(2)}, u32[]{:S(2)}) async-start(bf16[64,48,128]{2,1,0:T(8,128)(2,1)} %reshape.69), calls=%async_computation.1 | async-start | bytes 1572864 | tf_op jit(solution)/shard_map/all_to_all | solution.py:125
  145.3 24.5 %copy-start.13 = (f32[128]{0:T(128)S(1)}, f32[128]{0:T(128)}, u32[]{:S(2)}) copy-start(f32[128]{0:T(128)} %copy-done.12) | copy-start | bytes 1540
  (7 other events, 11.3 us)
